TPU v7x, 128 devices: a whole 4x4x4 slice. The times are simulated.
128 devices in a mesh: src: 16 (over x_lo, z, core), loop: 8 (over x_hi, y).
Axes of the slice: x: 4 (x_hi: 2, x_lo: 2; x = x_hi * 2 + x_lo), y: 4, z: 4, core: 2. Of those that a mesh axis runs over, the one named last changes fastest.
Arguments:
- sources: bfloat16 [65536, 768], P(('src', 'loop')), may hold values from -48 to 48
- log_a: float32 [65536], P(('src', 'loop')), may hold values from -3 to 0
- targets: bfloat16 [128, 512, 768], P('src'), may hold values from -6 to 6
- g_old: bfloat16 [128, 512], P('src'), may hold values from -2.5 to 2.5
- log_b: float32 [128, 512], P('src'), may hold values from -3 to 0
- tile_ids: int32 [128, 16, 2], P(('src', 'loop')), may hold values from 0 to 127, as said below
- live_count: int32 [128, 16], P(('src', 'loop')), may hold values from 1 to 2, as said below
Outputs:
- f_new: float32 [65536], P(('src', 'loop'))
- g_new: float32 [128, 512], P('src')
Inputs may be any that keep to these rules, and one draw needn't show every extreme that they name: `tile_ids`: tile ids of one device for index o of src lie in o * 8 to (o + 1) * 8 - 1 and are distinct within that group of 2 slots; every tile is in use in some device's list. `live_count`: every index of src has a full group of 2 slots in use in some device's list.
All inputs are finite; a program needn't handle non-finite values.
Results may differ from a plain program's by a relative error of at most 0.0003.
Values may be sent and summed in bfloat16 or wider, within the bound.
No kernel may reach another device: no remote copies, remote signals or barrier semaphores. Data moves between devices by JAX's collectives and lax.ppermute only.
A program may use at most 128 MiB of HBM per device.

v0:
```python
import math

import jax
import jax.numpy as jnp
from jax import lax
from jax.sharding import PartitionSpec as P

EPSILON = 0.1
VERY_LOW = -1e30


def combined_all(part, axis, combine):
    gathered = jax.tree.map(lambda a: lax.all_gather(a, axis), part)

    def take(source):
        return jax.tree.map(lambda a: lax.dynamic_index_in_dim(a, source, 0, False), gathered)

    return lax.fori_loop(
        1, lax.axis_size(axis), lambda source, state: combine(state, take(source)), take(0)
    )


def similarity(rows_bf, fetched):
    kernel = jnp.einsum("rd,ctd->rct", rows_bf, fetched, preferred_element_type=jnp.float32)
    return kernel / math.sqrt(rows_bf.shape[1])


def row_part(rows_bf, fetched, potential, live_slots):
    kernel = similarity(rows_bf, fetched)
    logits = (potential.astype(jnp.float32)[None] + kernel) / EPSILON
    logits = jnp.where(live_slots[None, :, None], logits, VERY_LOW)
    top = jnp.max(logits, axis=(1, 2))
    total = jnp.sum(jnp.exp(logits - top[:, None, None]), axis=(1, 2))
    return (top, total)


def col_part(rows_bf, row_potential, fetched, live_slots):
    kernel = similarity(rows_bf, fetched)
    logits = (row_potential[:, None, None] + kernel) / EPSILON
    top = jnp.max(logits, axis=0)
    total = jnp.sum(jnp.exp(logits - top[None]), axis=0)
    top = jnp.where(live_slots[:, None], top, VERY_LOW)
    total = jnp.where(live_slots[:, None], total, 0.0)
    return (top, total)


def combine(first, second):
    top = jnp.maximum(first[0], second[0])
    total = first[1] * jnp.exp(first[0] - top) + second[1] * jnp.exp(second[0] - top)
    return (top, total)


def fold_rows(row_top, row_total):
    top = jnp.max(row_top, axis=0)
    total = jnp.sum(row_total * jnp.exp(row_top - top[None]), axis=0)
    return (top, total)


def local(sources, log_a, targets, g_old, log_b, tile_ids, live_count):
    tiles_own = targets.shape[0]
    width = targets.shape[1]
    slots_per = tile_ids.shape[2]
    requested = tile_ids[0]
    live_slots = jnp.arange(slots_per, dtype=jnp.int32)[None, :] < live_count[0][:, None]
    base_id = lax.axis_index("src") * tiles_own
    arrived = lax.all_to_all(requested, "src", split_axis=0, concat_axis=0, tiled=True)
    local_ids = arrived - base_id
    packed = targets[local_ids]
    packed_pot = g_old[local_ids]
    fetched, fetched_pot = (
        lax.all_to_all(packed, "src", split_axis=0, concat_axis=0, tiled=True),
        lax.all_to_all(packed_pot, "src", split_axis=0, concat_axis=0, tiled=True),
    )

    def rows_of(item):
        return row_part(sources, item[0], item[1], item[2])

    row_top, row_total = lax.map(rows_of, (fetched, fetched_pot, live_slots))
    top, total = fold_rows(row_top, row_total)
    f_new = EPSILON * log_a - EPSILON * (top + jnp.log(total))

    def cols_of(item):
        return col_part(sources, f_new, item[0], item[1])

    col_top, col_total = lax.map(cols_of, (fetched, live_slots))
    col_top, col_total = (
        lax.all_to_all(col_top, "src", split_axis=0, concat_axis=0, tiled=True),
        lax.all_to_all(col_total, "src", split_axis=0, concat_axis=0, tiled=True),
    )
    flat_ids = local_ids.reshape(-1)
    flat_top = col_top.reshape(-1, width)
    flat_total = col_total.reshape(-1, width)
    onehot = flat_ids[:, None] == jnp.arange(tiles_own, dtype=jnp.int32)[None, :]
    tile_top = jnp.max(jnp.where(onehot[:, :, None], flat_top[:, None, :], VERY_LOW), axis=0)
    scaled = flat_total[:, None, :] * jnp.exp(
        jnp.minimum(flat_top[:, None, :] - tile_top[None], 0.0)
    )
    tile_total = jnp.sum(jnp.where(onehot[:, :, None], scaled, 0.0), axis=0)
    tile_top, tile_total = combined_all((tile_top, tile_total), "loop", combine)
    g_new = EPSILON * log_b - EPSILON * (tile_top + jnp.log(tile_total))
    return (f_new, g_new)


def solution(mesh):
    return jax.shard_map(
        local,
        mesh=mesh,
        in_specs=(
            P(("src", "loop"), None),
            P(("src", "loop")),
            P("src", None, None),
            P("src", None),
            P("src", None),
            P(("src", "loop"), None, None),
            P(("src", "loop"), None),
        ),
        out_specs=(P(("src", "loop")), P("src", None)),
        check_vma=False,
    )
```

profile of v0, /device:TPU:0, one launch (start us, length us, event | category | flops | bytes accessed | tf_op | source)
XLA Modules:
  0.0 627.7 jit_solution(8107096106254679023)
XLA Ops:
  2.0 6.5 %all-to-all-start = ((s32[16,1,2]{2,1,0:T(1,128)}), s32[16,1,2]{2,1,0:T(1,128)S(1)}, u32[]{:S(2)}, u32[]{:S(2)}) async-start(s32[16,1,2]{2,1,0:T(1,128)} %copy.16), calls=%async_computation | async-start | bytes 16384 | tf_op jit(solution)/shard_map/all_to_all | solution.py:66
  8.5 6.0 all-to-all-done
  17.2 3.5 all-to-all-start.1
  20.7 12.8 %gather_fusion.1 = bf16[32,512,768]{2,1,0:T(8,128)(2,1)} fusion(bf16[8,512,768]{2,1,0:T(8,128)(2,1)} %param.15, s32[1024]{0:T(1024)S(1)} %pad_clamp_fusion), kind=kCustom, calls=%fused_computation.1 | custom fusion | bytes 50331776 | tf_op jit(solution)/shard_map/gather | solution.py:68
  33.5 5.9 all-to-all-start.2
  39.7 393.7 %all-to-all-done.2 = bf16[16,2,512,768]{3,2,1,0:T(8,128)(2,1)} async-done(((bf16[16,2,512,768]{3,2,1,0:T(8,128)(2,1)}), bf16[16,2,512,768]{3,2,1,0:T(8,128)(2,1)}, u32[]{:S(2)}, u32[]{:S(2)}) %all-to-all-start.2) | async-done | bytes 25165856 | tf_op jit(solution)/shard_map/all_to_all | solution.py:71
  433.4 49.4 %while.41 = (s32[]{:T(128)}, f32[16,512]{1,0:T(8,128)S(1)}, f32[16,512]{1,0:T(8,128)S(1)}, pred[16,2]{1,0:T(8,128)(4,1)S(1)}, bf16[16,2,512]{2,1,0:T(2,128)(2,1)...) while((s32[]{:T(128)}, f32[16,512]{1,0:T(8,128)S(1)}, ...), condition=%wide.region_3.4_spmd, body=%wide.region_0.3_spmd.sunk | while | flops 808976384 | bytes 6578803 | solution.py:78
  442.7 2.5 fusion.21
  445.7 2.5 fusion.21
  448.8 2.5 fusion.21
  451.9 2.5 fusion.21
  455.0 2.5 fusion.21
  461.2 2.5 fusion.21
  464.3 2.5 fusion.21
  470.5 2.5 fusion.21
  473.6 2.5 fusion.21
  476.7 2.5 fusion.21
  479.7 2.5 fusion.21
  482.9 59.2 %while.42 = (s32[]{:T(128)}, f32[16,2,512]{2,1,0:T(2,128)}, f32[16,2,512]{2,1,0:T(2,128)}, pred[16,2]{1,0:T(8,128)(4,1)S(1)}, f32[512]{0:T(512)S(1)}, /*index=5*...) while((s32[]{:T(128)}, f32[16,2,512]{2,1,0:T(2,128)}, f32[16,2,512]{2,1,0:T(2,128)}, ...), condition=%wide.region_9.10_spmd, body=%wide.region_6.9_spmd.sunk | while | flops 810024960 | bytes 6587487 | solution.py:85
  542.0 5.8 all-to-all-start.3
  548.0 6.1 all-to-all-done.3
  554.1 3.5 all-to-all-start.4
  557.7 34.5 %all-gather = f32[64,512]{1,0:T(8,128)S(1)} all-gather(f32[8,512]{1,0:T(8,128)S(1)} %select_reduce_fusion.1), channel_id=2, replica_groups=mesh['src'=16,'loop'=8] {'loop'}, dimensions={0}, use_global_device_ids=true | all-gather | bytes 147456 | tf_op jit(solution)/shard_map/all_gather | solution.py:13
  592.5 34.2 %all-gather.1 = f32[64,512]{1,0:T(8,128)S(1)} all-gather(f32[8,512]{1,0:T(8,128)S(1)} %select_reduce_fusion), channel_id=3, replica_groups=mesh['src'=16,'loop'=8] {'loop'}, dimensions={0}, use_global_device_ids=true | all-gather | bytes 147456 | tf_op jit(solution)/shard_map/all_gather | solution.py:13
  (198 shorter events, 85.5 us)
Async XLA Ops:
  0.6 15.3 %copy-start = (bf16[8,512]{1,0:T(8,128)(2,1)S(1)}, bf16[8,512]{1,0:T(8,128)(2,1)}, u32[]{:S(2)}) copy-start(bf16[8,512]{1,0:T(8,128)(2,1)} %param.16) | copy-start | bytes 24580
  2.0 12.5 %all-to-all-start = ((s32[16,1,2]{2,1,0:T(1,128)}), s32[16,1,2]{2,1,0:T(1,128)S(1)}, u32[]{:S(2)}, u32[]{:S(2)}) async-start(s32[16,1,2]{2,1,0:T(1,128)} %copy.16), calls=%async_computation | async-start | bytes 16384 | tf_op jit(solution)/shard_map/all_to_all | solution.py:66
  17.2 16.3 %all-to-all-start.1 = ((bf16[16,2,512]{2,1,0:T(2,128)(2,1)}), bf16[16,2,512]{2,1,0:T(2,128)(2,1)S(1)}, u32[]{:S(2)}, u32[]{:S(2)}) async-start(bf16[16,2,512]{2,1,0:T(2,128)(2,1)} %reshape.131), calls=%async_computation.1 | async-start | bytes 65536 | tf_op jit(solution)/shard_map/all_to_all | solution.py:72
  33.5 6.0 copy-start.4
  33.5 399.8 %copy-start.5 = (bf16[512,768]{1,0:T(8,128)(2,1)S(1)}, bf16[512,768]{1,0:T(8,128)(2,1)}, u32[]{:S(2)}) copy-start(bf16[512,768]{1,0:T(8,128)(2,1)} %param.13) | copy-start | bytes 2359300
  33.5 399.8 %all-to-all-start.2 = ((bf16[16,2,512,768]{3,2,1,0:T(8,128)(2,1)}), bf16[16,2,512,768]{3,2,1,0:T(8,128)(2,1)}, u32[]{:S(2)}, u32[]{:S(2)}) async-start(bf16[16,2,512,768]{3,2,1,0:T(8,128)(2,1)} %bitcast.91), calls=%async_computation.2 | async-start | bytes 50331648 | tf_op jit(solution)/shard_map/all_to_all | solution.py:71
  433.4 49.5 %copy-start.3 = (f32[512]{0:T(512)S(1)}, f32[512]{0:T(512)}, u32[]{:S(2)}) copy-start(f32[512]{0:T(512)} %param.14) | copy-start | bytes 6148
  482.9 144.2 %copy-start.2 = (f32[8,512]{1,0:T(8,128)S(1)}, f32[8,512]{1,0:T(8,128)}, u32[]{:S(2)}) copy-start(f32[8,512]{1,0:T(8,128)} %param.17) | copy-start | bytes 49156
  542.0 85.6 %copy-start.1 = (f32[512]{0:T(512)}, f32[512]{0:T(512)S(1)}, u32[]{:S(2)}) copy-start(f32[512]{0:T(512)S(1)} %get-tuple-element.477) | copy-start | bytes 6148
  542.0 12.0 %all-to-all-start.3 = ((f32[16,2,512]{2,1,0:T(2,128)}), f32[16,2,512]{2,1,0:T(2,128)S(1)}, u32[]{:S(2)}, u32[]{:S(2)}) async-start(f32[16,2,512]{2,1,0:T(2,128)} %get-tuple-element.213), calls=%async_computation.3 | async-start | bytes 131072 | tf_op jit(solution)/shard_map/all_to_all | solution.py:87
  554.1 38.2 %all-to-all-start.4 = ((f32[16,2,512]{2,1,0:T(2,128)}), f32[16,2,512]{2,1,0:T(2,128)S(1)}, u32[]{:S(2)}, u32[]{:S(2)}) async-start(f32[16,2,512]{2,1,0:T(2,128)} %get-tuple-element.214), calls=%async_computation.4 | async-start | bytes 131072 | tf_op jit(solution)/shard_map/all_to_all | solution.py:88
where the time goes:
time: 629 us; the launch traced here: 628 us
  waiting for transfers between devices  406 us (65%)
  matrix products  79.6 us (13%)
  blocking collectives  68.8 us (11%)
  other arithmetic  27.5 us (4%)
  starting transfers between devices  25.2 us (4%)
  local copies, waits for them, and re-layouts  18.8 us (3%)
    all_to_all x1, waiting for transfers between devices, local(): lax.all_to_all(packed, 'src', split_axis=0, concat_axis=0, tiled=True)  394 us
    dot_general x32, matrix products, similarity(): jnp.einsum('rd,ctd->rct', rows_bf, fetched, preferred_element_type=jnp.fl...  79.6 us
    all_gather x2, blocking collectives, combined_all(): gathered = jax.tree.map(lambda a: lax.all_gather(a, axis), part)  68.8 us
    gather x1, local copies, waits for them, and re-layouts, local(): packed = targets[local_ids]  12.8 us
  transfers between devices with their start and end apart: 5, of which 3 were waited for; matrix products, arithmetic and copies ran while one was open for 2% of the time, Pallas kernels for 0%

commit v1 on v0

v1 whole, which is shorter than its diff:
```python
import math

import jax
import jax.numpy as jnp
from jax import lax
from jax.sharding import PartitionSpec as P

EPSILON = 0.1
VERY_LOW = -1e30


def similarity(rows_bf, fetched):
    kernel = jnp.einsum("rd,ctd->rct", rows_bf, fetched, preferred_element_type=jnp.float32)
    return kernel / math.sqrt(rows_bf.shape[1])


def row_part(rows_bf, fetched, potential, live_slots):
    kernel = similarity(rows_bf, fetched)
    logits = (potential.astype(jnp.float32)[None] + kernel) / EPSILON
    logits = jnp.where(live_slots[None, :, None], logits, VERY_LOW)
    top = jnp.max(logits, axis=(1, 2))
    total = jnp.sum(jnp.exp(logits - top[:, None, None]), axis=(1, 2))
    return (top, total)


def col_part(rows_bf, row_potential, fetched, live_slots):
    kernel = similarity(rows_bf, fetched)
    logits = (row_potential[:, None, None] + kernel) / EPSILON
    top = jnp.max(logits, axis=0)
    total = jnp.sum(jnp.exp(logits - top[None]), axis=0)
    top = jnp.where(live_slots[:, None], top, VERY_LOW)
    total = jnp.where(live_slots[:, None], total, 0.0)
    return (top, total)


def local(sources, log_a, targets, g_old, log_b, tile_ids, live_count):
    tiles_own = targets.shape[0]
    width = targets.shape[1]
    slots_per = tile_ids.shape[2]
    me = lax.axis_index("src")
    rows_all = lax.all_gather(sources, "src")
    log_a_all = lax.all_gather(log_a, "src")
    ids_all = lax.all_gather(tile_ids[0], "src")
    live_all = lax.all_gather(live_count[0], "src")
    my_ids = lax.dynamic_index_in_dim(ids_all, me, 1, False) - me * tiles_own
    my_count = lax.dynamic_index_in_dim(live_all, me, 1, False)
    live_slots = jnp.arange(slots_per, dtype=jnp.int32)[None, :] < my_count[:, None]

    def rows_of(item):
        rows_bf, ids, live = item
        return row_part(rows_bf, targets[ids], g_old[ids], live)

    row_top, row_total = lax.map(rows_of, (rows_all, my_ids, live_slots))
    top = lax.pmax(row_top, "src")
    total = lax.psum(row_total * jnp.exp(row_top - top), "src")
    f_all = EPSILON * log_a_all - EPSILON * (top + jnp.log(total))
    f_new = lax.dynamic_index_in_dim(f_all, me, 0, False)

    def cols_of(item):
        rows_bf, f_rows, ids, live = item
        return col_part(rows_bf, f_rows, targets[ids], live)

    col_top, col_total = lax.map(cols_of, (rows_all, f_all, my_ids, live_slots))
    flat_ids = my_ids.reshape(-1)
    flat_top = col_top.reshape(-1, width)
    flat_total = col_total.reshape(-1, width)
    onehot = flat_ids[:, None] == jnp.arange(tiles_own, dtype=jnp.int32)[None, :]
    tile_top = jnp.max(jnp.where(onehot[:, :, None], flat_top[:, None, :], VERY_LOW), axis=0)
    scaled = flat_total[:, None, :] * jnp.exp(
        jnp.minimum(flat_top[:, None, :] - tile_top[None], 0.0)
    )
    tile_total = jnp.sum(jnp.where(onehot[:, :, None], scaled, 0.0), axis=0)
    all_top = lax.pmax(tile_top, "loop")
    all_total = lax.psum(tile_total * jnp.exp(tile_top - all_top), "loop")
    g_new = EPSILON * log_b - EPSILON * (all_top + jnp.log(all_total))
    return (f_new, g_new)


def solution(mesh):
    return jax.shard_map(
        local,
        mesh=mesh,
        in_specs=(
            P(("src", "loop"), None),
            P(("src", "loop")),
            P("src", None, None),
            P("src", None),
            P("src", None),
            P(("src", "loop"), None, None),
            P(("src", "loop"), None),
        ),
        out_specs=(P(("src", "loop")), P("src", None)),
        check_vma=False,
    )
```

time: 629 us -> 505 us (0.80)
  waiting for transfers between devices: 406 us -> 18.7 us
  blocking collectives: 68.8 us -> 244 us
  local copies, waits for them, and re-layouts: 18.8 us -> 134 us
  starting transfers between devices: 25.2 us -> 0.04 us
  between operations: 0.84 us -> 14.1 us
  other arithmetic: 27.5 us -> 18.2 us
  matrix products: 79.6 us -> 70.9 us
    all_to_all x5 -> x0, waiting for transfers between devices: 406 us -> none  [the longest x1 394 us: local(): lax.all_to_all(packed, 'src', split_axis=0, concat_axis=0, tiled=True)]
    gather x3 -> x48, local copies, waits for them, and re-layouts: 14.1 us -> 130 us  [the longest x32 75.1 us: rows_of(): return row_part(rows_bf, targets[ids], g_old[ids], live)]
    pmax x0 -> x2, blocking collectives: none -> 97.1 us  [the longest x1 55.7 us: local(): top = lax.pmax(row_top, 'src')]
    psum x0 -> x2, blocking collectives: none -> 89.6 us  [the longest x1 52.9 us: local(): total = lax.psum(row_total * jnp.exp(row_top - top), 'src')]
    all_to_all x5 -> x0, starting transfers between devices: 25.2 us -> none  [the longest x1 6.46 us: local(): lax.all_to_all(requested, 'src', split_axis=0, concat_axis=0, tiled=True)]
    all_gather x0 -> x1, waiting for transfers between devices: none -> 18 us  [local(): rows_all = lax.all_gather(sources, 'src')]
    all_gather x2 -> x3, blocking collectives: 68.8 us -> 56.9 us  [the longest x1 21.4 us: local(): ids_all = lax.all_gather(tile_ids[0], 'src')]
    dynamic_update_slice x16, other arithmetic: 10.8 us -> 1.36 us  [local(): col_top, col_total = lax.map(cols_of, (rows_all, f_all, my_ids, live_slots))]
  transfers between devices with their start and end apart: 5 -> 1, of which waited for: 3 -> 1; matrix products, arithmetic and copies ran while one was open for 2% -> 0% of each run, Pallas kernels for 0% -> 0%
where the time goes in v1:
time: 505 us; the launch traced here: 501 us
  blocking collectives  244 us (48%)
  local copies, waits for them, and re-layouts  134 us (27%)
  matrix products  70.9 us (14%)
  waiting for transfers between devices  18.7 us (4%)
  other arithmetic  18.2 us (4%)
  between operations  14.1 us (3%)
    gather x32, local copies, waits for them, and re-layouts, rows_of(): return row_part(rows_bf, targets[ids], g_old[ids], live)  75.1 us
    dot_general x32, matrix products, similarity(): jnp.einsum('rd,ctd->rct', rows_bf, fetched, preferred_element_type=jnp.fl...  70.9 us
    pmax x1, blocking collectives, local(): top = lax.pmax(row_top, 'src')  55.7 us
    gather x16, local copies, waits for them, and re-layouts, cols_of(): return col_part(rows_bf, f_rows, targets[ids], live)  54.9 us
    psum x1, blocking collectives, local(): total = lax.psum(row_total * jnp.exp(row_top - top), 'src')  52.9 us
    pmax x1, blocking collectives, local(): all_top = lax.pmax(tile_top, 'loop')  41.4 us
    psum x1, blocking collectives, local(): all_total = lax.psum(tile_total * jnp.exp(tile_top - all_top), 'loop')  36.6 us
    all_gather x1, blocking collectives, local(): ids_all = lax.all_gather(tile_ids[0], 'src')  21.4 us
  transfers between devices with their start and end apart: 1, of which 1 were waited for; matrix products, arithmetic and copies ran while one was open for 0% of the time, Pallas kernels for 0%

profile of v1, /device:TPU:0, one launch (start us, length us, event | category | flops | bytes accessed | tf_op | source)
XLA Modules:
  0.0 501.2 jit_solution(8894537044187313514)
XLA Ops:
  7.9 21.4 %all_gather.21 = s32[16,16,2]{1,2,0:T(2,128)S(1)} all-gather(s32[1,16,2]{1,2,0:T(2,128)} %param.16), channel_id=1, replica_groups=mesh['src'=16,'loop'=8] {'src'}, dimensions={0}, use_global_device_ids=true | all-gather | bytes 2176 | tf_op jit(solution)/shard_map/all_gather | solution.py:43
  30.1 17.0 %all-gather.3 = s32[16,1,16]{2,1,0:T(1,128)S(1)} all-gather(s32[1,1,16]{2,1,0:T(1,128)} %bitcast.87), channel_id=1, replica_groups=mesh['src'=16,'loop'=8] {'src'}, dimensions={0}, use_global_device_ids=true | all-gather | bytes 1088 | tf_op jit(solution)/shard_map/all_gather | solution.py:44
  47.5 18.6 %all-gather.2 = f32[16,1,512]{2,1,0:T(1,128)S(1)} all-gather(f32[1,1,512]{2,1,0:T(1,128)} %bitcast.85), channel_id=2, replica_groups=mesh['src'=16,'loop'=8] {'src'}, dimensions={0}, use_global_device_ids=true | all-gather | bytes 34816 | tf_op jit(solution)/shard_map/all_gather | solution.py:42
  66.2 18.0 %all-gather.6.cloned.1.call-done = bf16[8192,768]{1,0:T(8,128)(2,1)} async-done(((bf16[512,768]{1,0:T(8,128)(2,1)}), bf16[8192,768]{1,0:T(8,128)(2,1)}) %all-gather.6.cloned.1.call-update) | async-done | bytes 12582928 | tf_op jit(solution)/shard_map/all_gather | solution.py:41
  84.2 120.7 %while.24 = (s32[]{:T(128)}, f32[16,512]{1,0:T(8,128)S(1)}, f32[16,512]{1,0:T(8,128)S(1)}, pred[16,2]{1,0:T(8,128)(4,1)S(1)}, s32[16,2]{1,0:T(8,128)S(1)}, /*ind...) while((s32[]{:T(128)}, f32[16,512]{1,0:T(8,128)S(1)}, ...), condition=%wide.region_3.4_spmd, body=%wide.region_0.3_spmd.sunk | while | flops 808977408 | bytes 9732271 | solution.py:53
  85.5 3.4 gather_fusion
  100.6 3.4 gather_fusion
  108.1 3.4 gather_fusion
  115.7 3.4 gather_fusion
  123.2 3.4 gather_fusion
  153.4 3.4 gather_fusion
  161.0 3.4 gather_fusion
  168.5 3.4 gather_fusion
  198.7 3.4 gather_fusion
  204.9 55.7 %pmax.14 = f32[16,512]{1,0:T(8,128)S(1)} all-reduce(f32[16,512]{1,0:T(8,128)S(1)} %get-tuple-element.88), channel_id=1, replica_groups=mesh['src'=16,'loop'=8] {'src'}, use_global_device_ids=true, to_apply=%region_4.5 | all-reduce | flops 8192 | bytes 65536 | tf_op jit(solution)/shard_map/pmax | solution.py:54
  260.7 52.9 %psum.14 = f32[16,512]{1,0:T(8,128)S(1)} all-reduce(f32[16,512]{1,0:T(8,128)S(1)} %exponential_multiply_fusion), channel_id=1, replica_groups=mesh['src'=16,'loop'=8] {'src'}, use_global_device_ids=true, to_apply=%region_5.6 | all-reduce | flops 8192 | bytes 65536 | tf_op jit(solution)/shard_map/psum | solution.py:55
  314.2 101.2 %while.25 = (s32[]{:T(128)}, f32[16,2,512]{2,1,0:T(2,128)S(1)}, f32[16,2,512]{2,1,0:T(2,128)S(1)}, pred[16,2]{1,0:T(8,128)(4,1)S(1)}, f32[16,512]{1,0:T(8,128)S(...) while((s32[]{:T(128)}, f32[16,2,512]{2,1,0:T(2,128)S(1)}, ...), condition=%wide.region_9.10_spmd, body=%wide.region_6.9_spmd.sunk | while | flops 810025984 | bytes 9740957 | solution.py:63
  314.2 3.4 gather_fusion.2
  326.9 3.4 gather_fusion.2
  339.5 3.4 gather_fusion.2
  352.2 3.4 gather_fusion.2
  364.8 3.4 gather_fusion.2
  415.6 41.4 %pmax.15 = f32[8,512]{1,0:T(8,128)S(1)} all-reduce(f32[8,512]{1,0:T(8,128)S(1)} %select_reduce_fusion.1), channel_id=1, replica_groups=mesh['src'=16,'loop'=8] {'loop'}, use_global_device_ids=true, to_apply=%region_11.12 | all-reduce | flops 4096 | bytes 32768 | tf_op jit(solution)/shard_map/pmax | solution.py:73
  457.1 36.6 %psum.15 = f32[8,512]{1,0:T(8,128)S(1)} all-reduce(f32[8,512]{1,0:T(8,128)S(1)} %exponential_multiply_fusion.1), channel_id=1, replica_groups=mesh['src'=16,'loop'=8] {'loop'}, use_global_device_ids=true, to_apply=%region_13.14 | all-reduce | flops 4096 | bytes 32768 | tf_op jit(solution)/shard_map/psum | solution.py:74
  (299 shorter events, 175.8 us)
Async XLA Ops:
  7.2 77.0 %all-gather.6.cloned.1.call-start = ((), (), s32[]{:S(2)}) async-start(), calls=%async_computation | async-start | bytes 13369344 | tf_op jit(solution)/shard_map/all_gather | solution.py:41
  314.2 179.6 %copy-start = (f32[8,512]{1,0:T(8,128)S(1)}, f32[8,512]{1,0:T(8,128)}, u32[]{:S(2)}) copy-start(f32[8,512]{1,0:T(8,128)} %param.15) | copy-start | bytes 49156
Sparse Core Ops, SparseCore 0:
  9.7 74.4 all-gather.5

commit v2 on v1

v2 whole, which is shorter than its diff:
```python
import math

import jax
import jax.numpy as jnp
from jax import lax
from jax.experimental import pallas as pl
from jax.experimental.pallas import tpu as pltpu
from jax.sharding import PartitionSpec as P

EPSILON = 0.1
VERY_LOW = -1e30
NT_DIMS = (((1,), (1,)), ((), ()))


def row_kernel(ids_ref, cnt_ref, g_ref, t_ref, x_ref, top_ref, tot_ref, *, scale):
    s = pl.program_id(0)
    c = pl.program_id(1)

    @pl.when(c == 0)
    def _():
        top_ref[...] = jnp.full(top_ref.shape, VERY_LOW, jnp.float32)
        tot_ref[...] = jnp.zeros(tot_ref.shape, jnp.float32)

    @pl.when(c < cnt_ref[s])
    def _():
        kt = lax.dot_general(t_ref[...], x_ref[...], NT_DIMS, preferred_element_type=jnp.float32)
        logits = g_ref[...] + kt * scale
        old = top_ref[...]
        new = jnp.maximum(old, jnp.max(logits, axis=0, keepdims=True))
        tot_ref[...] = tot_ref[...] * jnp.exp(old - new) + jnp.sum(
            jnp.exp(logits - new), axis=0, keepdims=True
        )
        top_ref[...] = new


def col_kernel(ids_ref, cnt_ref, f_ref, x_ref, t_ref, top_ref, tot_ref, *, scale):
    s = pl.program_id(0)
    c = pl.program_id(1)

    @pl.when((s == 0) & (c == 0))
    def _():
        top_ref[...] = jnp.full(top_ref.shape, VERY_LOW, jnp.float32)
        tot_ref[...] = jnp.zeros(tot_ref.shape, jnp.float32)

    @pl.when(c < cnt_ref[s])
    def _():
        k = lax.dot_general(x_ref[...], t_ref[...], NT_DIMS, preferred_element_type=jnp.float32)
        logits = f_ref[...] + k * scale
        t = ids_ref[s, c]
        old = top_ref[t]
        new = jnp.maximum(old, jnp.max(logits, axis=0, keepdims=True))
        tot_ref[t] = tot_ref[t] * jnp.exp(old - new) + jnp.sum(
            jnp.exp(logits - new), axis=0, keepdims=True
        )
        top_ref[t] = new


def pick_tile(s, c, ids_ref, cnt_ref):
    live = c < cnt_ref[s]
    return (jnp.where(live, ids_ref[s, c], ids_ref[s, 0]), 0, 0)


def pass_call(body, ids, cnt, column, x_all, targets, rows, out_rows, scale, transposed):
    blocks, depth = x_all.shape[0], x_all.shape[2]
    slots = ids.shape[1]
    width = targets.shape[1]
    x_spec = pl.BlockSpec((None, rows, depth), lambda s, c, ids_ref, cnt_ref: (s, 0, 0))
    t_spec = pl.BlockSpec((None, width, depth), pick_tile)
    if transposed:
        col_spec = pl.BlockSpec((None, width, 1), pick_tile)
        in_specs = [col_spec, t_spec, x_spec]
        operands = (column, targets, x_all)
        out_spec = pl.BlockSpec((None, 1, rows), lambda s, c, ids_ref, cnt_ref: (s, 0, 0))
        out_shape = jax.ShapeDtypeStruct((out_rows, 1, rows), jnp.float32)
    else:
        col_spec = pl.BlockSpec((None, rows, 1), lambda s, c, ids_ref, cnt_ref: (s, 0, 0))
        in_specs = [col_spec, x_spec, t_spec]
        operands = (column, x_all, targets)
        out_spec = pl.BlockSpec((out_rows, 1, width), lambda s, c, ids_ref, cnt_ref: (0, 0, 0))
        out_shape = jax.ShapeDtypeStruct((out_rows, 1, width), jnp.float32)
    flops = 2 * blocks * slots * rows * width * depth
    cost = pl.CostEstimate(
        flops=flops,
        transcendentals=blocks * slots * rows * width,
        bytes_accessed=2 * (x_all.size + blocks * slots * width * depth),
    )
    return pl.pallas_call(
        lambda *refs: body(*refs, scale=scale),
        out_shape=(out_shape, out_shape),
        grid_spec=pltpu.PrefetchScalarGridSpec(
            num_scalar_prefetch=2,
            grid=(blocks, slots),
            in_specs=in_specs,
            out_specs=(out_spec, out_spec),
        ),
        compiler_params=pltpu.CompilerParams(dimension_semantics=("arbitrary", "arbitrary")),
        cost_estimate=cost,
    )(ids, cnt, *operands)


def local(sources, log_a, targets, g_old, log_b, tile_ids, live_count):
    tiles_own, width, depth = targets.shape
    rows = sources.shape[0]
    slots_per = tile_ids.shape[2]
    groups = tile_ids.shape[1]
    me = lax.axis_index("src")
    scale = 1.0 / (math.sqrt(depth) * EPSILON)

    meta = jnp.concatenate([tile_ids[0].reshape(-1), live_count[0].reshape(-1)])
    meta_rows = jnp.zeros((16, depth), jnp.bfloat16).at[0, : meta.shape[0]].set(
        meta.astype(jnp.bfloat16)
    )
    packed = jnp.concatenate([sources, meta_rows], axis=0)
    x_all = lax.all_gather(packed, "src")
    meta_all = x_all[:, rows, : meta.shape[0]].astype(jnp.int32)
    blocks = x_all.shape[0]
    ids_all = meta_all[:, : groups * slots_per].reshape(blocks, groups, slots_per)
    cnt_all = meta_all[:, groups * slots_per :]
    my_ids = jnp.clip(lax.dynamic_index_in_dim(ids_all, me, 1, False) - me * tiles_own, 0, tiles_own - 1)
    my_cnt = lax.dynamic_index_in_dim(cnt_all, me, 1, False)

    g_col = (g_old.astype(jnp.float32) / EPSILON)[:, :, None]
    row_top, row_total = pass_call(
        row_kernel, my_ids, my_cnt, g_col, x_all, targets, rows, blocks, scale, True
    )
    stats = jnp.concatenate(
        [row_top.reshape(blocks, rows), row_total.reshape(blocks, rows), log_a[None]], axis=0
    )
    stats_all = lax.all_gather(stats, "src")
    tops = stats_all[:, :blocks]
    top = jnp.max(tops, axis=0)
    total = jnp.sum(stats_all[:, blocks : 2 * blocks] * jnp.exp(tops - top[None]), axis=0)
    log_a_all = stats_all[:, 2 * blocks]
    f_all = EPSILON * log_a_all - EPSILON * (top + jnp.log(total))
    f_new = lax.dynamic_index_in_dim(f_all, me, 0, False)

    f_col = (f_all / EPSILON)[:, :, None]
    tile_top, tile_total = pass_call(
        col_kernel, my_ids, my_cnt, f_col, x_all, targets, rows, tiles_own, scale, False
    )
    col = jnp.concatenate([tile_top.reshape(tiles_own, width), tile_total.reshape(tiles_own, width)])
    col_all = lax.all_gather(col, "loop")
    tops = col_all[:, :tiles_own]
    all_top = jnp.max(tops, axis=0)
    all_total = jnp.sum(col_all[:, tiles_own:] * jnp.exp(tops - all_top[None]), axis=0)
    g_new = EPSILON * log_b - EPSILON * (all_top + jnp.log(all_total))
    return (f_new, g_new)


def solution(mesh):
    return jax.shard_map(
        local,
        mesh=mesh,
        in_specs=(
            P(("src", "loop"), None),
            P(("src", "loop")),
            P("src", None, None),
            P("src", None),
            P("src", None),
            P(("src", "loop"), None, None),
            P(("src", "loop"), None),
        ),
        out_specs=(P(("src", "loop")), P("src", None)),
        check_vma=False,
    )
```

time: 505 us -> 258 us (0.51)
  blocking collectives: 244 us -> 34.4 us
  local copies, waits for them, and re-layouts: 134 us -> 9.53 us
  waiting for transfers between devices: 18.7 us -> 108 us
  Pallas kernels: 0 us -> 75.8 us
  matrix products: 70.9 us -> 0 us
    gather x48 -> x0, local copies, waits for them, and re-layouts: 130 us -> none  [the longest x32 75.1 us: rows_of(): return row_part(rows_bf, targets[ids], g_old[ids], live)]
    pmax x2 -> x0, blocking collectives: 97.1 us -> none  [the longest x1 55.7 us: local(): top = lax.pmax(row_top, 'src')]
    all_gather x1 -> x2, waiting for transfers between devices: 18 us -> 108 us  [the longest x1 73.6 us: local(): x_all = lax.all_gather(packed, 'src')]
    psum x2 -> x0, blocking collectives: 89.6 us -> none  [the longest x1 52.9 us: local(): total = lax.psum(row_total * jnp.exp(row_top - top), 'src')]
    pallas_call x0 -> x2, Pallas kernels: none -> 75.8 us  [pass_call(): pl.pallas_call(lambda *refs: body(*refs, scale=scale), out_shape=(out_sha...]
    dot_general x32 -> x0, matrix products: 70.9 us -> none  [similarity(): jnp.einsum('rd,ctd->rct', rows_bf, fetched, preferred_element_type=jnp.fl...]
    all_gather x3 -> x1, blocking collectives: 56.9 us -> 34.4 us  [local(): col_all = lax.all_gather(col, 'loop')]
    reduce_sum x33 -> x2, other arithmetic: 14.9 us -> 1.35 us  [the longest x1 1.32 us: local(): jnp.sum(stats_all[:, blocks:2 * blocks] * jnp.exp(tops - top[None]), axis=0)]
  transfers between devices with their start and end apart: 1 -> 2, of which waited for: 1 -> 2; matrix products, arithmetic and copies ran while one was open for 0% -> 1% of each run, Pallas kernels for 0% -> 0%
where the time goes in v2:
time: 258 us; the launch traced here: 256 us
  waiting for transfers between devices  108 us (42%)
  Pallas kernels  75.8 us (29%)
  blocking collectives  34.4 us (13%)
  between operations  14.1 us (5%)
  other arithmetic  13.8 us (5%)
  local copies, waits for them, and re-layouts  9.53 us (4%)
    pallas_call x2, Pallas kernels, pass_call(): pl.pallas_call(lambda *refs: body(*refs, scale=scale), out_shape=(out_sha...  75.8 us
    all_gather x1, waiting for transfers between devices, local(): x_all = lax.all_gather(packed, 'src')  73.6 us
    all_gather x1, waiting for transfers between devices, local(): stats_all = lax.all_gather(stats, 'src')  34.6 us
    all_gather x1, blocking collectives, local(): col_all = lax.all_gather(col, 'loop')  34.4 us
  transfers between devices with their start and end apart: 2, of which 2 were waited for; matrix products, arithmetic and copies ran while one was open for 1% of the time, Pallas kernels for 0%

profile of v2, /device:TPU:0, one launch (start us, length us, event | category | flops | bytes accessed | tf_op | source)
XLA Modules:
  0.0 256.0 jit_solution(17632915987858322906)
XLA Ops:
  7.2 0.7 convert.8
  7.9 0.7 convert.9
  8.8 2.1 pad_maximum_fusion
  11.0 0.7 multiply_bitcast_fusion
  11.7 2.0 copy.38.refs_2_
  13.7 73.6 %all-gather.7.cloned.1.call-done = bf16[8448,768]{1,0:T(8,128)(2,1)} async-done(((bf16[528,768]{1,0:T(8,128)(2,1)}), bf16[8448,768]{1,0:T(8,128)(2,1)}) %all-gather.7.cloned.1.call-update) | async-done | bytes 12976144 | tf_op jit(solution)/shard_map/all_gather | solution.py:114
  87.3 0.8 slice_convert_fusion
  88.2 0.7 dynamic-slice_reduce_fusion.refs_1_
  88.9 0.7 copy.37.refs_0_
  89.6 38.1 %shard_map.86 = (f32[16,1,512]{2,1,0:T(1,128)}, f32[16,1,512]{2,1,0:T(1,128)}) custom-call(s32[16,2]{1,0:T(8,128)} %copy.37.refs_0_, s32[16]{0:T(128)} %dynamic-slice_reduce_fusion.refs_1_, f32[8,512,1]{2,1,0:T(8,128)} %copy.38.refs_2_, bf16[8,512,768]{2,1,0:T(8,128)(2,1)} %refs_4_.1, bf16[16,528,768]{2,1,0:T(8,128)(2,1)} %bitcast.39), custom_call_target="tpu_custom_call" | custom-call | flops 12884901888 | bytes 38141952 | tf_op jit(solution)/shard_map/pallas_call | solution.py:87
  127.7 0.8 copy_bitcast_fusion
  128.5 0.6 maximum_bitcast_fusion
  129.2 34.6 %all-gather.9.cloned.1.call-done = f32[16,33,512]{2,1,0:T(8,128)} async-done(((f32[1,33,512]{2,1,0:T(8,128)}), f32[16,33,512]{2,1,0:T(8,128)}) %all-gather.9.cloned.1.call-update) | async-done | bytes 1081360 | tf_op jit(solution)/shard_map/all_gather | solution.py:129
  163.8 1.0 slice.51
  164.8 1.1 slice_reduce_fusion
  165.8 1.3 fusion
  167.2 2.6 %copy.40 = f32[16,512,1]{2,1,0:T(8,128)} copy(f32[16,512,1]{1,0,2:T(8,128)S(1)} %get-tuple-element.22) | data formatting | bytes 65536 | tf_op jit(solution)/shard_map/sub | solution.py:134
  169.8 4.5 %broadcast_multiply_fusion.refs_2_ = f32[16,512,1]{2,1,0:T(8,128)} fusion(f32[16,512,1]{2,1,0:T(8,128)} %copy.40), kind=kLoop, calls=%fused_computation | loop fusion | flops 8192 | bytes 65536 | tf_op jit(solution)/shard_map/div | solution.py:137
  174.4 37.7 %shard_map.87 = (f32[8,1,512]{2,1,0:T(1,128)}, f32[8,1,512]{2,1,0:T(1,128)}) custom-call(s32[16,2]{1,0:T(8,128)} %copy.37.refs_0_, s32[16]{0:T(128)} %dynamic-slice_reduce_fusion.refs_1_, f32[16,512,1]{2,1,0:T(8,128)} %broadcast_multiply_fusion.refs_2_, bf16[16,528,768]{2,1,0:T(8,128)(2,1)} %bitcast.40, bf16[8,512,768]{2,1,0:T(8,128)(2,1)} %refs_4_.1), custom_call_target="tpu_custom_call" | custom-call | flops 12884901888 | bytes 38141952 | tf_op jit(solution)/shard_map/pallas_call | solution.py:87
  212.1 0.7 copy.57
  212.8 0.7 copy.56
  213.5 34.4 %all-gather.2 = f32[128,512]{1,0:T(8,128)S(1)} all-gather(f32[16,512]{1,0:T(8,128)S(1)} %pad_maximum_fusion.1), channel_id=4, replica_groups=mesh['src'=16,'loop'=8] {'loop'}, dimensions={0}, use_global_device_ids=true | all-gather | bytes 294912 | tf_op jit(solution)/shard_map/all_gather | solution.py:142
  248.0 0.6 dynamic-slice_subtract_fusion
  248.5 0.6 multiply_subtract_fusion
  (19 shorter events, 0.6 us)
Async XLA Ops:
  7.2 80.1 %all-gather.7.cloned.1.call-start = ((), (), s32[]{:S(2)}) async-start(), calls=%async_computation | async-start | bytes 13787136 | tf_op jit(solution)/shard_map/all_gather | solution.py:114
  10.9 152.8 %all-gather.9.cloned.1.call-start = ((), (), s32[]{:S(2)}) async-start(), calls=%async_computation.1 | async-start | bytes 1392640 | tf_op jit(solution)/shard_map/all_gather | solution.py:129
  89.6 38.9 %copy-start.1 = (f32[512]{0:T(512)S(1)}, f32[512]{0:T(512)}, u32[]{:S(2)}) copy-start(f32[512]{0:T(512)} %param.10) | copy-start | bytes 6148
  174.4 74.2 %copy-start = (f32[8,512]{1,0:T(8,128)S(1)}, f32[8,512]{1,0:T(8,128)}, u32[]{:S(2)}) copy-start(f32[8,512]{1,0:T(8,128)} %param.13) | copy-start | bytes 49156
Sparse Core Ops, SparseCore 0:
  11.1 76.1 all-gather.6
  129.3 34.4 all-gather.8

commit v3 on v2

v3 whole, which is shorter than its diff:
```python
import math

import jax
import jax.numpy as jnp
from jax import lax
from jax.experimental import pallas as pl
from jax.experimental.pallas import tpu as pltpu
from jax.sharding import PartitionSpec as P

EPSILON = 0.1
VERY_LOW = -1e30
NT_DIMS = (((1,), (1,)), ((), ()))


def row_kernel(ids_ref, cnt_ref, g_ref, t_ref, x_ref, top_ref, tot_ref, k_ref, *, scale):
    s = pl.program_id(0)
    c = pl.program_id(1)

    @pl.when(c == 0)
    def _():
        top_ref[...] = jnp.full(top_ref.shape, VERY_LOW, jnp.float32)
        tot_ref[...] = jnp.zeros(tot_ref.shape, jnp.float32)

    @pl.when(c < cnt_ref[s])
    def _():
        kt = lax.dot_general(t_ref[...], x_ref[...], NT_DIMS, preferred_element_type=jnp.float32)
        kt = kt * scale
        k_ref[...] = kt
        logits = g_ref[...] + kt
        old = top_ref[...]
        new = jnp.maximum(old, jnp.max(logits, axis=0, keepdims=True))
        tot_ref[...] = tot_ref[...] * jnp.exp(old - new) + jnp.sum(
            jnp.exp(logits - new), axis=0, keepdims=True
        )
        top_ref[...] = new


def col_kernel(ids_ref, cnt_ref, f_ref, k_ref, top_ref, tot_ref):
    s = pl.program_id(0)
    c = pl.program_id(1)

    @pl.when((s == 0) & (c == 0))
    def _():
        top_ref[...] = jnp.full(top_ref.shape, VERY_LOW, jnp.float32)
        tot_ref[...] = jnp.zeros(tot_ref.shape, jnp.float32)

    @pl.when(c < cnt_ref[s])
    def _():
        logits = k_ref[...] + f_ref[...]
        t = ids_ref[s, c]
        old = top_ref[t]
        new = jnp.maximum(old, jnp.max(logits, axis=1, keepdims=True))
        tot_ref[t] = tot_ref[t] * jnp.exp(old - new) + jnp.sum(
            jnp.exp(logits - new), axis=1, keepdims=True
        )
        top_ref[t] = new


def pick_tile(s, c, ids_ref, cnt_ref):
    live = c < cnt_ref[s]
    return (jnp.where(live, ids_ref[s, c], ids_ref[s, 0]), 0, 0)


def pick_slot(s, c, ids_ref, cnt_ref):
    return (s, jnp.where(c < cnt_ref[s], c, 0), 0, 0)


def row_call(ids, cnt, g_col, targets, x_all, rows, scale):
    blocks, depth = x_all.shape[0], x_all.shape[2]
    slots = ids.shape[1]
    width = targets.shape[1]
    stat_spec = pl.BlockSpec((None, 1, rows), lambda s, c, ids_ref, cnt_ref: (s, 0, 0))
    stat_shape = jax.ShapeDtypeStruct((blocks, 1, rows), jnp.float32)
    cost = pl.CostEstimate(
        flops=2 * blocks * slots * rows * width * depth,
        transcendentals=blocks * slots * rows * width,
        bytes_accessed=2 * (x_all.size + blocks * slots * width * depth)
        + 4 * blocks * slots * rows * width,
    )
    return pl.pallas_call(
        lambda *refs: row_kernel(*refs, scale=scale),
        out_shape=(
            stat_shape,
            stat_shape,
            jax.ShapeDtypeStruct((blocks, slots, width, rows), jnp.float32),
        ),
        grid_spec=pltpu.PrefetchScalarGridSpec(
            num_scalar_prefetch=2,
            grid=(blocks, slots),
            in_specs=[
                pl.BlockSpec((None, width, 1), pick_tile),
                pl.BlockSpec((None, width, depth), pick_tile),
                pl.BlockSpec((None, rows, depth), lambda s, c, ids_ref, cnt_ref: (s, 0, 0)),
            ],
            out_specs=(stat_spec, stat_spec, pl.BlockSpec((None, None, width, rows), pick_slot)),
        ),
        compiler_params=pltpu.CompilerParams(dimension_semantics=("arbitrary", "arbitrary")),
        cost_estimate=cost,
    )(ids, cnt, g_col, targets, x_all)


def col_call(ids, cnt, f_row, k_all, tiles_own):
    blocks, slots, width, rows = k_all.shape
    acc_spec = pl.BlockSpec((tiles_own, width, 1), lambda s, c, ids_ref, cnt_ref: (0, 0, 0))
    acc_shape = jax.ShapeDtypeStruct((tiles_own, width, 1), jnp.float32)
    cost = pl.CostEstimate(
        flops=4 * blocks * slots * rows * width,
        transcendentals=blocks * slots * rows * width,
        bytes_accessed=4 * blocks * slots * rows * width,
    )
    return pl.pallas_call(
        col_kernel,
        out_shape=(acc_shape, acc_shape),
        grid_spec=pltpu.PrefetchScalarGridSpec(
            num_scalar_prefetch=2,
            grid=(blocks, slots),
            in_specs=[
                pl.BlockSpec((None, 1, rows), lambda s, c, ids_ref, cnt_ref: (s, 0, 0)),
                pl.BlockSpec((None, None, width, rows), pick_slot),
            ],
            out_specs=(acc_spec, acc_spec),
        ),
        compiler_params=pltpu.CompilerParams(dimension_semantics=("arbitrary", "arbitrary")),
        cost_estimate=cost,
    )(ids, cnt, f_row, k_all)


def local(sources, log_a, targets, g_old, log_b, tile_ids, live_count):
    tiles_own, width, depth = targets.shape
    rows = sources.shape[0]
    slots_per = tile_ids.shape[2]
    groups = tile_ids.shape[1]
    me = lax.axis_index("src")
    scale = 1.0 / (math.sqrt(depth) * EPSILON)

    meta = jnp.concatenate([tile_ids[0].reshape(-1), live_count[0].reshape(-1)])
    meta_rows = jnp.zeros((16, depth), jnp.bfloat16).at[0, : meta.shape[0]].set(
        meta.astype(jnp.bfloat16)
    )
    packed = jnp.concatenate([sources, meta_rows], axis=0)
    x_all = lax.all_gather(packed, "src")
    meta_all = x_all[:, rows, : meta.shape[0]].astype(jnp.int32)
    blocks = x_all.shape[0]
    ids_all = meta_all[:, : groups * slots_per].reshape(blocks, groups, slots_per)
    cnt_all = meta_all[:, groups * slots_per :]
    my_ids = jnp.clip(lax.dynamic_index_in_dim(ids_all, me, 1, False) - me * tiles_own, 0, tiles_own - 1)
    my_cnt = lax.dynamic_index_in_dim(cnt_all, me, 1, False)

    g_col = (g_old.astype(jnp.float32) / EPSILON)[:, :, None]
    row_top, row_total, k_all = row_call(my_ids, my_cnt, g_col, targets, x_all, rows, scale)
    stats = jnp.concatenate(
        [row_top.reshape(blocks, rows), row_total.reshape(blocks, rows), log_a[None]], axis=0
    )
    stats_all = lax.all_gather(stats, "src")
    tops = stats_all[:, :blocks]
    top = jnp.max(tops, axis=0)
    total = jnp.sum(stats_all[:, blocks : 2 * blocks] * jnp.exp(tops - top[None]), axis=0)
    log_a_all = stats_all[:, 2 * blocks]
    f_all = EPSILON * log_a_all - EPSILON * (top + jnp.log(total))
    f_new = lax.dynamic_index_in_dim(f_all, me, 0, False)

    f_row = (f_all / EPSILON)[:, None, :]
    tile_top, tile_total = col_call(my_ids, my_cnt, f_row, k_all, tiles_own)
    col = jnp.concatenate([tile_top.reshape(tiles_own, width), tile_total.reshape(tiles_own, width)])
    loop_size = lax.axis_size("loop")
    col_all = lax.all_to_all(
        jnp.broadcast_to(col[None], (loop_size,) + col.shape), "loop", 0, 0, tiled=True
    )
    tops = col_all[:, :tiles_own]
    all_top = jnp.max(tops, axis=0)
    all_total = jnp.sum(col_all[:, tiles_own:] * jnp.exp(tops - all_top[None]), axis=0)
    g_new = EPSILON * log_b - EPSILON * (all_top + jnp.log(all_total))
    return (f_new, g_new)


def solution(mesh):
    return jax.shard_map(
        local,
        mesh=mesh,
        in_specs=(
            P(("src", "loop"), None),
            P(("src", "loop")),
            P("src", None, None),
            P("src", None),
            P("src", None),
            P(("src", "loop"), None, None),
            P(("src", "loop"), None),
        ),
        out_specs=(P(("src", "loop")), P("src", None)),
        check_vma=False,
    )
```

time: 258 us -> 233 us (0.903)
  blocking collectives: 34.4 us -> 0 us
  waiting for transfers between devices: 108 us -> 117 us
  starting transfers between devices: 0.08 us -> 5.98 us
  local copies, waits for them, and re-layouts: 9.53 us -> 6.18 us
    all_gather x1 -> x0, blocking collectives: 34.4 us -> none  [local(): col_all = lax.all_gather(col, 'loop')]
    all_to_all x0 -> x1, waiting for transfers between devices: none -> 8.6 us  [local(): lax.all_to_all(jnp.broadcast_to(col[None], (loop_size,) + col.shape), 'lo...]
    all_to_all x0 -> x1, starting transfers between devices: none -> 5.9 us  [local(): lax.all_to_all(jnp.broadcast_to(col[None], (loop_size,) + col.shape), 'lo...]
    div x1, other arithmetic: 4.52 us -> 0.65 us  [local(): f_row = (f_all / EPSILON)[:, None, :]]
    pallas_call x0 -> x2, other arithmetic: none -> 2.96 us  [col_call(): pl.pallas_call(col_kernel, out_shape=(acc_shape, acc_shape), grid_spec=pl...]
    sub x1 -> x0, local copies, waits for them, and re-layouts: 2.65 us -> none  [local(): f_all = EPSILON * log_a_all - EPSILON * (top + jnp.log(total))]
  transfers between devices with their start and end apart: 2 -> 3, of which waited for: 2 -> 3; matrix products, arithmetic and copies ran while one was open for 1% -> 1% of each run, Pallas kernels for 0% -> 0%
where the time goes in v3:
time: 233 us; the launch traced here: 231 us
  waiting for transfers between devices  117 us (50%)
  Pallas kernels  75.7 us (32%)
  between operations  14.1 us (6%)
  other arithmetic  12.2 us (5%)
  local copies, waits for them, and re-layouts  6.18 us (3%)
  starting transfers between devices  5.98 us (3%)
    all_gather x1, waiting for transfers between devices, local(): x_all = lax.all_gather(packed, 'src')  74.3 us
    pallas_call x1, Pallas kernels, row_call(): pl.pallas_call(lambda *refs: row_kernel(*refs, scale=scale), out_shape=(s...  45.3 us
    all_gather x1, waiting for transfers between devices, local(): stats_all = lax.all_gather(stats, 'src')  33.7 us
    pallas_call x1, Pallas kernels, col_call(): pl.pallas_call(col_kernel, out_shape=(acc_shape, acc_shape), grid_spec=pl...  30.5 us
    all_to_all x1, waiting for transfers between devices, local(): lax.all_to_all(jnp.broadcast_to(col[None], (loop_size,) + col.shape), 'lo...  8.6 us
    all_to_all x1, starting transfers between devices, local(): lax.all_to_all(jnp.broadcast_to(col[None], (loop_size,) + col.shape), 'lo...  5.9 us
  transfers between devices with their start and end apart: 3, of which 3 were waited for; matrix products, arithmetic and copies ran while one was open for 1% of the time, Pallas kernels for 0%

profile of v3, /device:TPU:0, one launch (start us, length us, event | category | flops | bytes accessed | tf_op | source)
XLA Modules:
  0.0 230.8 jit_solution(15150561004886795363)
XLA Ops:
  7.2 0.7 convert.8
  7.9 0.7 convert.9
  8.8 2.1 pad_maximum_fusion
  11.0 2.0 copy.30.refs_2_
  13.0 74.3 %all-gather.6.cloned.1.call-done = bf16[8448,768]{1,0:T(8,128)(2,1)} async-done(((bf16[528,768]{1,0:T(8,128)(2,1)}), bf16[8448,768]{1,0:T(8,128)(2,1)}) %all-gather.6.cloned.1.call-update) | async-done | bytes 12976144 | tf_op jit(solution)/shard_map/all_gather | solution.py:141
  87.3 0.8 slice_convert_fusion
  88.2 0.7 dynamic-slice_reduce_fusion.refs_1_.cnt_ref
  88.9 0.7 copy.29.refs_0_.ids_ref
  89.6 45.3 %shard_map.86 = (f32[16,1,512]{2,1,0:T(1,128)}, f32[16,1,512]{2,1,0:T(1,128)}, f32[16,2,512,512]{3,2,1,0:T(8,128)}) custom-call(s32[16,2]{1,0:T(8,128)} %copy.29.refs_0_.ids_ref, s32[16]{0:T(128)} %dynamic-slice_reduce_fusion.refs_1_.cnt_ref, f32[8,512,1]{2,1,0:T(8,128)} %copy.30.refs_2_, bf16[8,512,768]{2,1,0:T(8,128)(2,1)} %refs_3_.1, ...), custom_call_target="tpu_custom_call" | custom-call | flops 12884901888 | bytes 71696384 | tf_op jit(solution)/shard_map/pallas_call | solution.py:80
  134.9 0.8 copy_bitcast_fusion
  135.6 0.7 maximum_bitcast_fusion
  136.3 33.7 %all-gather.8.cloned.1.call-done = f32[16,33,512]{2,1,0:T(8,128)} async-done(((f32[1,33,512]{2,1,0:T(8,128)}), f32[16,33,512]{2,1,0:T(8,128)}) %all-gather.8.cloned.1.call-update) | async-done | bytes 1081360 | tf_op jit(solution)/shard_map/all_gather | solution.py:154
  170.0 1.1 slice_reduce_fusion
  171.1 1.3 fusion
  172.4 1.0 slice.51
  173.4 0.6 fusion.7.f_ref
  174.1 30.5 %shard_map.87 = (f32[8,512,1]{2,1,0:T(8,128)}, f32[8,512,1]{2,1,0:T(8,128)}) custom-call(s32[16,2]{1,0:T(8,128)} %copy.29.refs_0_.ids_ref, s32[16]{0:T(128)} %dynamic-slice_reduce_fusion.refs_1_.cnt_ref, f32[16,1,512]{2,1,0:T(1,128)} %fusion.7.f_ref, f32[16,2,512,512]{3,2,1,0:T(8,128)} %get-tuple-element.21.k_ref), custom_call_target="tpu_custom_call" | custom-call | flops 33554432 | bytes 33554432 | tf_op jit(solution)/shard_map/pallas_call | solution.py:111
  204.5 2.3 %reduce.3 = f32[8,512]{1,0:T(8,128)S(1)} reduce(f32[8,512,1]{2,1,0:T(8,128)} %get-tuple-element.22, f32[]{:T(128)} %constant.70), dimensions={2}, to_apply=%get-tuple-element.22.reduce_sub_computation | reduce | bytes 32772 | tf_op jit(solution)/shard_map/pallas_call | solution.py:111
  206.9 0.6 reduce.4
  207.5 0.7 broadcast_in_dim.8
  208.2 5.9 %all-to-all-start = ((f32[8,16,512]{2,1,0:T(8,128)}), f32[8,16,512]{2,1,0:T(8,128)S(1)}, u32[]{:S(2)}, u32[]{:S(2)}) async-start(f32[8,16,512]{2,1,0:T(8,128)} %broadcast_in_dim.8), calls=%async_computation | async-start | bytes 524288 | tf_op jit(solution)/shard_map/all_to_all | solution.py:166
  214.1 0.6 dynamic-slice_subtract_fusion
  214.7 8.6 %all-to-all-done = f32[8,16,512]{2,1,0:T(8,128)S(1)} async-done(((f32[8,16,512]{2,1,0:T(8,128)}), f32[8,16,512]{2,1,0:T(8,128)S(1)}, u32[]{:S(2)}, u32[]{:S(2)}) %all-to-all-start) | async-done | bytes 262176 | tf_op jit(solution)/shard_map/all_to_all | solution.py:166
  223.4 0.6 multiply_subtract_fusion
  (24 shorter events, 0.6 us)
Async XLA Ops:
  7.2 3.8 %copy-start.2 = (bf16[8,512]{1,0:T(8,128)(2,1)S(1)}, bf16[8,512]{1,0:T(8,128)(2,1)}, u32[]{:S(2)}) copy-start(bf16[8,512]{1,0:T(8,128)(2,1)} %param.12) | copy-start | bytes 24580
  7.2 80.1 %all-gather.6.cloned.1.call-start = ((), (), s32[]{:S(2)}) async-start(), calls=%async_computation.1 | async-start | bytes 13787136 | tf_op jit(solution)/shard_map/all_gather | solution.py:141
  10.9 159.1 %all-gather.8.cloned.1.call-start = ((), (), s32[]{:S(2)}) async-start(), calls=%async_computation.2 | async-start | bytes 1392640 | tf_op jit(solution)/shard_map/all_gather | solution.py:154
  89.6 46.1 %copy-start.3 = (f32[512]{0:T(512)S(1)}, f32[512]{0:T(512)}, u32[]{:S(2)}) copy-start(f32[512]{0:T(512)} %param.10) | copy-start | bytes 6148
  204.5 2.4 %copy-start = (f32[8,512,1]{2,1,0:T(8,128)S(1)}, f32[8,512,1]{2,1,0:T(8,128)}, u32[]{:S(2)}) copy-start(f32[8,512,1]{2,1,0:T(8,128)} %get-tuple-element.23) | copy-start | bytes 49156
  206.9 16.5 %copy-start.1 = (f32[8,512]{1,0:T(8,128)S(1)}, f32[8,512]{1,0:T(8,128)}, u32[]{:S(2)}) copy-start(f32[8,512]{1,0:T(8,128)} %param.13) | copy-start | bytes 49156
  208.2 15.1 %all-to-all-start = ((f32[8,16,512]{2,1,0:T(8,128)}), f32[8,16,512]{2,1,0:T(8,128)S(1)}, u32[]{:S(2)}, u32[]{:S(2)}) async-start(f32[8,16,512]{2,1,0:T(8,128)} %broadcast_in_dim.8), calls=%async_computation | async-start | bytes 524288 | tf_op jit(solution)/shard_map/all_to_all | solution.py:166
Sparse Core Ops, SparseCore 0:
  11.1 76.1 all-gather.5
  136.4 33.5 all-gather.7

commit v4 on v3

--- a/solution.py
+++ b/solution.py
@@ -151,7 +151,9 @@
     stats = jnp.concatenate(
         [row_top.reshape(blocks, rows), row_total.reshape(blocks, rows), log_a[None]], axis=0
     )
-    stats_all = lax.all_gather(stats, "src")
+    stats_all = lax.all_to_all(
+        jnp.broadcast_to(stats[None], (blocks,) + stats.shape), "src", 0, 0, tiled=True
+    )
     tops = stats_all[:, :blocks]
     top = jnp.max(tops, axis=0)
     total = jnp.sum(stats_all[:, blocks : 2 * blocks] * jnp.exp(tops - top[None]), axis=0)

time: 233 us -> 219 us (0.940)
  waiting for transfers between devices: 117 us -> 82.5 us
  blocking collectives: 0 us -> 25.6 us
  other arithmetic: 12.2 us -> 9.31 us
    all_gather x1 -> x0, waiting for transfers between devices: 33.7 us -> none  [local(): stats_all = lax.all_gather(stats, 'src')]
    all_to_all x0 -> x1, blocking collectives: none -> 25.6 us  [local(): lax.all_to_all(jnp.broadcast_to(stats[None], (blocks,) + stats.shape), 's...]
  transfers between devices with their start and end apart: 3 -> 2, of which waited for: 3 -> 2; matrix products, arithmetic and copies ran while one was open for 1% -> 1% of each run, Pallas kernels for 0% -> 0%
where the time goes in v4:
time: 219 us; the launch traced here: 218 us
  waiting for transfers between devices  82.5 us (38%)
  Pallas kernels  73.8 us (34%)
  blocking collectives  25.6 us (12%)
  between operations  14.2 us (6%)
  other arithmetic  9.31 us (4%)
  starting transfers between devices  6.83 us (3%)
  local copies, waits for them, and re-layouts  5.38 us (2%)
    all_gather x1, waiting for transfers between devices, local(): x_all = lax.all_gather(packed, 'src')  74.3 us
    pallas_call x1, Pallas kernels, row_call(): pl.pallas_call(lambda *refs: row_kernel(*refs, scale=scale), out_shape=(s...  43.9 us
    pallas_call x1, Pallas kernels, col_call(): pl.pallas_call(col_kernel, out_shape=(acc_shape, acc_shape), grid_spec=pl...  30 us
    all_to_all x1, blocking collectives, local(): lax.all_to_all(jnp.broadcast_to(stats[None], (blocks,) + stats.shape), 's...  25.6 us
    all_to_all x1, waiting for transfers between devices, local(): lax.all_to_all(jnp.broadcast_to(col[None], (loop_size,) + col.shape), 'lo...  8.14 us
    all_to_all x1, starting transfers between devices, local(): lax.all_to_all(jnp.broadcast_to(col[None], (loop_size,) + col.shape), 'lo...  6.79 us
  transfers between devices with their start and end apart: 2, of which 2 were waited for; matrix products, arithmetic and copies ran while one was open for 1% of the time, Pallas kernels for 0%

profile of v4, /device:TPU:0, one launch (start us, length us, event | category | flops | bytes accessed | tf_op | source)
XLA Modules:
  0.0 217.6 jit_solution(1235245209661875842)
XLA Ops:
  7.2 0.7 convert.8
  7.9 0.7 convert.9
  8.6 0.1 copy.27
  8.7 0.1 concatenate.22
  8.8 2.1 pad_maximum_fusion
  11.0 2.0 copy.30.refs_2_
  12.9 74.3 %all-gather.3.cloned.1.call-done = bf16[8448,768]{1,0:T(8,128)(2,1)} async-done(((bf16[528,768]{1,0:T(8,128)(2,1)}), bf16[8448,768]{1,0:T(8,128)(2,1)}) %all-gather.3.cloned.1.call-update) | async-done | bytes 12976144 | tf_op jit(solution)/shard_map/all_gather | solution.py:141
  87.3 0.8 slice_convert_fusion
  88.2 0.7 dynamic-slice_reduce_fusion.refs_1_.cnt_ref
  88.9 0.7 copy.29.refs_0_.ids_ref
  89.6 43.9 %shard_map.86 = (f32[16,1,512]{2,1,0:T(1,128)}, f32[16,1,512]{2,1,0:T(1,128)}, f32[16,2,512,512]{3,2,1,0:T(8,128)}) custom-call(s32[16,2]{1,0:T(8,128)} %copy.29.refs_0_.ids_ref, s32[16]{0:T(128)} %dynamic-slice_reduce_fusion.refs_1_.cnt_ref, f32[8,512,1]{2,1,0:T(8,128)} %copy.30.refs_2_, bf16[8,512,768]{2,1,0:T(8,128)(2,1)} %refs_3_.1, ...), custom_call_target="tpu_custom_call" | custom-call | flops 12884901888 | bytes 71696384 | tf_op jit(solution)/shard_map/pallas_call | solution.py:80
  133.5 0.8 copy_bitcast_fusion
  134.3 0.1 broadcast_in_dim.10
  134.4 25.6 %all_to_all.10 = f32[16,33,512]{2,1,0:T(8,128)S(1)} all-to-all(f32[16,33,512]{2,1,0:T(8,128)S(1)} %broadcast_in_dim.10), channel_id=1, replica_groups=mesh['src'=16,'loop'=8] {'src'}, dimensions={0} | all-to-all | bytes 2162688 | tf_op jit(solution)/shard_map/all_to_all | solution.py:154
  160.1 0.1 fusion
  160.3 0.6 fusion.7.f_ref
  160.9 30.0 %shard_map.87 = (f32[8,512,1]{2,1,0:T(8,128)}, f32[8,512,1]{2,1,0:T(8,128)}) custom-call(s32[16,2]{1,0:T(8,128)} %copy.29.refs_0_.ids_ref, s32[16]{0:T(128)} %dynamic-slice_reduce_fusion.refs_1_.cnt_ref, f32[16,1,512]{2,1,0:T(1,128)} %fusion.7.f_ref, f32[16,2,512,512]{3,2,1,0:T(8,128)} %get-tuple-element.21.k_ref), custom_call_target="tpu_custom_call" | custom-call | flops 33554432 | bytes 33554432 | tf_op jit(solution)/shard_map/pallas_call | solution.py:111
  190.9 2.3 %reduce.3 = f32[8,512]{1,0:T(8,128)S(1)} reduce(f32[8,512,1]{2,1,0:T(8,128)} %get-tuple-element.22, f32[]{:T(128)} %constant.70), dimensions={2}, to_apply=%get-tuple-element.22.reduce_sub_computation | reduce | bytes 32772 | tf_op jit(solution)/shard_map/pallas_call | solution.py:111
  193.2 0.6 reduce.4
  193.9 0.7 broadcast_in_dim.11
  194.6 6.8 %all-to-all-start.1 = ((f32[8,16,512]{2,1,0:T(8,128)}), f32[8,16,512]{2,1,0:T(8,128)S(1)}, u32[]{:S(2)}, u32[]{:S(2)}) async-start(f32[8,16,512]{2,1,0:T(8,128)} %broadcast_in_dim.11), calls=%async_computation.1 | async-start | bytes 524288 | tf_op jit(solution)/shard_map/all_to_all | solution.py:168
  201.4 0.6 dynamic-slice_subtract_fusion
  202.0 8.1 %all-to-all-done.1 = f32[8,16,512]{2,1,0:T(8,128)S(1)} async-done(((f32[8,16,512]{2,1,0:T(8,128)}), f32[8,16,512]{2,1,0:T(8,128)S(1)}, u32[]{:S(2)}, u32[]{:S(2)}) %all-to-all-start.1) | async-done | bytes 262176 | tf_op jit(solution)/shard_map/all_to_all | solution.py:168
  210.2 0.6 multiply_subtract_fusion
  (23 shorter events, 0.4 us)
Async XLA Ops:
  7.2 3.8 %copy-start.2 = (bf16[8,512]{1,0:T(8,128)(2,1)S(1)}, bf16[8,512]{1,0:T(8,128)(2,1)}, u32[]{:S(2)}) copy-start(bf16[8,512]{1,0:T(8,128)(2,1)} %param.12) | copy-start | bytes 24580
  7.2 80.1 %all-gather.3.cloned.1.call-start = ((), (), s32[]{:S(2)}) async-start(), calls=%async_computation.2 | async-start | bytes 13787136 | tf_op jit(solution)/shard_map/all_gather | solution.py:141
  89.6 44.7 %copy-start.3 = (f32[512]{0:T(512)S(1)}, f32[512]{0:T(512)}, u32[]{:S(2)}) copy-start(f32[512]{0:T(512)} %param.10) | copy-start | bytes 6148
  190.9 2.4 %copy-start = (f32[8,512,1]{2,1,0:T(8,128)S(1)}, f32[8,512,1]{2,1,0:T(8,128)}, u32[]{:S(2)}) copy-start(f32[8,512,1]{2,1,0:T(8,128)} %get-tuple-element.23) | copy-start | bytes 49156
  193.2 16.9 %copy-start.1 = (f32[8,512]{1,0:T(8,128)S(1)}, f32[8,512]{1,0:T(8,128)}, u32[]{:S(2)}) copy-start(f32[8,512]{1,0:T(8,128)} %param.13) | copy-start | bytes 49156
  194.6 15.5 %all-to-all-start.1 = ((f32[8,16,512]{2,1,0:T(8,128)}), f32[8,16,512]{2,1,0:T(8,128)S(1)}, u32[]{:S(2)}, u32[]{:S(2)}) async-start(f32[8,16,512]{2,1,0:T(8,128)} %broadcast_in_dim.11), calls=%async_computation.1 | async-start | bytes 524288 | tf_op jit(solution)/shard_map/all_to_all | solution.py:168
Sparse Core Ops, SparseCore 0:
  11.1 76.1 all-gather.2

commit v5 on v4

--- a/solution.py
+++ b/solution.py
@@ -35,7 +35,10 @@
         top_ref[...] = new
 
 
-def col_kernel(ids_ref, cnt_ref, f_ref, k_ref, top_ref, tot_ref):
+def col_kernel(ids_ref, cnt_ref, *refs):
+    parts = (len(refs) - 2) // 2
+    f_refs, k_refs = refs[:parts], refs[parts : 2 * parts]
+    top_ref, tot_ref = refs[2 * parts :]
     s = pl.program_id(0)
     c = pl.program_id(1)
 
@@ -46,13 +49,16 @@
 
     @pl.when(c < cnt_ref[s])
     def _():
-        logits = k_ref[...] + f_ref[...]
+        logits = [k_ref[...] + f_ref[...] for f_ref, k_ref in zip(f_refs, k_refs)]
         t = ids_ref[s, c]
         old = top_ref[t]
-        new = jnp.maximum(old, jnp.max(logits, axis=1, keepdims=True))
-        tot_ref[t] = tot_ref[t] * jnp.exp(old - new) + jnp.sum(
-            jnp.exp(logits - new), axis=1, keepdims=True
-        )
+        new = old
+        for part in logits:
+            new = jnp.maximum(new, jnp.max(part, axis=1, keepdims=True))
+        acc = tot_ref[t] * jnp.exp(old - new)
+        for part in logits:
+            acc = acc + jnp.sum(jnp.exp(part - new), axis=1, keepdims=True)
+        tot_ref[t] = acc
         top_ref[t] = new
 
 
@@ -99,8 +105,9 @@
     )(ids, cnt, g_col, targets, x_all)
 
 
-def col_call(ids, cnt, f_row, k_all, tiles_own):
-    blocks, slots, width, rows = k_all.shape
+def col_call(ids, cnt, f_rows, k_parts, tiles_own):
+    blocks, slots, width, part_rows = k_parts[0].shape
+    rows = part_rows * len(k_parts)
     acc_spec = pl.BlockSpec((tiles_own, width, 1), lambda s, c, ids_ref, cnt_ref: (0, 0, 0))
     acc_shape = jax.ShapeDtypeStruct((tiles_own, width, 1), jnp.float32)
     cost = pl.CostEstimate(
@@ -108,21 +115,20 @@
         transcendentals=blocks * slots * rows * width,
         bytes_accessed=4 * blocks * slots * rows * width,
     )
+    f_spec = pl.BlockSpec((None, 1, part_rows), lambda s, c, ids_ref, cnt_ref: (s, 0, 0))
+    k_spec = pl.BlockSpec((None, None, width, part_rows), pick_slot)
     return pl.pallas_call(
         col_kernel,
         out_shape=(acc_shape, acc_shape),
         grid_spec=pltpu.PrefetchScalarGridSpec(
             num_scalar_prefetch=2,
             grid=(blocks, slots),
-            in_specs=[
-                pl.BlockSpec((None, 1, rows), lambda s, c, ids_ref, cnt_ref: (s, 0, 0)),
-                pl.BlockSpec((None, None, width, rows), pick_slot),
-            ],
+            in_specs=[f_spec] * len(f_rows) + [k_spec] * len(k_parts),
             out_specs=(acc_spec, acc_spec),
         ),
         compiler_params=pltpu.CompilerParams(dimension_semantics=("arbitrary", "arbitrary")),
         cost_estimate=cost,
-    )(ids, cnt, f_row, k_all)
+    )(ids, cnt, *f_rows, *k_parts)
 
 
 def local(sources, log_a, targets, g_old, log_b, tile_ids, live_count):
@@ -137,20 +143,22 @@
     meta_rows = jnp.zeros((16, depth), jnp.bfloat16).at[0, : meta.shape[0]].set(
         meta.astype(jnp.bfloat16)
     )
-    packed = jnp.concatenate([sources, meta_rows], axis=0)
-    x_all = lax.all_gather(packed, "src")
-    meta_all = x_all[:, rows, : meta.shape[0]].astype(jnp.int32)
-    blocks = x_all.shape[0]
+    half = rows // 2
+    x_first = lax.all_gather(jnp.concatenate([sources[:half], meta_rows], axis=0), "src")
+    x_second = lax.all_gather(sources[half:], "src")
+    meta_all = x_first[:, half, : meta.shape[0]].astype(jnp.int32)
+    blocks = x_first.shape[0]
     ids_all = meta_all[:, : groups * slots_per].reshape(blocks, groups, slots_per)
     cnt_all = meta_all[:, groups * slots_per :]
     my_ids = jnp.clip(lax.dynamic_index_in_dim(ids_all, me, 1, False) - me * tiles_own, 0, tiles_own - 1)
     my_cnt = lax.dynamic_index_in_dim(cnt_all, me, 1, False)
 
     g_col = (g_old.astype(jnp.float32) / EPSILON)[:, :, None]
-    row_top, row_total, k_all = row_call(my_ids, my_cnt, g_col, targets, x_all, rows, scale)
-    stats = jnp.concatenate(
-        [row_top.reshape(blocks, rows), row_total.reshape(blocks, rows), log_a[None]], axis=0
-    )
+    top_a, total_a, k_a = row_call(my_ids, my_cnt, g_col, targets, x_first, half, scale)
+    top_b, total_b, k_b = row_call(my_ids, my_cnt, g_col, targets, x_second, half, scale)
+    row_top = jnp.concatenate([top_a, top_b], axis=2).reshape(blocks, rows)
+    row_total = jnp.concatenate([total_a, total_b], axis=2).reshape(blocks, rows)
+    stats = jnp.concatenate([row_top, row_total, log_a[None]], axis=0)
     stats_all = lax.all_to_all(
         jnp.broadcast_to(stats[None], (blocks,) + stats.shape), "src", 0, 0, tiled=True
     )
@@ -162,7 +170,8 @@
     f_new = lax.dynamic_index_in_dim(f_all, me, 0, False)
 
     f_row = (f_all / EPSILON)[:, None, :]
-    tile_top, tile_total = col_call(my_ids, my_cnt, f_row, k_all, tiles_own)
+    f_rows = (f_row[:, :, :half], f_row[:, :, half:])
+    tile_top, tile_total = col_call(my_ids, my_cnt, f_rows, (k_a, k_b), tiles_own)
     col = jnp.concatenate([tile_top.reshape(tiles_own, width), tile_total.reshape(tiles_own, width)])
     loop_size = lax.axis_size("loop")
     col_all = lax.all_to_all(

time: 219 us -> 226 us (1.032)
  Pallas kernels: 73.8 us -> 100 us
  waiting for transfers between devices: 82.5 us -> 60.1 us
  local copies, waits for them, and re-layouts: 5.38 us -> 8.58 us
    pallas_call x1 -> x2, Pallas kernels: 43.9 us -> 68.8 us  [row_call(): pl.pallas_call(lambda *refs: row_kernel(*refs, scale=scale), out_shape=(s...]
    all_gather x1 -> x2, waiting for transfers between devices: 74.3 us -> 51.3 us  [the longest x1 44 us: local(): lax.all_gather(jnp.concatenate([sources[:half], meta_rows], axis=0), 'src')]
    slice x0 -> x2, local copies, waits for them, and re-layouts: none -> 2.55 us  [the longest x1 1.93 us: local(): x_second = lax.all_gather(sources[half:], 'src')]
  transfers between devices with their start and end apart: 2 -> 3, of which waited for: 2 -> 3; matrix products, arithmetic and copies ran while one was open for 1% -> 2% of each run, Pallas kernels for 0% -> 16%
where the time goes in v5:
time: 226 us; the launch traced here: 223 us
  Pallas kernels  100 us (44%)
  waiting for transfers between devices  60.1 us (27%)
  blocking collectives  23.9 us (11%)
  between operations  14.2 us (6%)
  local copies, waits for them, and re-layouts  8.58 us (4%)
  other arithmetic  8.19 us (4%)
  starting transfers between devices  8.02 us (4%)
    pallas_call x2, Pallas kernels, row_call(): pl.pallas_call(lambda *refs: row_kernel(*refs, scale=scale), out_shape=(s...  68.8 us
    all_gather x1, waiting for transfers between devices, local(): lax.all_gather(jnp.concatenate([sources[:half], meta_rows], axis=0), 'src')  44 us
    pallas_call x1, Pallas kernels, col_call(): pl.pallas_call(col_kernel, out_shape=(acc_shape, acc_shape), grid_spec=pl...  31.4 us
    all_to_all x1, blocking collectives, local(): lax.all_to_all(jnp.broadcast_to(stats[None], (blocks,) + stats.shape), 's...  23.9 us
    all_to_all x1, waiting for transfers between devices, local(): lax.all_to_all(jnp.broadcast_to(col[None], (loop_size,) + col.shape), 'lo...  8.14 us
    all_to_all x1, starting transfers between devices, local(): lax.all_to_all(jnp.broadcast_to(col[None], (loop_size,) + col.shape), 'lo...  7.94 us
    all_gather x1, waiting for transfers between devices, local(): x_second = lax.all_gather(sources[half:], 'src')  7.27 us
  transfers between devices with their start and end apart: 3, of which 3 were waited for; matrix products, arithmetic and copies ran while one was open for 2% of the time, Pallas kernels for 16%

profile of v5, /device:TPU:0, one launch (start us, length us, event | category | flops | bytes accessed | tf_op | source)
XLA Modules:
  0.0 223.2 jit_solution(1585545198771522827)
XLA Ops:
  7.2 0.7 convert.8
  7.9 0.7 convert.9
  8.8 1.9 fusion.10
  10.8 0.8 pad_maximum_fusion
  11.6 0.7 all-gather.7.cloned.1.call-update
  12.4 2.0 copy.41.refs_2_
  14.3 44.0 %all-gather.5.cloned.1.call-done = bf16[4352,768]{1,0:T(8,128)(2,1)} async-done(((bf16[272,768]{1,0:T(8,128)(2,1)}), bf16[4352,768]{1,0:T(8,128)(2,1)}) %all-gather.5.cloned.1.call-update) | async-done | bytes 6684688 | tf_op jit(solution)/shard_map/all_gather | solution.py:147
  58.3 0.8 slice_convert_fusion
  59.2 0.7 copy.40.refs_0_.ids_ref
  59.9 0.7 dynamic-slice_reduce_fusion.refs_1_.cnt_ref
  60.6 34.9 %shard_map.86 = (f32[16,1,256]{2,1,0:T(1,128)}, f32[16,1,256]{2,1,0:T(1,128)}, f32[16,2,512,256]{3,2,1,0:T(8,128)}) custom-call(s32[16,2]{1,0:T(8,128)} %copy.40.refs_0_.ids_ref, s32[16]{0:T(128)} %dynamic-slice_reduce_fusion.refs_1_.cnt_ref, f32[8,512,1]{2,1,0:T(8,128)} %copy.41.refs_2_, bf16[8,512,768]{2,1,0:T(8,128)(2,1)} %refs_3_.3, ...), custom_call_target="tpu_custom_call" | custom-call | flops 6442450944 | bytes 48627712 | tf_op jit(solution)/shard_map/pallas_call | solution.py:86
  95.5 0.7 copy.44
  96.2 7.3 %all-gather.7.cloned.1.call-done = bf16[4096,768]{1,0:T(8,128)(2,1)} async-done(((bf16[256,768]{1,0:T(8,128)(2,1)}), bf16[4096,768]{1,0:T(8,128)(2,1)}) %all-gather.7.cloned.1.call-update) | async-done | bytes 6291472 | tf_op jit(solution)/shard_map/all_gather | solution.py:148
  103.5 34.0 %shard_map.87 = (f32[16,1,256]{2,1,0:T(1,128)}, f32[16,1,256]{2,1,0:T(1,128)}, f32[16,2,512,256]{3,2,1,0:T(8,128)}) custom-call(s32[16,2]{1,0:T(8,128)} %copy.40.refs_0_.ids_ref, s32[16]{0:T(128)} %dynamic-slice_reduce_fusion.refs_1_.cnt_ref, f32[8,512,1]{2,1,0:T(8,128)} %copy.41.refs_2_, bf16[8,512,768]{2,1,0:T(8,128)(2,1)} %refs_3_.3, ...), custom_call_target="tpu_custom_call" | custom-call | flops 6442450944 | bytes 48234496 | tf_op jit(solution)/shard_map/pallas_call | solution.py:86
  137.4 0.7 copy.45
  138.2 0.7 pad_maximum_fusion.2
  139.1 23.9 %all_to_all.10 = f32[16,33,512]{2,1,0:T(8,128)S(1)} all-to-all(f32[16,33,512]{2,1,0:T(8,128)S(1)} %broadcast_in_dim.10), channel_id=1, replica_groups=mesh['src'=16,'loop'=8] {'src'}, dimensions={0} | all-to-all | bytes 2162688 | tf_op jit(solution)/shard_map/all_to_all | solution.py:162
  163.3 0.6 fusion.11
  163.9 31.4 %shard_map.88 = (f32[8,512,1]{2,1,0:T(8,128)}, f32[8,512,1]{2,1,0:T(8,128)}) custom-call(s32[16,2]{1,0:T(8,128)} %copy.40.refs_0_.ids_ref, s32[16]{0:T(128)} %dynamic-slice_reduce_fusion.refs_1_.cnt_ref, f32[16,1,256]{2,1,0:T(1,128)} %get-tuple-element.33.refs_0_, f32[16,1,256]{2,1,0:T(1,128)} %get-tuple-element.32.refs_1_, ...), custom_call_target="tpu_custom_call" | custom-call | flops 33554432 | bytes 33554432 | tf_op jit(solution)/shard_map/pallas_call | solution.py:120
  195.3 2.3 %reduce.3 = f32[8,512]{1,0:T(8,128)S(1)} reduce(f32[8,512,1]{2,1,0:T(8,128)} %get-tuple-element.28, f32[]{:T(128)} %constant.70), dimensions={2}, to_apply=%get-tuple-element.28.reduce_sub_computation | reduce | bytes 32772 | tf_op jit(solution)/shard_map/pallas_call | solution.py:120
  198.3 0.7 broadcast_in_dim.11
  199.0 7.9 %all-to-all-start.1 = ((f32[8,16,512]{2,1,0:T(8,128)}), f32[8,16,512]{2,1,0:T(8,128)S(1)}, u32[]{:S(2)}, u32[]{:S(2)}) async-start(f32[8,16,512]{2,1,0:T(8,128)} %broadcast_in_dim.11), calls=%async_computation.1 | async-start | bytes 524288 | tf_op jit(solution)/shard_map/all_to_all | solution.py:177
  207.6 8.1 %all-to-all-done.1 = f32[8,16,512]{2,1,0:T(8,128)S(1)} async-done(((f32[8,16,512]{2,1,0:T(8,128)}), f32[8,16,512]{2,1,0:T(8,128)S(1)}, u32[]{:S(2)}, u32[]{:S(2)}) %all-to-all-start.1) | async-done | bytes 262176 | tf_op jit(solution)/shard_map/all_to_all | solution.py:177
  215.8 0.6 multiply_subtract_fusion
  (34 shorter events, 2.2 us)
Async XLA Ops:
  7.2 5.2 %copy-start.3 = (bf16[8,512]{1,0:T(8,128)(2,1)S(1)}, bf16[8,512]{1,0:T(8,128)(2,1)}, u32[]{:S(2)}) copy-start(bf16[8,512]{1,0:T(8,128)(2,1)} %param.12) | copy-start | bytes 24580
  7.2 51.1 %all-gather.5.cloned.1.call-start = ((), (), s32[]{:S(2)}) async-start(), calls=%async_computation.2 | async-start | bytes 7102464 | tf_op jit(solution)/shard_map/all_gather | solution.py:147
  11.6 91.9 %all-gather.7.cloned.1.call-start = ((), (), s32[]{:S(2)}) async-start(), calls=%async_computation.3 | async-start | bytes 6684672 | tf_op jit(solution)/shard_map/all_gather | solution.py:148
  103.5 34.7 %copy-start.2 = (f32[16,1,256]{2,1,0:T(1,128)S(1)}, f32[16,1,256]{2,1,0:T(1,128)}, u32[]{:S(2)}) copy-start(f32[16,1,256]{2,1,0:T(1,128)} %get-tuple-element.24) | copy-start | bytes 49156
  103.5 35.4 %copy-start.4 = (f32[512]{0:T(512)S(1)}, f32[512]{0:T(512)}, u32[]{:S(2)}) copy-start(f32[512]{0:T(512)} %param.10) | copy-start | bytes 6148
  195.3 2.4 %copy-start = (f32[8,512,1]{2,1,0:T(8,128)S(1)}, f32[8,512,1]{2,1,0:T(8,128)}, u32[]{:S(2)}) copy-start(f32[8,512,1]{2,1,0:T(8,128)} %get-tuple-element.29) | copy-start | bytes 49156
  197.7 18.1 %copy-start.1 = (f32[8,512]{1,0:T(8,128)S(1)}, f32[8,512]{1,0:T(8,128)}, u32[]{:S(2)}) copy-start(f32[8,512]{1,0:T(8,128)} %param.13) | copy-start | bytes 49156
  199.0 16.7 %all-to-all-start.1 = ((f32[8,16,512]{2,1,0:T(8,128)}), f32[8,16,512]{2,1,0:T(8,128)S(1)}, u32[]{:S(2)}, u32[]{:S(2)}) async-start(f32[8,16,512]{2,1,0:T(8,128)} %broadcast_in_dim.11), calls=%async_computation.1 | async-start | bytes 524288 | tf_op jit(solution)/shard_map/all_to_all | solution.py:177
Sparse Core Ops, SparseCore 0:
  11.7 46.5 all-gather.4
  60.0 43.4 all-gather.6

commit v6 on v2

v6 whole, which is shorter than its diff:
```python
import math

import jax
import jax.numpy as jnp
from jax import lax
from jax.experimental import pallas as pl
from jax.experimental.pallas import tpu as pltpu
from jax.sharding import PartitionSpec as P

EPSILON = 0.1
VERY_LOW = -1e30
NT_DIMS = (((1,), (1,)), ((), ()))


def load_all(t_hbm, x_hbm, t_vmem, x_vmem, t_sem, x_sem, window):
    tiles, blocks = t_vmem.shape[0], x_vmem.shape[0]
    rows = x_vmem.shape[1]

    def x_copy(s):
        return pltpu.make_async_copy(x_hbm.at[s, pl.ds(0, rows)], x_vmem.at[s], x_sem.at[s])

    def t_copy(t):
        return pltpu.make_async_copy(t_hbm.at[t], t_vmem.at[t], t_sem.at[t])

    for t in range(tiles):
        t_copy(t).start()
    for s in range(min(window, blocks)):
        x_copy(s).start()
    for t in range(tiles):
        t_copy(t).wait()

    def arrive(s):
        x_copy(s).wait()

        @pl.when(s + window < blocks)
        def _():
            x_copy(jnp.minimum(s + window, blocks - 1)).start()

    return arrive


def row_kernel(ids_ref, cnt_ref, g_ref, t_hbm, x_hbm, top_ref, tot_ref, t_vmem, x_vmem, t_sem, x_sem, *, scale, slots, window):
    arrive = load_all(t_hbm, x_hbm, t_vmem, x_vmem, t_sem, x_sem, window)

    def step(s, carry):
        arrive(s)
        top_ref[s] = jnp.full(top_ref.shape[1:], VERY_LOW, jnp.float32)
        tot_ref[s] = jnp.zeros(tot_ref.shape[1:], jnp.float32)
        for c in range(slots):

            @pl.when(c < cnt_ref[s])
            def _():
                t = ids_ref[s * slots + c]
                kt = lax.dot_general(t_vmem[t], x_vmem[s], NT_DIMS, preferred_element_type=jnp.float32)
                logits = g_ref[t] + kt * scale
                old = top_ref[s]
                new = jnp.maximum(old, jnp.max(logits, axis=0, keepdims=True))
                tot_ref[s] = tot_ref[s] * jnp.exp(old - new) + jnp.sum(
                    jnp.exp(logits - new), axis=0, keepdims=True
                )
                top_ref[s] = new

        return carry

    lax.fori_loop(0, x_vmem.shape[0], step, 0)


def col_kernel(ids_ref, cnt_ref, f_ref, t_hbm, x_hbm, top_ref, tot_ref, t_vmem, x_vmem, t_sem, x_sem, *, scale, slots, window):
    arrive = load_all(t_hbm, x_hbm, t_vmem, x_vmem, t_sem, x_sem, window)
    top_ref[...] = jnp.full(top_ref.shape, VERY_LOW, jnp.float32)
    tot_ref[...] = jnp.zeros(tot_ref.shape, jnp.float32)

    def step(s, carry):
        arrive(s)
        for c in range(slots):

            @pl.when(c < cnt_ref[s])
            def _():
                t = ids_ref[s * slots + c]
                kt = lax.dot_general(t_vmem[t], x_vmem[s], NT_DIMS, preferred_element_type=jnp.float32)
                logits = kt * scale + f_ref[s]
                old = top_ref[t]
                new = jnp.maximum(old, jnp.max(logits, axis=1, keepdims=True))
                tot_ref[t] = tot_ref[t] * jnp.exp(old - new) + jnp.sum(
                    jnp.exp(logits - new), axis=1, keepdims=True
                )
                top_ref[t] = new

        return carry

    lax.fori_loop(0, x_vmem.shape[0], step, 0)


def resident_call(body, ids, cnt, side, targets, x_all, rows, out_shape, scale):
    tiles, width, depth = targets.shape
    blocks = x_all.shape[0]
    slots = ids.shape[1]
    smem = pl.BlockSpec(memory_space=pltpu.SMEM)
    vmem = pl.BlockSpec(memory_space=pltpu.VMEM)
    hbm = pl.BlockSpec(memory_space=pl.ANY)
    cost = pl.CostEstimate(
        flops=2 * blocks * slots * rows * width * depth,
        transcendentals=blocks * slots * rows * width,
        bytes_accessed=2 * (targets.size + blocks * rows * depth),
    )
    kernel = lambda *refs: body(*refs, scale=scale, slots=slots, window=4)
    return pl.pallas_call(
        kernel,
        out_shape=(out_shape, out_shape),
        in_specs=[smem, smem, vmem, hbm, hbm],
        out_specs=(vmem, vmem),
        scratch_shapes=[
            pltpu.VMEM((tiles, width, depth), targets.dtype),
            pltpu.VMEM((blocks, rows, depth), x_all.dtype),
            pltpu.SemaphoreType.DMA((tiles,)),
            pltpu.SemaphoreType.DMA((blocks,)),
        ],
        compiler_params=pltpu.CompilerParams(vmem_limit_bytes=56 * 1024 * 1024),
        cost_estimate=cost,
    )(ids.reshape(-1), cnt, side, targets, x_all)


def local(sources, log_a, targets, g_old, log_b, tile_ids, live_count):
    tiles_own, width, depth = targets.shape
    rows = sources.shape[0]
    slots_per = tile_ids.shape[2]
    groups = tile_ids.shape[1]
    me = lax.axis_index("src")
    scale = 1.0 / (math.sqrt(depth) * EPSILON)

    meta = jnp.concatenate([tile_ids[0].reshape(-1), live_count[0].reshape(-1)])
    meta_rows = jnp.zeros((16, depth), jnp.bfloat16).at[0, : meta.shape[0]].set(
        meta.astype(jnp.bfloat16)
    )
    packed = jnp.concatenate([sources, meta_rows], axis=0)
    x_all = lax.all_gather(packed, "src")
    meta_all = x_all[:, rows, : meta.shape[0]].astype(jnp.int32)
    blocks = x_all.shape[0]
    ids_all = meta_all[:, : groups * slots_per].reshape(blocks, groups, slots_per)
    cnt_all = meta_all[:, groups * slots_per :]
    my_ids = jnp.clip(lax.dynamic_index_in_dim(ids_all, me, 1, False) - me * tiles_own, 0, tiles_own - 1)
    my_cnt = lax.dynamic_index_in_dim(cnt_all, me, 1, False)

    g_col = (g_old.astype(jnp.float32) / EPSILON)[:, :, None]
    row_top, row_total = resident_call(
        row_kernel, my_ids, my_cnt, g_col, targets, x_all, rows,
        jax.ShapeDtypeStruct((blocks, 1, rows), jnp.float32), scale,
    )
    stats = jnp.concatenate(
        [row_top.reshape(blocks, rows), row_total.reshape(blocks, rows), log_a[None]], axis=0
    )
    stats_all = lax.all_to_all(
        jnp.broadcast_to(stats[None], (blocks,) + stats.shape), "src", 0, 0, tiled=True
    )
    tops = stats_all[:, :blocks]
    top = jnp.max(tops, axis=0)
    total = jnp.sum(stats_all[:, blocks : 2 * blocks] * jnp.exp(tops - top[None]), axis=0)
    log_a_all = stats_all[:, 2 * blocks]
    f_all = EPSILON * log_a_all - EPSILON * (top + jnp.log(total))
    f_new = lax.dynamic_index_in_dim(f_all, me, 0, False)

    f_row = (f_all / EPSILON)[:, None, :]
    tile_top, tile_total = resident_call(
        col_kernel, my_ids, my_cnt, f_row, targets, x_all, rows,
        jax.ShapeDtypeStruct((tiles_own, width, 1), jnp.float32), scale,
    )
    col = jnp.concatenate([tile_top.reshape(tiles_own, width), tile_total.reshape(tiles_own, width)])
    loop_size = lax.axis_size("loop")
    col_all = lax.all_to_all(
        jnp.broadcast_to(col[None], (loop_size,) + col.shape), "loop", 0, 0, tiled=True
    )
    tops = col_all[:, :tiles_own]
    all_top = jnp.max(tops, axis=0)
    all_total = jnp.sum(col_all[:, tiles_own:] * jnp.exp(tops - all_top[None]), axis=0)
    g_new = EPSILON * log_b - EPSILON * (all_top + jnp.log(all_total))
    return (f_new, g_new)


def solution(mesh):
    return jax.shard_map(
        local,
        mesh=mesh,
        in_specs=(
            P(("src", "loop"), None),
            P(("src", "loop")),
            P("src", None, None),
            P("src", None),
            P("src", None),
            P(("src", "loop"), None, None),
            P(("src", "loop"), None),
        ),
        out_specs=(P(("src", "loop")), P("src", None)),
        check_vma=False,
    )
```

time: 258 us -> 220 us (0.85)
  waiting for transfers between devices: 108 us -> 82.9 us
  blocking collectives: 34.4 us -> 21.9 us
  other arithmetic: 13.8 us -> 9.33 us
  local copies, waits for them, and re-layouts: 9.53 us -> 5.39 us
  starting transfers between devices: 0.08 us -> 3.45 us
  Pallas kernels: 75.8 us -> 78.6 us
    all_gather x1 -> x0, waiting for transfers between devices: 34.6 us -> none  [local(): stats_all = lax.all_gather(stats, 'src')]
    all_gather x1 -> x0, blocking collectives: 34.4 us -> none  [local(): col_all = lax.all_gather(col, 'loop')]
    all_to_all x0 -> x1, blocking collectives: none -> 21.9 us  [local(): lax.all_to_all(jnp.broadcast_to(stats[None], (blocks,) + stats.shape), 's...]
    all_to_all x0 -> x1, waiting for transfers between devices: none -> 8.57 us  [local(): lax.all_to_all(jnp.broadcast_to(col[None], (loop_size,) + col.shape), 'lo...]
    div x1, other arithmetic: 4.52 us -> 0.65 us  [local(): f_row = (f_all / EPSILON)[:, None, :]]
    all_to_all x0 -> x1, starting transfers between devices: none -> 3.41 us  [local(): lax.all_to_all(jnp.broadcast_to(col[None], (loop_size,) + col.shape), 'lo...]
    pallas_call x0 -> x2, other arithmetic: none -> 2.96 us  [resident_call(): pl.pallas_call(kernel, out_shape=(out_shape, out_shape), in_specs=[smem,...]
    pallas_call x2, Pallas kernels: 75.8 us -> 78.6 us  [resident_call(): pl.pallas_call(kernel, out_shape=(out_shape, out_shape), in_specs=[smem,...]
where the time goes in v6:
time: 220 us; the launch traced here: 216 us
  waiting for transfers between devices  82.9 us (38%)
  Pallas kernels  78.6 us (36%)
  blocking collectives  21.9 us (10%)
  between operations  14.2 us (6%)
  other arithmetic  9.33 us (4%)
  local copies, waits for them, and re-layouts  5.39 us (2%)
  starting transfers between devices  3.45 us (2%)
    pallas_call x2, Pallas kernels, resident_call(): pl.pallas_call(kernel, out_shape=(out_shape, out_shape), in_specs=[smem,...  78.6 us
    all_gather x1, waiting for transfers between devices, local(): x_all = lax.all_gather(packed, 'src')  74.3 us
    all_to_all x1, blocking collectives, local(): lax.all_to_all(jnp.broadcast_to(stats[None], (blocks,) + stats.shape), 's...  21.9 us
    all_to_all x1, waiting for transfers between devices, local(): lax.all_to_all(jnp.broadcast_to(col[None], (loop_size,) + col.shape), 'lo...  8.57 us
  transfers between devices with their start and end apart: 2, of which 2 were waited for; matrix products, arithmetic and copies ran while one was open for 1% of the time, Pallas kernels for 0%

profile of v6, /device:TPU:0, one launch (start us, length us, event | category | flops | bytes accessed | tf_op | source)
XLA Modules:
  0.0 215.7 jit_solution(2345404709511419634)
XLA Ops:
  7.2 0.7 convert.9
  7.9 0.7 convert.8
  8.6 0.1 copy.23
  8.7 0.1 concatenate.22
  8.8 2.1 pad_maximum_fusion
  11.0 2.0 copy.26.refs_2_
  13.0 74.3 %all-gather.3.cloned.1.call-done = bf16[8448,768]{1,0:T(8,128)(2,1)} async-done(((bf16[528,768]{1,0:T(8,128)(2,1)}), bf16[8448,768]{1,0:T(8,128)(2,1)}) %all-gather.3.cloned.1.call-update) | async-done | bytes 12976144 | tf_op jit(solution)/shard_map/all_gather | solution.py:136
  87.3 0.8 slice_convert_fusion
  88.3 0.6 min.12.refs_0_
  88.9 0.7 dynamic-slice_reduce_fusion.refs_1_
  89.6 28.9 %shard_map.86 = (f32[16,1,512]{2,1,0:T(1,128)}, f32[16,1,512]{2,1,0:T(1,128)}) custom-call(s32[32]{0:T(128)} %min.12.refs_0_, s32[16]{0:T(128)} %dynamic-slice_reduce_fusion.refs_1_, f32[8,512,1]{2,1,0:T(8,128)} %copy.26.refs_2_, bf16[8,512,768]{2,1,0:T(8,128)(2,1)} %refs_3_.3, bf16[16,528,768]{2,1,0:T(8,128)(2,1)} %bitcast.22), custom_call_target="tpu_custom_call" | custom-call | flops 12884901888 | bytes 18874368 | tf_op jit(solution)/shard_map/pallas_call | solution.py:107
  118.5 0.8 copy_bitcast_fusion
  119.3 0.1 broadcast_in_dim.10
  119.5 21.9 %all_to_all.10 = f32[16,33,512]{2,1,0:T(8,128)S(1)} all-to-all(f32[16,33,512]{2,1,0:T(8,128)S(1)} %broadcast_in_dim.10), channel_id=1, replica_groups=mesh['src'=16,'loop'=8] {'src'}, dimensions={0} | all-to-all | bytes 2162688 | tf_op jit(solution)/shard_map/all_to_all | solution.py:152
  141.4 0.1 fusion
  141.6 0.6 fusion.7.refs_2_
  142.2 49.7 %shard_map.87 = (f32[8,512,1]{2,1,0:T(8,128)}, f32[8,512,1]{2,1,0:T(8,128)}) custom-call(s32[32]{0:T(128)} %min.12.refs_0_, s32[16]{0:T(128)} %dynamic-slice_reduce_fusion.refs_1_, f32[16,1,512]{2,1,0:T(1,128)} %fusion.7.refs_2_, bf16[8,512,768]{2,1,0:T(8,128)(2,1)} %refs_3_.3, bf16[16,528,768]{2,1,0:T(8,128)(2,1)} %bitcast.23), custom_call_target="tpu_custom_call" | custom-call | flops 12884901888 | bytes 18874368 | tf_op jit(solution)/shard_map/pallas_call | solution.py:107
  191.9 2.3 %reduce.4 = f32[8,512]{1,0:T(8,128)S(1)} reduce(f32[8,512,1]{2,1,0:T(8,128)} %get-tuple-element.21, f32[]{:T(128)} %constant.70), dimensions={2}, to_apply=%get-tuple-element.21.reduce_sub_computation | reduce | bytes 32772 | tf_op jit(solution)/shard_map/pallas_call | solution.py:107
  194.3 0.6 reduce.3
  194.9 0.7 broadcast_in_dim.11
  195.6 3.4 %all-to-all-start.1 = ((f32[8,16,512]{2,1,0:T(8,128)}), f32[8,16,512]{2,1,0:T(8,128)S(1)}, u32[]{:S(2)}, u32[]{:S(2)}) async-start(f32[8,16,512]{2,1,0:T(8,128)} %broadcast_in_dim.11), calls=%async_computation.1 | async-start | bytes 524288 | tf_op jit(solution)/shard_map/all_to_all | solution.py:169
  199.0 0.6 dynamic-slice_subtract_fusion
  199.6 8.6 %all-to-all-done.1 = f32[8,16,512]{2,1,0:T(8,128)S(1)} async-done(((f32[8,16,512]{2,1,0:T(8,128)}), f32[8,16,512]{2,1,0:T(8,128)S(1)}, u32[]{:S(2)}, u32[]{:S(2)}) %all-to-all-start.1) | async-done | bytes 262176 | tf_op jit(solution)/shard_map/all_to_all | solution.py:169
  208.3 0.6 multiply_subtract_fusion
  (24 shorter events, 0.5 us)
Async XLA Ops:
  7.2 3.8 %copy-start.2 = (bf16[8,512]{1,0:T(8,128)(2,1)S(1)}, bf16[8,512]{1,0:T(8,128)(2,1)}, u32[]{:S(2)}) copy-start(bf16[8,512]{1,0:T(8,128)(2,1)} %param.12) | copy-start | bytes 24580
  7.2 80.1 %all-gather.3.cloned.1.call-start = ((), (), s32[]{:S(2)}) async-start(), calls=%async_computation.2 | async-start | bytes 13787136 | tf_op jit(solution)/shard_map/all_gather | solution.py:136
  89.6 29.7 %copy-start.3 = (f32[512]{0:T(512)S(1)}, f32[512]{0:T(512)}, u32[]{:S(2)}) copy-start(f32[512]{0:T(512)} %param.10) | copy-start | bytes 6148
  191.9 2.4 %copy-start = (f32[8,512,1]{2,1,0:T(8,128)S(1)}, f32[8,512,1]{2,1,0:T(8,128)}, u32[]{:S(2)}) copy-start(f32[8,512,1]{2,1,0:T(8,128)} %get-tuple-element.20) | copy-start | bytes 49156
  194.3 14.0 %copy-start.1 = (f32[8,512]{1,0:T(8,128)S(1)}, f32[8,512]{1,0:T(8,128)}, u32[]{:S(2)}) copy-start(f32[8,512]{1,0:T(8,128)} %param.13) | copy-start | bytes 49156
  195.6 12.6 %all-to-all-start.1 = ((f32[8,16,512]{2,1,0:T(8,128)}), f32[8,16,512]{2,1,0:T(8,128)S(1)}, u32[]{:S(2)}, u32[]{:S(2)}) async-start(f32[8,16,512]{2,1,0:T(8,128)} %broadcast_in_dim.11), calls=%async_computation.1 | async-start | bytes 524288 | tf_op jit(solution)/shard_map/all_to_all | solution.py:169
Sparse Core Ops, SparseCore 0:
  11.1 76.1 all-gather.2

commit v7 on v6

--- a/solution.py
+++ b/solution.py
@@ -77,12 +77,12 @@
             @pl.when(c < cnt_ref[s])
             def _():
                 t = ids_ref[s * slots + c]
-                kt = lax.dot_general(t_vmem[t], x_vmem[s], NT_DIMS, preferred_element_type=jnp.float32)
-                logits = kt * scale + f_ref[s]
+                k = lax.dot_general(x_vmem[s], t_vmem[t], NT_DIMS, preferred_element_type=jnp.float32)
+                logits = f_ref[s] + k * scale
                 old = top_ref[t]
-                new = jnp.maximum(old, jnp.max(logits, axis=1, keepdims=True))
+                new = jnp.maximum(old, jnp.max(logits, axis=0, keepdims=True))
                 tot_ref[t] = tot_ref[t] * jnp.exp(old - new) + jnp.sum(
-                    jnp.exp(logits - new), axis=1, keepdims=True
+                    jnp.exp(logits - new), axis=0, keepdims=True
                 )
                 top_ref[t] = new
 
@@ -159,10 +159,10 @@
     f_all = EPSILON * log_a_all - EPSILON * (top + jnp.log(total))
     f_new = lax.dynamic_index_in_dim(f_all, me, 0, False)
 
-    f_row = (f_all / EPSILON)[:, None, :]
+    f_col = (f_all / EPSILON)[:, :, None]
     tile_top, tile_total = resident_call(
-        col_kernel, my_ids, my_cnt, f_row, targets, x_all, rows,
-        jax.ShapeDtypeStruct((tiles_own, width, 1), jnp.float32), scale,
+        col_kernel, my_ids, my_cnt, f_col, targets, x_all, rows,
+        jax.ShapeDtypeStruct((tiles_own, 1, width), jnp.float32), scale,
     )
     col = jnp.concatenate([tile_top.reshape(tiles_own, width), tile_total.reshape(tiles_own, width)])
     loop_size = lax.axis_size("loop")

time: 220 us -> 204 us (0.927); the launches traced: 216 us -> 204 us
  Pallas kernels: 78.6 us -> 57.1 us
  local copies, waits for them, and re-layouts: 5.39 us -> 9.5 us
  blocking collectives: 21.9 us -> 25.5 us
    pallas_call x2, Pallas kernels: 78.6 us -> 57.1 us  [resident_call(): pl.pallas_call(kernel, out_shape=(out_shape, out_shape), in_specs=[smem,...]
    div x1, other arithmetic: 0.65 us -> 4.52 us  [local(): f_col = (f_all / EPSILON)[:, :, None]]
    all_to_all x1, blocking collectives: 21.9 us -> 25.5 us  [local(): lax.all_to_all(jnp.broadcast_to(stats[None], (blocks,) + stats.shape), 's...]
    pallas_call x2 -> x0, other arithmetic: 2.96 us -> none  [resident_call(): pl.pallas_call(kernel, out_shape=(out_shape, out_shape), in_specs=[smem,...]
    sub x0 -> x1, local copies, waits for them, and re-layouts: none -> 2.65 us  [local(): f_all = EPSILON * log_a_all - EPSILON * (top + jnp.log(total))]
  transfers between devices with their start and end apart: 2 -> 2, of which waited for: 2 -> 2; matrix products, arithmetic and copies ran while one was open for 1% -> 2% of each run, Pallas kernels for 0% -> 0%
where the time goes in v7:
time: 204 us
  waiting for transfers between devices  81.8 us (40%)
  Pallas kernels  57.1 us (28%)
  blocking collectives  25.5 us (12%)
  between operations  14.1 us (7%)
  other arithmetic  11 us (5%)
  local copies, waits for them, and re-layouts  9.5 us (5%)
  starting transfers between devices  5.04 us (2%)
    all_gather x1, waiting for transfers between devices, local(): x_all = lax.all_gather(packed, 'src')  73.7 us
    pallas_call x2, Pallas kernels, resident_call(): pl.pallas_call(kernel, out_shape=(out_shape, out_shape), in_specs=[smem,...  57.1 us
    all_to_all x1, blocking collectives, local(): lax.all_to_all(jnp.broadcast_to(stats[None], (blocks,) + stats.shape), 's...  25.5 us
    all_to_all x1, waiting for transfers between devices, local(): lax.all_to_all(jnp.broadcast_to(col[None], (loop_size,) + col.shape), 'lo...  8.13 us
    all_to_all x1, starting transfers between devices, local(): lax.all_to_all(jnp.broadcast_to(col[None], (loop_size,) + col.shape), 'lo...  5 us
    div x1, other arithmetic, local(): f_col = (f_all / EPSILON)[:, :, None]  4.52 us
  transfers between devices with their start and end apart: 2, of which 2 were waited for; matrix products, arithmetic and copies ran while one was open for 2% of the time, Pallas kernels for 0%

profile of v7, /device:TPU:0, one launch (start us, length us, event | category | flops | bytes accessed | tf_op | source)
XLA Modules:
  0.0 203.9 jit_solution(3274170217705061142)
XLA Ops:
  7.2 0.7 convert.8
  7.9 0.7 convert.9
  8.8 2.1 %pad_maximum_fusion = bf16[528,768]{1,0:T(8,128)(2,1)} fusion(bf16[16,768]{1,0:T(8,128)(2,1)S(1)} %fusion.8, bf16[512,768]{1,0:T(8,128)(2,1)} %param.9), kind=kLoop, calls=%fused_computation.1 | loop fusion | flops 1622016 | bytes 1622016 | tf_op jit(solution)/shard_map/concatenate | solution.py:135
  10.9 0.7 multiply_bitcast_fusion
  11.7 2.0 copy.40.refs_2_
  13.6 73.7 %all-gather.3.cloned.1.call-done = bf16[8448,768]{1,0:T(8,128)(2,1)} async-done(((bf16[528,768]{1,0:T(8,128)(2,1)}), bf16[8448,768]{1,0:T(8,128)(2,1)}) %all-gather.3.cloned.1.call-update) | async-done | bytes 12976144 | tf_op jit(solution)/shard_map/all_gather | solution.py:136
  87.3 0.8 slice_convert_fusion
  88.2 0.7 dynamic-slice_reduce_fusion.refs_1_
  89.0 0.6 min.12.refs_0_
  89.6 28.1 %shard_map.86 = (f32[16,1,512]{2,1,0:T(1,128)}, f32[16,1,512]{2,1,0:T(1,128)}) custom-call(s32[32]{0:T(128)} %min.12.refs_0_, s32[16]{0:T(128)} %dynamic-slice_reduce_fusion.refs_1_, f32[8,512,1]{2,1,0:T(8,128)} %copy.40.refs_2_, bf16[8,512,768]{2,1,0:T(8,128)(2,1)} %refs_3_.3, bf16[16,528,768]{2,1,0:T(8,128)(2,1)} %bitcast.34), custom_call_target="tpu_custom_call" | custom-call | flops 12884901888 | bytes 18874368 | tf_op jit(solution)/shard_map/pallas_call | solution.py:107
  117.8 0.8 copy_bitcast_fusion
  118.6 0.1 broadcast_in_dim.10
  118.7 25.5 %all_to_all.10 = f32[16,33,512]{2,1,0:T(8,128)S(1)} all-to-all(f32[16,33,512]{2,1,0:T(8,128)S(1)} %broadcast_in_dim.10), channel_id=1, replica_groups=mesh['src'=16,'loop'=8] {'src'}, dimensions={0} | all-to-all | bytes 2162688 | tf_op jit(solution)/shard_map/all_to_all | solution.py:152
  144.3 0.1 fusion
  144.4 2.6 %copy.42 = f32[16,512,1]{2,1,0:T(8,128)} copy(f32[16,512,1]{1,0,2:T(8,128)S(1)} %get-tuple-element.22) | data formatting | bytes 65536 | tf_op jit(solution)/shard_map/sub | solution.py:159
  147.1 4.5 %broadcast_multiply_fusion.refs_2_ = f32[16,512,1]{2,1,0:T(8,128)} fusion(f32[16,512,1]{2,1,0:T(8,128)} %copy.42), kind=kLoop, calls=%fused_computation | loop fusion | flops 8192 | bytes 65536 | tf_op jit(solution)/shard_map/div | solution.py:162
  151.6 28.9 %shard_map.87 = (f32[8,1,512]{2,1,0:T(1,128)}, f32[8,1,512]{2,1,0:T(1,128)}) custom-call(s32[32]{0:T(128)} %min.12.refs_0_, s32[16]{0:T(128)} %dynamic-slice_reduce_fusion.refs_1_, f32[16,512,1]{2,1,0:T(8,128)} %broadcast_multiply_fusion.refs_2_, bf16[8,512,768]{2,1,0:T(8,128)(2,1)} %refs_3_.3, bf16[16,528,768]{2,1,0:T(8,128)(2,1)} %bitcast.35), custom_call_target="tpu_custom_call" | custom-call | flops 12884901888 | bytes 18874368 | tf_op jit(solution)/shard_map/pallas_call | solution.py:107
  180.5 0.7 copy.58
  181.2 0.7 copy.57
  182.0 0.7 broadcast_in_dim.11
  182.7 5.0 %all-to-all-start.1 = ((f32[8,16,512]{2,1,0:T(8,128)}), f32[8,16,512]{2,1,0:T(8,128)S(1)}, u32[]{:S(2)}, u32[]{:S(2)}) async-start(f32[8,16,512]{2,1,0:T(8,128)} %broadcast_in_dim.11), calls=%async_computation.1 | async-start | bytes 524288 | tf_op jit(solution)/shard_map/all_to_all | solution.py:169
  187.7 0.6 dynamic-slice_subtract_fusion
  188.3 8.1 %all-to-all-done.1 = f32[8,16,512]{2,1,0:T(8,128)S(1)} async-done(((f32[8,16,512]{2,1,0:T(8,128)}), f32[8,16,512]{2,1,0:T(8,128)S(1)}, u32[]{:S(2)}, u32[]{:S(2)}) %all-to-all-start.1) | async-done | bytes 262176 | tf_op jit(solution)/shard_map/all_to_all | solution.py:169
  196.5 0.6 multiply_subtract_fusion
  (21 shorter events, 0.7 us)
Async XLA Ops:
  7.2 80.1 %all-gather.3.cloned.1.call-start = ((), (), s32[]{:S(2)}) async-start(), calls=%async_computation.2 | async-start | bytes 13787136 | tf_op jit(solution)/shard_map/all_gather | solution.py:136
  89.6 28.9 %copy-start.1 = (f32[512]{0:T(512)S(1)}, f32[512]{0:T(512)}, u32[]{:S(2)}) copy-start(f32[512]{0:T(512)} %param.10) | copy-start | bytes 6148
  151.6 44.9 %copy-start = (f32[8,512]{1,0:T(8,128)S(1)}, f32[8,512]{1,0:T(8,128)}, u32[]{:S(2)}) copy-start(f32[8,512]{1,0:T(8,128)} %param.13) | copy-start | bytes 49156
  182.7 13.7 %all-to-all-start.1 = ((f32[8,16,512]{2,1,0:T(8,128)}), f32[8,16,512]{2,1,0:T(8,128)S(1)}, u32[]{:S(2)}, u32[]{:S(2)}) async-start(f32[8,16,512]{2,1,0:T(8,128)} %broadcast_in_dim.11), calls=%async_computation.1 | async-start | bytes 524288 | tf_op jit(solution)/shard_map/all_to_all | solution.py:169
Sparse Core Ops, SparseCore 0:
  11.1 76.1 all-gather.2

commit v8 on v7

v8 whole, which is shorter than its diff:
```python
import math

import jax
import jax.numpy as jnp
from jax import lax
from jax.experimental import pallas as pl
from jax.experimental.pallas import tpu as pltpu
from jax.sharding import Mesh, PartitionSpec as P


EPSILON = 0.1
VERY_LOW = -1e30
NT_DIMS = (((1,), (1,)), ((), ()))


def load_all(t_hbm, x_parts, t_vmem, x_vmem, t_sem, x_sem, window):
    tiles = t_vmem.shape[0]
    rows = x_vmem.shape[1]
    per = x_parts[0].shape[0]

    def x_copy(q, j):
        return pltpu.make_async_copy(
            x_parts[q].at[j, pl.ds(0, rows)], x_vmem.at[q * per + j], x_sem.at[q * per + j]
        )

    def t_copy(t):
        return pltpu.make_async_copy(t_hbm.at[t], t_vmem.at[t], t_sem.at[t])

    for t in range(tiles):
        t_copy(t).start()
    for q in range(len(x_parts)):
        for j in range(min(window, per)):
            x_copy(q, j).start()
    for t in range(tiles):
        t_copy(t).wait()

    def arrive(q, j):
        x_copy(q, j).wait()

        @pl.when(j + window < per)
        def _():
            x_copy(q, jnp.minimum(j + window, per - 1)).start()

    return arrive, per


def row_kernel(ids_ref, cnt_ref, g_ref, t_hbm, *refs, scale, slots, window, parts):
    x_parts = refs[:parts]
    top_ref, tot_ref, t_vmem, x_vmem, t_sem, x_sem = refs[parts:]
    arrive, per = load_all(t_hbm, x_parts, t_vmem, x_vmem, t_sem, x_sem, window)

    def step(q, j):
        arrive(q, j)
        s = q * per + j
        top_ref[s] = jnp.full(top_ref.shape[1:], VERY_LOW, jnp.float32)
        tot_ref[s] = jnp.zeros(tot_ref.shape[1:], jnp.float32)
        for c in range(slots):

            @pl.when(c < cnt_ref[s])
            def _():
                t = ids_ref[s * slots + c]
                kt = lax.dot_general(t_vmem[t], x_vmem[s], NT_DIMS, preferred_element_type=jnp.float32)
                logits = g_ref[t] + kt * scale
                old = top_ref[s]
                new = jnp.maximum(old, jnp.max(logits, axis=0, keepdims=True))
                tot_ref[s] = tot_ref[s] * jnp.exp(old - new) + jnp.sum(
                    jnp.exp(logits - new), axis=0, keepdims=True
                )
                top_ref[s] = new

    for q in range(parts):
        lax.fori_loop(0, per, lambda j, carry, q=q: (step(q, j), carry)[1], 0)


def col_kernel(ids_ref, cnt_ref, f_ref, t_hbm, *refs, scale, slots, window, parts):
    x_parts = refs[:parts]
    top_ref, tot_ref, t_vmem, x_vmem, t_sem, x_sem = refs[parts:]
    arrive, per = load_all(t_hbm, x_parts, t_vmem, x_vmem, t_sem, x_sem, window)
    top_ref[...] = jnp.full(top_ref.shape, VERY_LOW, jnp.float32)
    tot_ref[...] = jnp.zeros(tot_ref.shape, jnp.float32)

    def step(q, j):
        arrive(q, j)
        s = q * per + j
        for c in range(slots):

            @pl.when(c < cnt_ref[s])
            def _():
                t = ids_ref[s * slots + c]
                k = lax.dot_general(x_vmem[s], t_vmem[t], NT_DIMS, preferred_element_type=jnp.float32)
                logits = f_ref[s] + k * scale
                old = top_ref[t]
                new = jnp.maximum(old, jnp.max(logits, axis=0, keepdims=True))
                tot_ref[t] = tot_ref[t] * jnp.exp(old - new) + jnp.sum(
                    jnp.exp(logits - new), axis=0, keepdims=True
                )
                top_ref[t] = new

    for q in range(parts):
        lax.fori_loop(0, per, lambda j, carry, q=q: (step(q, j), carry)[1], 0)


def resident_call(body, ids, cnt, side, targets, x_parts, rows, out_shape, scale):
    tiles, width, depth = targets.shape
    blocks = sum(x.shape[0] for x in x_parts)
    slots = ids.shape[1]
    smem = pl.BlockSpec(memory_space=pltpu.SMEM)
    vmem = pl.BlockSpec(memory_space=pltpu.VMEM)
    hbm = pl.BlockSpec(memory_space=pl.ANY)
    cost = pl.CostEstimate(
        flops=2 * blocks * slots * rows * width * depth,
        transcendentals=blocks * slots * rows * width,
        bytes_accessed=2 * (targets.size + blocks * rows * depth),
    )
    kernel = lambda *refs: body(*refs, scale=scale, slots=slots, window=4, parts=len(x_parts))
    return pl.pallas_call(
        kernel,
        out_shape=(out_shape, out_shape),
        in_specs=[smem, smem, vmem, hbm] + [hbm] * len(x_parts),
        out_specs=(vmem, vmem),
        scratch_shapes=[
            pltpu.VMEM((tiles, width, depth), targets.dtype),
            pltpu.VMEM((blocks, rows, depth), x_parts[0].dtype),
            pltpu.SemaphoreType.DMA((tiles,)),
            pltpu.SemaphoreType.DMA((blocks,)),
        ],
        compiler_params=pltpu.CompilerParams(vmem_limit_bytes=56 * 1024 * 1024),
        cost_estimate=cost,
    )(ids.reshape(-1), cnt, side, targets, *x_parts)


def local_body(sources, log_a, targets, g_old, log_b, tile_ids, live_count):
    tiles_own, width, depth = targets.shape
    rows = sources.shape[0]
    slots_per = tile_ids.shape[2]
    groups = tile_ids.shape[1]
    me = lax.axis_index(SRC)
    core = lax.axis_index(CORE)
    scale = 1.0 / (math.sqrt(depth) * EPSILON)

    meta = jnp.concatenate([tile_ids[0].reshape(-1), live_count[0].reshape(-1)])
    meta_rows = jnp.zeros((16, depth), jnp.bfloat16).at[0, : meta.shape[0]].set(
        meta.astype(jnp.bfloat16)
    )
    packed = jnp.concatenate([sources, meta_rows], axis=0)
    x_own = lax.all_gather(packed, CHIPS)
    pairs = lax.axis_size(CORE)
    x_other = lax.ppermute(x_own, CORE, [(i, (i + 1) % pairs) for i in range(pairs)])
    per = x_own.shape[0]
    blocks = per * pairs
    pos = jnp.arange(per, dtype=jnp.int32) * pairs
    order = jnp.concatenate([pos + core, pos + (core + 1) % pairs])

    def listed(meta_part):
        meta_part = meta_part.astype(jnp.int32)
        ids_part = meta_part[:, : groups * slots_per].reshape(per, groups, slots_per)
        ids_part = lax.dynamic_index_in_dim(ids_part, me, 1, False) - me * tiles_own
        cnt_part = lax.dynamic_index_in_dim(meta_part[:, groups * slots_per :], me, 1, False)
        return jnp.clip(ids_part, 0, tiles_own - 1), cnt_part

    g_col = (g_old.astype(jnp.float32) / EPSILON)[:, :, None]
    stat_shape = jax.ShapeDtypeStruct((per, 1, rows), jnp.float32)
    ids_a, cnt_a = listed(x_own[:, rows, : meta.shape[0]])
    top_a, total_a = resident_call(
        row_kernel, ids_a, cnt_a, g_col, targets, [x_own], rows, stat_shape, scale
    )
    meta_b, top_a = lax.optimization_barrier((x_other[:, rows, : meta.shape[0]], top_a))
    ids_b, cnt_b = listed(meta_b)
    my_ids = jnp.concatenate([ids_a, ids_b])
    my_cnt = jnp.concatenate([cnt_a, cnt_b])
    top_b, total_b = resident_call(
        row_kernel, ids_b, cnt_b, g_col, targets, [x_other], rows, stat_shape, scale
    )
    inverse = jnp.argsort(order)
    row_top = jnp.concatenate([top_a, top_b]).reshape(blocks, rows)[inverse]
    row_total = jnp.concatenate([total_a, total_b]).reshape(blocks, rows)[inverse]
    stats = jnp.concatenate([row_top, row_total, log_a[None]], axis=0)
    stats_all = lax.all_to_all(
        jnp.broadcast_to(stats[None], (blocks,) + stats.shape), SRC, 0, 0, tiled=True
    )
    tops = stats_all[:, :blocks]
    top = jnp.max(tops, axis=0)
    total = jnp.sum(stats_all[:, blocks : 2 * blocks] * jnp.exp(tops - top[None]), axis=0)
    log_a_all = stats_all[:, 2 * blocks]
    f_all = EPSILON * log_a_all - EPSILON * (top + jnp.log(total))
    f_new = lax.dynamic_index_in_dim(f_all, me, 0, False)

    f_col = (f_all[order] / EPSILON)[:, :, None]
    tile_top, tile_total = resident_call(
        col_kernel, my_ids, my_cnt, f_col, targets, [x_own, x_other], rows,
        jax.ShapeDtypeStruct((tiles_own, 1, width), jnp.float32), scale,
    )
    col = jnp.concatenate([tile_top.reshape(tiles_own, width), tile_total.reshape(tiles_own, width)])
    loop_size = lax.axis_size(LOOP)
    col_all = lax.all_to_all(
        jnp.broadcast_to(col[None], (loop_size,) + col.shape), LOOP, 0, 0, tiled=True
    )
    tops = col_all[:, :tiles_own]
    all_top = jnp.max(tops, axis=0)
    all_total = jnp.sum(col_all[:, tiles_own:] * jnp.exp(tops - all_top[None]), axis=0)
    g_new = EPSILON * log_b - EPSILON * (all_top + jnp.log(all_total))
    return (f_new, g_new)


PARTS = (("x_lo", 2), ("z", 4), ("core", 2), ("x_hi", 2), ("y", 4))
CHIPS = ("x_lo", "z")
CORE = "core"
SRC = ("x_lo", "z", "core")
LOOP = ("x_hi", "y")


def solution(mesh):
    parted = Mesh(
        mesh.devices.reshape(tuple(size for _, size in PARTS)), tuple(name for name, _ in PARTS)
    )
    rows_spec = SRC + LOOP
    return jax.shard_map(
        local_body,
        mesh=parted,
        in_specs=(
            P(rows_spec, None),
            P(rows_spec),
            P(SRC, None, None),
            P(SRC, None),
            P(SRC, None),
            P(rows_spec, None, None),
            P(rows_spec, None),
        ),
        out_specs=(P(rows_spec), P(SRC, None)),
        check_vma=False,
    )
```

time: 204 us -> 212 us (1.039)
  blocking collectives: 25.5 us -> 0 us
  waiting for transfers between devices: 81.8 us -> 104 us
  starting transfers between devices: 5.04 us -> 11 us
  local copies, waits for them, and re-layouts: 9.5 us -> 14.5 us
  other arithmetic: 11 us -> 8.05 us
    all_to_all x1 -> x0, blocking collectives: 25.5 us -> none  [local(): lax.all_to_all(jnp.broadcast_to(stats[None], (blocks,) + stats.shape), 's...]
    all_to_all x1 -> x2, waiting for transfers between devices: 8.13 us -> 27.1 us  [the longest x1 18.5 us: local_body(): lax.all_to_all(jnp.broadcast_to(stats[None], (blocks,) + stats.shape), SR...]
    all_to_all x1 -> x2, starting transfers between devices: 5 us -> 10.9 us  [the longest x1 6.5 us: local_body(): lax.all_to_all(jnp.broadcast_to(col[None], (loop_size,) + col.shape), LOO...]
    div x1, other arithmetic: 4.52 us -> 0.01 us  [local_body(): f_col = (f_all[order] / EPSILON)[:, :, None]]
    all_gather x1, waiting for transfers between devices: 73.7 us -> 76.9 us  [local_body(): x_own = lax.all_gather(packed, CHIPS)]
    div x0 -> x1, local copies, waits for them, and re-layouts: none -> 2.65 us  [local_body(): f_col = (f_all[order] / EPSILON)[:, :, None]]
    sub x1 -> x0, local copies, waits for them, and re-layouts: 2.65 us -> none  [local(): f_all = EPSILON * log_a_all - EPSILON * (top + jnp.log(total))]
    pallas_call x2 -> x3, Pallas kernels: 57.1 us -> 59 us  [resident_call(): pl.pallas_call(kernel, out_shape=(out_shape, out_shape), in_specs=[smem,...]
  transfers between devices with their start and end apart: 2 -> 4, of which waited for: 2 -> 3; matrix products, arithmetic and copies ran while one was open for 2% -> 3% of each run, Pallas kernels for 0% -> 9%
where the time goes in v8:
time: 212 us; the launch traced here: 211 us
  waiting for transfers between devices  104 us (49%)
  Pallas kernels  59 us (28%)
  local copies, waits for them, and re-layouts  14.5 us (7%)
  between operations  14.2 us (7%)
  starting transfers between devices  11 us (5%)
  other arithmetic  8.05 us (4%)
    all_gather x1, waiting for transfers between devices, local_body(): x_own = lax.all_gather(packed, CHIPS)  76.9 us
    pallas_call x3, Pallas kernels, resident_call(): pl.pallas_call(kernel, out_shape=(out_shape, out_shape), in_specs=[smem,...  59 us
    all_to_all x1, waiting for transfers between devices, local_body(): lax.all_to_all(jnp.broadcast_to(stats[None], (blocks,) + stats.shape), SR...  18.5 us
    all_to_all x1, waiting for transfers between devices, local_body(): lax.all_to_all(jnp.broadcast_to(col[None], (loop_size,) + col.shape), LOO...  8.6 us
    all_to_all x1, starting transfers between devices, local_body(): lax.all_to_all(jnp.broadcast_to(col[None], (loop_size,) + col.shape), LOO...  6.5 us
    all_to_all x1, starting transfers between devices, local_body(): lax.all_to_all(jnp.broadcast_to(stats[None], (blocks,) + stats.shape), SR...  4.41 us
  transfers between devices with their start and end apart: 4, of which 3 were waited for; matrix products, arithmetic and copies ran while one was open for 3% of the time, Pallas kernels for 9%

profile of v8, /device:TPU:0, one launch (start us, length us, event | category | flops | bytes accessed | tf_op | source)
XLA Modules:
  0.0 210.8 jit_solution(4860344774669439937)
XLA Ops:
  7.2 0.7 convert.8
  7.9 0.7 convert.9
  8.8 2.1 pad_maximum_fusion
  11.0 76.9 %all-gather.3.cloned.1.call-done = bf16[4224,768]{1,0:T(8,128)(2,1)} async-done(((bf16[528,768]{1,0:T(8,128)(2,1)}), bf16[4224,768]{1,0:T(8,128)(2,1)}) %all-gather.3.cloned.1.call-update) | async-done | bytes 6488080 | tf_op jit(solution)/shard_map/all_gather | solution.py:146
  87.8 2.0 copy.37.refs_2_
  89.9 1.2 sort.17
  91.2 0.7 slice_convert_fusion
  92.0 0.7 dynamic-slice_reduce_fusion.1.refs_1_
  93.4 18.5 %shard_map.86 = (f32[8,1,512]{2,1,0:T(1,128)}, f32[8,1,512]{2,1,0:T(1,128)}) custom-call(s32[16]{0:T(128)} %min.22.refs_0_, s32[8]{0:T(128)} %dynamic-slice_reduce_fusion.1.refs_1_, f32[8,512,1]{2,1,0:T(8,128)} %copy.37.refs_2_, bf16[8,512,768]{2,1,0:T(8,128)(2,1)} %refs_3_.5, bf16[8,528,768]{2,1,0:T(8,128)(2,1)} %bitcast.61), custom_call_target="tpu_custom_call" | custom-call | flops 6442450944 | bytes 12582912 | tf_op jit(solution)/shard_map/pallas_call | solution.py:116
  111.9 0.7 slice.66
  112.9 0.6 compare_select_fusion.1
  114.3 13.1 %shard_map.87 = (f32[8,1,512]{2,1,0:T(1,128)}, f32[8,1,512]{2,1,0:T(1,128)}) custom-call(s32[16]{0:T(128)} %min.24.refs_0_, s32[8]{0:T(128)} %copy-done.6, f32[8,512,1]{2,1,0:T(8,128)} %copy.37.refs_2_, bf16[8,512,768]{2,1,0:T(8,128)(2,1)} %refs_3_.5, bf16[8,528,768]{2,1,0:T(8,128)(2,1)} %collective-permute-done.refs_4_.refs_5_), custom_call_target="tpu_custom_call" | custom-call | flops 6442450944 | bytes 12582912 | tf_op jit(solution)/shard_map/pallas_call | solution.py:116
  127.4 0.8 pad_maximum_fusion.2
  129.4 1.2 broadcast_in_dim.13
  130.7 4.4 %all-to-all-start = ((f32[16,33,512]{2,1,0:T(8,128)}), f32[16,33,512]{2,1,0:T(8,128)S(1)}, u32[]{:S(2)}, u32[]{:S(2)}) async-start(f32[16,33,512]{2,1,0:T(8,128)} %broadcast_in_dim.13), calls=%async_computation | async-start | bytes 2621440 | tf_op jit(solution)/shard_map/all_to_all | solution.py:178
  136.0 18.5 %all-to-all-done = f32[16,33,512]{2,1,0:T(8,128)S(1)} async-done(((f32[16,33,512]{2,1,0:T(8,128)}), f32[16,33,512]{2,1,0:T(8,128)S(1)}, u32[]{:S(2)}, u32[]{:S(2)}) %all-to-all-start) | async-done | bytes 1081376 | tf_op jit(solution)/shard_map/all_to_all | solution.py:178
  155.3 2.6 %copy.43.refs_2_ = f32[16,512,1]{2,1,0:T(8,128)} copy(f32[16,512,1]{1,0,2:T(8,128)S(1)} %multiply_bitcast_fusion) | data formatting | bytes 65536 | tf_op jit(solution)/shard_map/div | solution.py:188
  157.9 27.5 %shard_map.88 = (f32[8,1,512]{2,1,0:T(1,128)}, f32[8,1,512]{2,1,0:T(1,128)}) custom-call(s32[32]{0:T(128)} %reshape.172.refs_0_, s32[16]{0:T(128)} %get-tuple-element.33.refs_1_, f32[16,512,1]{2,1,0:T(8,128)} %copy.43.refs_2_, bf16[8,512,768]{2,1,0:T(8,128)(2,1)} %refs_3_.5, bf16[8,528,768]{2,1,0:T(8,128)(2,1)} %bitcast.62, ...), custom_call_target="tpu_custom_call" | custom-call | flops 12884901888 | bytes 18874368 | tf_op jit(solution)/shard_map/pallas_call | solution.py:116
  185.4 0.7 copy.63
  186.1 0.7 copy.62
  186.9 0.7 broadcast_in_dim.14
  187.6 6.5 %all-to-all-start.1 = ((f32[8,16,512]{2,1,0:T(8,128)}), f32[8,16,512]{2,1,0:T(8,128)S(1)}, u32[]{:S(2)}, u32[]{:S(2)}) async-start(f32[8,16,512]{2,1,0:T(8,128)} %broadcast_in_dim.14), calls=%async_computation.1 | async-start | bytes 524288 | tf_op jit(solution)/shard_map/all_to_all | solution.py:195
  194.7 8.6 %all-to-all-done.1 = f32[8,16,512]{2,1,0:T(8,128)S(1)} async-done(((f32[8,16,512]{2,1,0:T(8,128)}), f32[8,16,512]{2,1,0:T(8,128)S(1)}, u32[]{:S(2)}, u32[]{:S(2)}) %all-to-all-start.1) | async-done | bytes 262176 | tf_op jit(solution)/shard_map/all_to_all | solution.py:195
  203.3 0.6 multiply_subtract_fusion
  (63 shorter events, 5.8 us)
Async XLA Ops:
  7.2 80.7 %copy-start.3 = (bf16[8,512]{1,0:T(8,128)(2,1)S(1)}, bf16[8,512]{1,0:T(8,128)(2,1)}, u32[]{:S(2)}) copy-start(bf16[8,512]{1,0:T(8,128)(2,1)} %param.12) | copy-start | bytes 24580
  7.2 80.7 %all-gather.3.cloned.1.call-start = ((), (), s32[]{:S(2)}) async-start(), calls=%async_computation.2 | async-start | bytes 7299072 | tf_op jit(solution)/shard_map/all_gather | solution.py:146
  87.8 24.1 %collective-permute-start = (bf16[8,528,768]{2,1,0:T(8,128)(2,1)}, bf16[8,528,768]{2,1,0:T(8,128)(2,1)}, u32[]{:S(2)}, u32[]{:S(2)}) collective-permute-start(bf16[8,528,768]{2,1,0:T(8,128)(2,1)} %bitcast.59), channel_id=1, source_target_pairs={{0,8},{8,0},{1,9},{9,1},{2,10},{10,2},{3,11},{11,3},{4,12},{12,4},... | collective-permute-start | bytes 19464200 | tf_op jit(solution)/shard_map/ppermute | solution.py:148
  93.4 19.5 %copy-start.5 = (s32[8]{0:T(128)S(1)}, s32[8]{0:T(128)}, u32[]{:S(2)}) copy-start(s32[8]{0:T(128)} %dynamic-slice_reduce_fusion.1.refs_1_) | copy-start | bytes 100
  112.9 1.4 copy-start.6
  114.3 13.1 %copy-start.1 = (f32[8,1,512]{2,1,0:T(1,128)S(1)}, f32[8,1,512]{2,1,0:T(1,128)}, u32[]{:S(2)}) copy-start(f32[8,1,512]{2,1,0:T(1,128)} %get-tuple-element.24) | copy-start | bytes 49156
  114.3 13.1 %copy-start.2 = (f32[8,1,512]{2,1,0:T(1,128)S(1)}, f32[8,1,512]{2,1,0:T(1,128)}, u32[]{:S(2)}) copy-start(f32[8,1,512]{2,1,0:T(1,128)} %get-tuple-element.28) | copy-start | bytes 49156
  114.3 15.1 %copy-start.4 = (f32[512]{0:T(512)S(1)}, f32[512]{0:T(512)}, u32[]{:S(2)}) copy-start(f32[512]{0:T(512)} %param.10) | copy-start | bytes 6148
  130.7 23.8 %all-to-all-start = ((f32[16,33,512]{2,1,0:T(8,128)}), f32[16,33,512]{2,1,0:T(8,128)S(1)}, u32[]{:S(2)}, u32[]{:S(2)}) async-start(f32[16,33,512]{2,1,0:T(8,128)} %broadcast_in_dim.13), calls=%async_computation | async-start | bytes 2621440 | tf_op jit(solution)/shard_map/all_to_all | solution.py:178
  157.9 45.4 %copy-start = (f32[8,512]{1,0:T(8,128)S(1)}, f32[8,512]{1,0:T(8,128)}, u32[]{:S(2)}) copy-start(f32[8,512]{1,0:T(8,128)} %param.13) | copy-start | bytes 49156
  187.6 15.7 %all-to-all-start.1 = ((f32[8,16,512]{2,1,0:T(8,128)}), f32[8,16,512]{2,1,0:T(8,128)S(1)}, u32[]{:S(2)}, u32[]{:S(2)}) async-start(f32[8,16,512]{2,1,0:T(8,128)} %broadcast_in_dim.14), calls=%async_computation.1 | async-start | bytes 524288 | tf_op jit(solution)/shard_map/all_to_all | solution.py:195
Sparse Core Ops, SparseCore 0:
  11.1 76.7 all-gather.2

commit v9 on v7

--- a/solution.py
+++ b/solution.py
@@ -103,7 +103,7 @@
         transcendentals=blocks * slots * rows * width,
         bytes_accessed=2 * (targets.size + blocks * rows * depth),
     )
-    kernel = lambda *refs: body(*refs, scale=scale, slots=slots, window=4)
+    kernel = lambda *refs: body(*refs, scale=scale, slots=slots, window=16)
     return pl.pallas_call(
         kernel,
         out_shape=(out_shape, out_shape),

time: 204 us -> 209 us (1.025)
  Pallas kernels: 57.1 us -> 62.5 us
  blocking collectives: 25.5 us -> 23.3 us
    pallas_call x2, Pallas kernels: 57.1 us -> 62.5 us  [resident_call(): pl.pallas_call(kernel, out_shape=(out_shape, out_shape), in_specs=[smem,...]
    all_to_all x1, blocking collectives: 25.5 us -> 23.3 us  [local(): lax.all_to_all(jnp.broadcast_to(stats[None], (blocks,) + stats.shape), 's...]
where the time goes in v9:
time: 209 us
  waiting for transfers between devices  81.8 us (39%)
  Pallas kernels  62.5 us (30%)
  blocking collectives  23.3 us (11%)
  between operations  14.1 us (7%)
  other arithmetic  11 us (5%)
  local copies, waits for them, and re-layouts  9.5 us (5%)
  starting transfers between devices  6.61 us (3%)
    all_gather x1, waiting for transfers between devices, local(): x_all = lax.all_gather(packed, 'src')  73.7 us
    pallas_call x2, Pallas kernels, resident_call(): pl.pallas_call(kernel, out_shape=(out_shape, out_shape), in_specs=[smem,...  62.5 us
    all_to_all x1, blocking collectives, local(): lax.all_to_all(jnp.broadcast_to(stats[None], (blocks,) + stats.shape), 's...  23.3 us
    all_to_all x1, waiting for transfers between devices, local(): lax.all_to_all(jnp.broadcast_to(col[None], (loop_size,) + col.shape), 'lo...  8.13 us
    all_to_all x1, starting transfers between devices, local(): lax.all_to_all(jnp.broadcast_to(col[None], (loop_size,) + col.shape), 'lo...  6.57 us
    div x1, other arithmetic, local(): f_col = (f_all / EPSILON)[:, :, None]  4.52 us
  transfers between devices with their start and end apart: 2, of which 2 were waited for; matrix products, arithmetic and copies ran while one was open for 2% of the time, Pallas kernels for 0%

profile of v9, /device:TPU:0, one launch (start us, length us, event | category | flops | bytes accessed | tf_op | source)
XLA Modules:
  0.0 208.8 jit_solution(5043285372994064124)
XLA Ops:
  7.2 0.7 convert.8
  7.9 0.7 convert.9
  8.8 2.1 %pad_maximum_fusion = bf16[528,768]{1,0:T(8,128)(2,1)} fusion(bf16[16,768]{1,0:T(8,128)(2,1)S(1)} %fusion.8, bf16[512,768]{1,0:T(8,128)(2,1)} %param.9), kind=kLoop, calls=%fused_computation.1 | loop fusion | flops 1622016 | bytes 1622016 | tf_op jit(solution)/shard_map/concatenate | solution.py:135
  10.9 0.7 multiply_bitcast_fusion
  11.7 2.0 copy.40.refs_2_
  13.6 73.7 %all-gather.3.cloned.1.call-done = bf16[8448,768]{1,0:T(8,128)(2,1)} async-done(((bf16[528,768]{1,0:T(8,128)(2,1)}), bf16[8448,768]{1,0:T(8,128)(2,1)}) %all-gather.3.cloned.1.call-update) | async-done | bytes 12976144 | tf_op jit(solution)/shard_map/all_gather | solution.py:136
  87.3 0.8 slice_convert_fusion
  88.2 0.7 dynamic-slice_reduce_fusion.refs_1_
  89.0 0.6 min.12.refs_0_
  89.6 30.8 %shard_map.86 = (f32[16,1,512]{2,1,0:T(1,128)}, f32[16,1,512]{2,1,0:T(1,128)}) custom-call(s32[32]{0:T(128)} %min.12.refs_0_, s32[16]{0:T(128)} %dynamic-slice_reduce_fusion.refs_1_, f32[8,512,1]{2,1,0:T(8,128)} %copy.40.refs_2_, bf16[8,512,768]{2,1,0:T(8,128)(2,1)} %refs_3_.3, bf16[16,528,768]{2,1,0:T(8,128)(2,1)} %bitcast.34), custom_call_target="tpu_custom_call" | custom-call | flops 12884901888 | bytes 18874368 | tf_op jit(solution)/shard_map/pallas_call | solution.py:107
  120.5 0.8 copy_bitcast_fusion
  121.3 0.1 broadcast_in_dim.10
  121.4 23.3 %all_to_all.10 = f32[16,33,512]{2,1,0:T(8,128)S(1)} all-to-all(f32[16,33,512]{2,1,0:T(8,128)S(1)} %broadcast_in_dim.10), channel_id=1, replica_groups=mesh['src'=16,'loop'=8] {'src'}, dimensions={0} | all-to-all | bytes 2162688 | tf_op jit(solution)/shard_map/all_to_all | solution.py:152
  144.8 0.1 fusion
  145.0 2.6 %copy.42 = f32[16,512,1]{2,1,0:T(8,128)} copy(f32[16,512,1]{1,0,2:T(8,128)S(1)} %get-tuple-element.22) | data formatting | bytes 65536 | tf_op jit(solution)/shard_map/sub | solution.py:159
  147.6 4.5 %broadcast_multiply_fusion.refs_2_ = f32[16,512,1]{2,1,0:T(8,128)} fusion(f32[16,512,1]{2,1,0:T(8,128)} %copy.42), kind=kLoop, calls=%fused_computation | loop fusion | flops 8192 | bytes 65536 | tf_op jit(solution)/shard_map/div | solution.py:162
  152.1 31.6 %shard_map.87 = (f32[8,1,512]{2,1,0:T(1,128)}, f32[8,1,512]{2,1,0:T(1,128)}) custom-call(s32[32]{0:T(128)} %min.12.refs_0_, s32[16]{0:T(128)} %dynamic-slice_reduce_fusion.refs_1_, f32[16,512,1]{2,1,0:T(8,128)} %broadcast_multiply_fusion.refs_2_, bf16[8,512,768]{2,1,0:T(8,128)(2,1)} %refs_3_.3, bf16[16,528,768]{2,1,0:T(8,128)(2,1)} %bitcast.35), custom_call_target="tpu_custom_call" | custom-call | flops 12884901888 | bytes 18874368 | tf_op jit(solution)/shard_map/pallas_call | solution.py:107
  183.8 0.7 copy.58
  184.5 0.7 copy.57
  185.2 0.7 broadcast_in_dim.11
  185.9 6.6 %all-to-all-start.1 = ((f32[8,16,512]{2,1,0:T(8,128)}), f32[8,16,512]{2,1,0:T(8,128)S(1)}, u32[]{:S(2)}, u32[]{:S(2)}) async-start(f32[8,16,512]{2,1,0:T(8,128)} %broadcast_in_dim.11), calls=%async_computation.1 | async-start | bytes 524288 | tf_op jit(solution)/shard_map/all_to_all | solution.py:169
  192.5 0.6 dynamic-slice_subtract_fusion
  193.1 8.1 %all-to-all-done.1 = f32[8,16,512]{2,1,0:T(8,128)S(1)} async-done(((f32[8,16,512]{2,1,0:T(8,128)}), f32[8,16,512]{2,1,0:T(8,128)S(1)}, u32[]{:S(2)}, u32[]{:S(2)}) %all-to-all-start.1) | async-done | bytes 262176 | tf_op jit(solution)/shard_map/all_to_all | solution.py:169
  201.3 0.6 multiply_subtract_fusion
  (21 shorter events, 0.7 us)
Async XLA Ops:
  7.2 80.1 %all-gather.3.cloned.1.call-start = ((), (), s32[]{:S(2)}) async-start(), calls=%async_computation.2 | async-start | bytes 13787136 | tf_op jit(solution)/shard_map/all_gather | solution.py:136
  89.6 31.6 %copy-start.1 = (f32[512]{0:T(512)S(1)}, f32[512]{0:T(512)}, u32[]{:S(2)}) copy-start(f32[512]{0:T(512)} %param.10) | copy-start | bytes 6148
  152.1 49.2 %copy-start = (f32[8,512]{1,0:T(8,128)S(1)}, f32[8,512]{1,0:T(8,128)}, u32[]{:S(2)}) copy-start(f32[8,512]{1,0:T(8,128)} %param.13) | copy-start | bytes 49156
  185.9 15.3 %all-to-all-start.1 = ((f32[8,16,512]{2,1,0:T(8,128)}), f32[8,16,512]{2,1,0:T(8,128)S(1)}, u32[]{:S(2)}, u32[]{:S(2)}) async-start(f32[8,16,512]{2,1,0:T(8,128)} %broadcast_in_dim.11), calls=%async_computation.1 | async-start | bytes 524288 | tf_op jit(solution)/shard_map/all_to_all | solution.py:169
Sparse Core Ops, SparseCore 0:
  11.1 76.1 all-gather.2

commit v10 on v7

--- a/solution.py
+++ b/solution.py
@@ -12,7 +12,7 @@
 NT_DIMS = (((1,), (1,)), ((), ()))
 
 
-def load_all(t_hbm, x_hbm, t_vmem, x_vmem, t_sem, x_sem, window):
+def load_all(order_ref, t_hbm, x_hbm, t_vmem, x_vmem, t_sem, x_sem, flags, window):
     tiles, blocks = t_vmem.shape[0], x_vmem.shape[0]
     rows = x_vmem.shape[1]
 
@@ -23,11 +23,16 @@
         return pltpu.make_async_copy(t_hbm.at[t], t_vmem.at[t], t_sem.at[t])
 
     for t in range(tiles):
-        t_copy(t).start()
-    for s in range(min(window, blocks)):
-        x_copy(s).start()
-    for t in range(tiles):
-        t_copy(t).wait()
+        flags[t] = 0
+    issue = [("x", 0), ("t", 0), ("t", 1), ("x", 1), ("t", 2), ("x", 2), ("t", 3), ("x", 3)]
+    issue = [item for item in issue if item[1] < (blocks if item[0] == "x" else tiles)]
+    issue += [("x", s) for s in range(4, min(window, blocks))]
+    issue += [("t", k) for k in range(4, tiles)]
+    for kind, k in issue:
+        if kind == "x":
+            x_copy(k).start()
+        else:
+            t_copy(order_ref[k]).start()
 
     def arrive(s):
         x_copy(s).wait()
@@ -36,11 +41,21 @@
         def _():
             x_copy(jnp.minimum(s + window, blocks - 1)).start()
 
-    return arrive
-
-
-def row_kernel(ids_ref, cnt_ref, g_ref, t_hbm, x_hbm, top_ref, tot_ref, t_vmem, x_vmem, t_sem, x_sem, *, scale, slots, window):
-    arrive = load_all(t_hbm, x_hbm, t_vmem, x_vmem, t_sem, x_sem, window)
+    def need(t):
+        @pl.when(flags[t] == 0)
+        def _():
+            t_copy(t).wait()
+            flags[t] = 1
+
+    def finish():
+        for t in range(tiles):
+            need(t)
+
+    return arrive, need, finish
+
+
+def row_kernel(ids_ref, cnt_ref, order_ref, g_ref, t_hbm, x_hbm, top_ref, tot_ref, t_vmem, x_vmem, t_sem, x_sem, flags, *, scale, slots, window):
+    arrive, need, finish = load_all(order_ref, t_hbm, x_hbm, t_vmem, x_vmem, t_sem, x_sem, flags, window)
 
     def step(s, carry):
         arrive(s)
@@ -51,6 +66,7 @@
             @pl.when(c < cnt_ref[s])
             def _():
                 t = ids_ref[s * slots + c]
+                need(t)
                 kt = lax.dot_general(t_vmem[t], x_vmem[s], NT_DIMS, preferred_element_type=jnp.float32)
                 logits = g_ref[t] + kt * scale
                 old = top_ref[s]
@@ -63,10 +79,11 @@
         return carry
 
     lax.fori_loop(0, x_vmem.shape[0], step, 0)
-
-
-def col_kernel(ids_ref, cnt_ref, f_ref, t_hbm, x_hbm, top_ref, tot_ref, t_vmem, x_vmem, t_sem, x_sem, *, scale, slots, window):
-    arrive = load_all(t_hbm, x_hbm, t_vmem, x_vmem, t_sem, x_sem, window)
+    finish()
+
+
+def col_kernel(ids_ref, cnt_ref, order_ref, f_ref, t_hbm, x_hbm, top_ref, tot_ref, t_vmem, x_vmem, t_sem, x_sem, flags, *, scale, slots, window):
+    arrive, need, finish = load_all(order_ref, t_hbm, x_hbm, t_vmem, x_vmem, t_sem, x_sem, flags, window)
     top_ref[...] = jnp.full(top_ref.shape, VERY_LOW, jnp.float32)
     tot_ref[...] = jnp.zeros(tot_ref.shape, jnp.float32)
 
@@ -77,6 +94,7 @@
             @pl.when(c < cnt_ref[s])
             def _():
                 t = ids_ref[s * slots + c]
+                need(t)
                 k = lax.dot_general(x_vmem[s], t_vmem[t], NT_DIMS, preferred_element_type=jnp.float32)
                 logits = f_ref[s] + k * scale
                 old = top_ref[t]
@@ -89,6 +107,16 @@
         return carry
 
     lax.fori_loop(0, x_vmem.shape[0], step, 0)
+    finish()
+
+
+def first_use_order(ids, cnt, tiles):
+    blocks, slots = ids.shape
+    live = jnp.arange(slots, dtype=jnp.int32)[None, :] < cnt[:, None]
+    position = jnp.arange(blocks * slots, dtype=jnp.int32).reshape(blocks, slots)
+    hit = (ids[:, :, None] == jnp.arange(tiles, dtype=jnp.int32)) & live[:, :, None]
+    first = jnp.min(jnp.where(hit, position[:, :, None], blocks * slots), axis=(0, 1))
+    return jnp.argsort(first).astype(jnp.int32)
 
 
 def resident_call(body, ids, cnt, side, targets, x_all, rows, out_shape, scale):
@@ -107,17 +135,18 @@
     return pl.pallas_call(
         kernel,
         out_shape=(out_shape, out_shape),
-        in_specs=[smem, smem, vmem, hbm, hbm],
+        in_specs=[smem, smem, smem, vmem, hbm, hbm],
         out_specs=(vmem, vmem),
         scratch_shapes=[
             pltpu.VMEM((tiles, width, depth), targets.dtype),
             pltpu.VMEM((blocks, rows, depth), x_all.dtype),
             pltpu.SemaphoreType.DMA((tiles,)),
             pltpu.SemaphoreType.DMA((blocks,)),
+            pltpu.SMEM((tiles,), jnp.int32),
         ],
         compiler_params=pltpu.CompilerParams(vmem_limit_bytes=56 * 1024 * 1024),
         cost_estimate=cost,
-    )(ids.reshape(-1), cnt, side, targets, x_all)
+    )(ids.reshape(-1), cnt, first_use_order(ids, cnt, tiles), side, targets, x_all)
 
 
 def local(sources, log_a, targets, g_old, log_b, tile_ids, live_count):

time: 204 us -> 202 us (level)
  blocking collectives: 25.5 us -> 22.6 us
  Pallas kernels: 57.1 us -> 54.7 us
    all_to_all x1, blocking collectives: 25.5 us -> 22.6 us  [local(): lax.all_to_all(jnp.broadcast_to(stats[None], (blocks,) + stats.shape), 's...]
    pallas_call x2, Pallas kernels: 57.1 us -> 54.7 us  [resident_call(): pl.pallas_call(kernel, out_shape=(out_shape, out_shape), in_specs=[smem,...]
where the time goes in v10:
time: 202 us; the launch traced here: 201 us
  waiting for transfers between devices  82.5 us (41%)
  Pallas kernels  54.7 us (27%)
  blocking collectives  22.6 us (11%)
  between operations  14.1 us (7%)
  other arithmetic  12.1 us (6%)
  local copies, waits for them, and re-layouts  8.95 us (4%)
  starting transfers between devices  5.75 us (3%)
    all_gather x1, waiting for transfers between devices, local(): x_all = lax.all_gather(packed, 'src')  73.7 us
    pallas_call x2, Pallas kernels, resident_call(): pl.pallas_call(kernel, out_shape=(out_shape, out_shape), in_specs=[smem,...  54.7 us
    all_to_all x1, blocking collectives, local(): lax.all_to_all(jnp.broadcast_to(stats[None], (blocks,) + stats.shape), 's...  22.6 us
    all_to_all x1, waiting for transfers between devices, local(): lax.all_to_all(jnp.broadcast_to(col[None], (loop_size,) + col.shape), 'lo...  8.83 us
    all_to_all x1, starting transfers between devices, local(): lax.all_to_all(jnp.broadcast_to(col[None], (loop_size,) + col.shape), 'lo...  5.71 us
    div x1, other arithmetic, local(): f_col = (f_all / EPSILON)[:, :, None]  4.52 us
  transfers between devices with their start and end apart: 2, of which 2 were waited for; matrix products, arithmetic and copies ran while one was open for 2% of the time, Pallas kernels for 0%

profile of v10, /device:TPU:0, one launch (start us, length us, event | category | flops | bytes accessed | tf_op | source)
XLA Modules:
  0.0 200.7 jit_solution(14327421170990248721)
XLA Ops:
  7.2 0.7 convert.8
  7.9 0.7 convert.9
  8.8 2.1 %pad_maximum_fusion = bf16[528,768]{1,0:T(8,128)(2,1)} fusion(bf16[16,768]{1,0:T(8,128)(2,1)S(1)} %fusion.8, bf16[512,768]{1,0:T(8,128)(2,1)} %param.9), kind=kLoop, calls=%fused_computation.1 | loop fusion | flops 1622016 | bytes 1622016 | tf_op jit(solution)/shard_map/concatenate | solution.py:164
  10.9 0.7 multiply_bitcast_fusion
  11.7 2.0 copy.45.refs_3_
  13.6 73.7 %all-gather.3.cloned.1.call-done = bf16[8448,768]{1,0:T(8,128)(2,1)} async-done(((bf16[528,768]{1,0:T(8,128)(2,1)}), bf16[8448,768]{1,0:T(8,128)(2,1)}) %all-gather.3.cloned.1.call-update) | async-done | bytes 12976144 | tf_op jit(solution)/shard_map/all_gather | solution.py:165
  87.3 0.8 slice_convert_fusion
  88.2 0.2 dynamic-slice_reduce_fusion.refs_1_
  88.5 0.6 min.14.refs_0_
  89.2 1.0 sort.19
  90.2 27.0 %shard_map.86 = (f32[16,1,512]{2,1,0:T(1,128)}, f32[16,1,512]{2,1,0:T(1,128)}) custom-call(s32[32]{0:T(128)} %min.14.refs_0_, s32[16]{0:T(128)} %copy-done.2, s32[8]{0:T(128)} %get-tuple-element.19.refs_2_, f32[8,512,1]{2,1,0:T(8,128)} %copy.45.refs_3_, bf16[8,512,768]{2,1,0:T(8,128)(2,1)} %refs_4_.3, bf16[16,528,768]{2,1,0:T(8,128)(2,1)} %bitcast.37), custom_call_target="tpu_custom_call" | custom-call | flops 12884901888 | bytes 18874368 | tf_op jit(solution)/shard_map/pallas_call | solution.py:135
  117.2 0.8 copy_bitcast_fusion
  118.0 0.1 broadcast_in_dim.28
  118.2 22.6 %all_to_all.10 = f32[16,33,512]{2,1,0:T(8,128)S(1)} all-to-all(f32[16,33,512]{2,1,0:T(8,128)S(1)} %broadcast_in_dim.28), channel_id=1, replica_groups=mesh['src'=16,'loop'=8] {'src'}, dimensions={0} | all-to-all | bytes 2162688 | tf_op jit(solution)/shard_map/all_to_all | solution.py:181
  141.0 2.6 %copy.47 = f32[16,512,1]{2,1,0:T(8,128)} copy(f32[16,512,1]{1,0,2:T(8,128)S(1)} %get-tuple-element.24) | data formatting | bytes 65536 | tf_op jit(solution)/shard_map/sub | solution.py:188
  143.7 4.5 %broadcast_multiply_fusion.refs_3_ = f32[16,512,1]{2,1,0:T(8,128)} fusion(f32[16,512,1]{2,1,0:T(8,128)} %copy.47), kind=kLoop, calls=%fused_computation | loop fusion | flops 8192 | bytes 65536 | tf_op jit(solution)/shard_map/div | solution.py:191
  148.2 27.7 %shard_map.87 = (f32[8,1,512]{2,1,0:T(1,128)}, f32[8,1,512]{2,1,0:T(1,128)}) custom-call(s32[32]{0:T(128)} %min.14.refs_0_, s32[16]{0:T(128)} %copy-done.2, s32[8]{0:T(128)} %get-tuple-element.19.refs_2_, f32[16,512,1]{2,1,0:T(8,128)} %broadcast_multiply_fusion.refs_3_, bf16[8,512,768]{2,1,0:T(8,128)(2,1)} %refs_4_.3, bf16[16,528,768]{2,1,0:T(8,128)(2,1)} %bitcast.38), custom_call_target="tpu_custom_call" | custom-call | flops 12884901888 | bytes 18874368 | tf_op jit(solution)/shard_map/pallas_call | solution.py:135
  175.9 0.7 copy.63
  176.6 0.7 copy.62
  177.3 0.7 broadcast_in_dim.29
  178.0 5.7 %all-to-all-start.1 = ((f32[8,16,512]{2,1,0:T(8,128)}), f32[8,16,512]{2,1,0:T(8,128)S(1)}, u32[]{:S(2)}, u32[]{:S(2)}) async-start(f32[8,16,512]{2,1,0:T(8,128)} %broadcast_in_dim.29), calls=%async_computation.1 | async-start | bytes 524288 | tf_op jit(solution)/shard_map/all_to_all | solution.py:198
  183.8 0.6 dynamic-slice_subtract_fusion
  184.4 8.8 %all-to-all-done.1 = f32[8,16,512]{2,1,0:T(8,128)S(1)} async-done(((f32[8,16,512]{2,1,0:T(8,128)}), f32[8,16,512]{2,1,0:T(8,128)S(1)}, u32[]{:S(2)}, u32[]{:S(2)}) %all-to-all-start.1) | async-done | bytes 262176 | tf_op jit(solution)/shard_map/all_to_all | solution.py:198
  193.2 0.6 multiply_subtract_fusion
  (29 shorter events, 1.0 us)
Async XLA Ops:
  7.2 80.1 %all-gather.3.cloned.1.call-start = ((), (), s32[]{:S(2)}) async-start(), calls=%async_computation.2 | async-start | bytes 13787136 | tf_op jit(solution)/shard_map/all_gather | solution.py:165
  88.4 1.8 copy-start.2
  90.2 27.8 %copy-start.1 = (f32[512]{0:T(512)S(1)}, f32[512]{0:T(512)}, u32[]{:S(2)}) copy-start(f32[512]{0:T(512)} %param.10) | copy-start | bytes 6148
  148.2 45.1 %copy-start = (f32[8,512]{1,0:T(8,128)S(1)}, f32[8,512]{1,0:T(8,128)}, u32[]{:S(2)}) copy-start(f32[8,512]{1,0:T(8,128)} %param.13) | copy-start | bytes 49156
  178.0 15.1 %all-to-all-start.1 = ((f32[8,16,512]{2,1,0:T(8,128)}), f32[8,16,512]{2,1,0:T(8,128)S(1)}, u32[]{:S(2)}, u32[]{:S(2)}) async-start(f32[8,16,512]{2,1,0:T(8,128)} %broadcast_in_dim.29), calls=%async_computation.1 | async-start | bytes 524288 | tf_op jit(solution)/shard_map/all_to_all | solution.py:198
Sparse Core Ops, SparseCore 0:
  11.1 76.1 all-gather.2

commit v11 on v10

--- a/solution.py
+++ b/solution.py
@@ -5,7 +5,7 @@
 from jax import lax
 from jax.experimental import pallas as pl
 from jax.experimental.pallas import tpu as pltpu
-from jax.sharding import PartitionSpec as P
+from jax.sharding import Mesh, PartitionSpec as P
 
 EPSILON = 0.1
 VERY_LOW = -1e30
@@ -154,7 +154,7 @@
     rows = sources.shape[0]
     slots_per = tile_ids.shape[2]
     groups = tile_ids.shape[1]
-    me = lax.axis_index("src")
+    me = lax.axis_index(SRC)
     scale = 1.0 / (math.sqrt(depth) * EPSILON)
 
     meta = jnp.concatenate([tile_ids[0].reshape(-1), live_count[0].reshape(-1)])
@@ -162,9 +162,15 @@
         meta.astype(jnp.bfloat16)
     )
     packed = jnp.concatenate([sources, meta_rows], axis=0)
-    x_all = lax.all_gather(packed, "src")
+    x_pair = lax.all_gather(packed, CROSS)
+    x_all = lax.all_gather(x_pair, ALONG)
+    cross, along = x_all.shape[1], x_all.shape[0]
+    blocks = cross * along
+    x_all = x_all.reshape((blocks,) + packed.shape)
+    position = jnp.arange(blocks, dtype=jnp.int32)
+    order = (position % cross) * along + position // cross
+    inverse = jnp.argsort(order)
     meta_all = x_all[:, rows, : meta.shape[0]].astype(jnp.int32)
-    blocks = x_all.shape[0]
     ids_all = meta_all[:, : groups * slots_per].reshape(blocks, groups, slots_per)
     cnt_all = meta_all[:, groups * slots_per :]
     my_ids = jnp.clip(lax.dynamic_index_in_dim(ids_all, me, 1, False) - me * tiles_own, 0, tiles_own - 1)
@@ -176,10 +182,11 @@
         jax.ShapeDtypeStruct((blocks, 1, rows), jnp.float32), scale,
     )
     stats = jnp.concatenate(
-        [row_top.reshape(blocks, rows), row_total.reshape(blocks, rows), log_a[None]], axis=0
+        [row_top.reshape(blocks, rows)[inverse], row_total.reshape(blocks, rows)[inverse], log_a[None]],
+        axis=0,
     )
     stats_all = lax.all_to_all(
-        jnp.broadcast_to(stats[None], (blocks,) + stats.shape), "src", 0, 0, tiled=True
+        jnp.broadcast_to(stats[None], (blocks,) + stats.shape), SRC, 0, 0, tiled=True
     )
     tops = stats_all[:, :blocks]
     top = jnp.max(tops, axis=0)
@@ -188,15 +195,15 @@
     f_all = EPSILON * log_a_all - EPSILON * (top + jnp.log(total))
     f_new = lax.dynamic_index_in_dim(f_all, me, 0, False)
 
-    f_col = (f_all / EPSILON)[:, :, None]
+    f_col = (f_all[order] / EPSILON)[:, :, None]
     tile_top, tile_total = resident_call(
         col_kernel, my_ids, my_cnt, f_col, targets, x_all, rows,
         jax.ShapeDtypeStruct((tiles_own, 1, width), jnp.float32), scale,
     )
     col = jnp.concatenate([tile_top.reshape(tiles_own, width), tile_total.reshape(tiles_own, width)])
-    loop_size = lax.axis_size("loop")
+    loop_size = lax.axis_size(LOOP)
     col_all = lax.all_to_all(
-        jnp.broadcast_to(col[None], (loop_size,) + col.shape), "loop", 0, 0, tiled=True
+        jnp.broadcast_to(col[None], (loop_size,) + col.shape), LOOP, 0, 0, tiled=True
     )
     tops = col_all[:, :tiles_own]
     all_top = jnp.max(tops, axis=0)
@@ -205,19 +212,30 @@
     return (f_new, g_new)
 
 
+PARTS = (("x_lo", 2), ("z", 4), ("core", 2), ("x_hi", 2), ("y", 4))
+CROSS = "x_lo"
+ALONG = ("z", "core")
+SRC = ("x_lo", "z", "core")
+LOOP = ("x_hi", "y")
+
+
 def solution(mesh):
+    parted = Mesh(
+        mesh.devices.reshape(tuple(size for _, size in PARTS)), tuple(name for name, _ in PARTS)
+    )
+    rows_spec = SRC + LOOP
     return jax.shard_map(
         local,
-        mesh=mesh,
+        mesh=parted,
         in_specs=(
-            P(("src", "loop"), None),
-            P(("src", "loop")),
-            P("src", None, None),
-            P("src", None),
-            P("src", None),
-            P(("src", "loop"), None, None),
-            P(("src", "loop"), None),
+            P(rows_spec, None),
+            P(rows_spec),
+            P(SRC, None, None),
+            P(SRC, None),
+            P(SRC, None),
+            P(rows_spec, None, None),
+            P(rows_spec, None),
         ),
-        out_specs=(P(("src", "loop")), P("src", None)),
+        out_specs=(P(rows_spec), P(SRC, None)),
         check_vma=False,
     )

time: 202 us -> 227 us (1.12)
  waiting for transfers between devices: 82.5 us -> 129 us
  blocking collectives: 22.6 us -> 0 us
  other arithmetic: 12.1 us -> 6.78 us
  local copies, waits for them, and re-layouts: 8.95 us -> 12.9 us
    all_gather x1 -> x2, waiting for transfers between devices: 73.7 us -> 101 us  [the longest x1 68.6 us: local(): x_all = lax.all_gather(x_pair, ALONG)]
    all_to_all x1 -> x0, blocking collectives: 22.6 us -> none  [local(): lax.all_to_all(jnp.broadcast_to(stats[None], (blocks,) + stats.shape), 's...]
    all_to_all x1 -> x2, waiting for transfers between devices: 8.83 us -> 27.4 us  [the longest x1 19.3 us: local(): lax.all_to_all(jnp.broadcast_to(stats[None], (blocks,) + stats.shape), SR...]
    div x1, other arithmetic: 4.52 us -> 0.01 us  [local(): f_col = (f_all[order] / EPSILON)[:, :, None]]
    sub x1 -> x0, local copies, waits for them, and re-layouts: 2.65 us -> none  [local(): f_all = EPSILON * log_a_all - EPSILON * (top + jnp.log(total))]
    div x0 -> x1, local copies, waits for them, and re-layouts: none -> 2.65 us  [local(): f_col = (f_all[order] / EPSILON)[:, :, None]]
    all_to_all x1 -> x2, starting transfers between devices: 5.71 us -> 7.11 us  [the longest x1 3.7 us: local(): lax.all_to_all(jnp.broadcast_to(stats[None], (blocks,) + stats.shape), SR...]
  transfers between devices with their start and end apart: 2 -> 4, of which waited for: 2 -> 4; matrix products, arithmetic and copies ran while one was open for 2% -> 2% of each run, Pallas kernels for 0% -> 0%
where the time goes in v11:
time: 227 us; the launch traced here: 226 us
  waiting for transfers between devices  129 us (57%)
  Pallas kernels  56.3 us (25%)
  between operations  14.2 us (6%)
  local copies, waits for them, and re-layouts  12.9 us (6%)
  starting transfers between devices  7.19 us (3%)
  other arithmetic  6.78 us (3%)
    all_gather x1, waiting for transfers between devices, local(): x_all = lax.all_gather(x_pair, ALONG)  68.6 us
    pallas_call x2, Pallas kernels, resident_call(): pl.pallas_call(kernel, out_shape=(out_shape, out_shape), in_specs=[smem,...  56.3 us
    all_gather x1, waiting for transfers between devices, local(): x_pair = lax.all_gather(packed, CROSS)  32.8 us
    all_to_all x1, waiting for transfers between devices, local(): lax.all_to_all(jnp.broadcast_to(stats[None], (blocks,) + stats.shape), SR...  19.3 us
    all_to_all x1, waiting for transfers between devices, local(): lax.all_to_all(jnp.broadcast_to(col[None], (loop_size,) + col.shape), LOO...  8.07 us
  transfers between devices with their start and end apart: 4, of which 4 were waited for; matrix products, arithmetic and copies ran while one was open for 2% of the time, Pallas kernels for 0%

profile of v11, /device:TPU:0, one launch (start us, length us, event | category | flops | bytes accessed | tf_op | source)
XLA Modules:
  0.0 226.3 jit_solution(3838280869163850583)
XLA Ops:
  7.2 0.7 convert.8
  7.9 0.7 convert.9
  8.8 2.1 pad_maximum_fusion
  11.0 32.8 %all-gather.5.cloned.1.call-done = bf16[1056,768]{1,0:T(8,128)(2,1)} async-done(((bf16[528,768]{1,0:T(8,128)(2,1)}), bf16[1056,768]{1,0:T(8,128)(2,1)}) %all-gather.5.cloned.1.call-update) | async-done | bytes 1622032 | tf_op jit(solution)/shard_map/all_gather | solution.py:165
  43.9 2.0 copy.29.refs_3_
  45.9 1.2 sort.37
  47.1 68.6 %all-gather.7.cloned.1.call-done.refs_5_ = bf16[16,528,768]{2,1,0:T(8,128)(2,1)} async-done(((bf16[2,528,768]{2,1,0:T(8,128)(2,1)}), bf16[16,528,768]{2,1,0:T(8,128)(2,1)}) %all-gather.7.cloned.1.call-update) | async-done | bytes 12976144 | tf_op jit(solution)/shard_map/all_gather | solution.py:166
  115.7 0.8 slice.54
  116.8 0.6 min.14.refs_0_
  117.5 1.0 sort.36
  118.5 27.8 %shard_map.86 = (f32[16,1,512]{2,1,0:T(1,128)}, f32[16,1,512]{2,1,0:T(1,128)}) custom-call(s32[32]{0:T(128)} %min.14.refs_0_, s32[16]{0:T(128)} %copy-done.3, s32[8]{0:T(128)} %get-tuple-element.20.refs_2_, f32[8,512,1]{2,1,0:T(8,128)} %copy.29.refs_3_, bf16[8,512,768]{2,1,0:T(8,128)(2,1)} %refs_4_.3, bf16[16,528,768]{2,1,0:T(8,128)(2,1)} %all-gather.7.cloned.1.call-done.refs_5_), custom_call_target="tpu_custom_call" | custom-call | flops 12884901888 | bytes 18874368 | tf_op jit(solution)/shard_map/pallas_call | solution.py:135
  146.3 0.8 copy_bitcast_fusion
  148.3 1.2 broadcast_in_dim.31
  149.5 3.7 %all-to-all-start = ((f32[16,33,512]{2,1,0:T(8,128)}), f32[16,33,512]{2,1,0:T(8,128)S(1)}, u32[]{:S(2)}, u32[]{:S(2)}) async-start(f32[16,33,512]{2,1,0:T(8,128)} %broadcast_in_dim.31), calls=%async_computation | async-start | bytes 2621440 | tf_op jit(solution)/shard_map/all_to_all | solution.py:188
  153.2 19.3 %all-to-all-done = f32[16,33,512]{2,1,0:T(8,128)S(1)} async-done(((f32[16,33,512]{2,1,0:T(8,128)}), f32[16,33,512]{2,1,0:T(8,128)S(1)}, u32[]{:S(2)}, u32[]{:S(2)}) %all-to-all-start) | async-done | bytes 1081376 | tf_op jit(solution)/shard_map/all_to_all | solution.py:188
  173.4 2.6 %copy.31.refs_3_ = f32[16,512,1]{2,1,0:T(8,128)} copy(f32[16,512,1]{1,0,2:T(8,128)S(1)} %multiply_bitcast_fusion) | data formatting | bytes 65536 | tf_op jit(solution)/shard_map/div | solution.py:198
  176.0 28.5 %shard_map.87 = (f32[8,1,512]{2,1,0:T(1,128)}, f32[8,1,512]{2,1,0:T(1,128)}) custom-call(s32[32]{0:T(128)} %min.14.refs_0_, s32[16]{0:T(128)} %copy-done.3, s32[8]{0:T(128)} %get-tuple-element.20.refs_2_, f32[16,512,1]{2,1,0:T(8,128)} %copy.31.refs_3_, bf16[8,512,768]{2,1,0:T(8,128)(2,1)} %refs_4_.3, bf16[16,528,768]{2,1,0:T(8,128)(2,1)} %all-gather.7.cloned.1.call-done.refs_5_), custom_call_target="tpu_custom_call" | custom-call | flops 12884901888 | bytes 18874368 | tf_op jit(solution)/shard_map/pallas_call | solution.py:135
  204.5 0.7 copy.48
  205.2 0.7 copy.47
  206.0 0.7 broadcast_in_dim.32
  206.7 3.4 %all-to-all-start.1 = ((f32[8,16,512]{2,1,0:T(8,128)}), f32[8,16,512]{2,1,0:T(8,128)S(1)}, u32[]{:S(2)}, u32[]{:S(2)}) async-start(f32[8,16,512]{2,1,0:T(8,128)} %broadcast_in_dim.32), calls=%async_computation.1 | async-start | bytes 524288 | tf_op jit(solution)/shard_map/all_to_all | solution.py:205
  210.1 0.6 constant_dynamic-slice_fusion
  210.7 8.1 %all-to-all-done.1 = f32[8,16,512]{2,1,0:T(8,128)S(1)} async-done(((f32[8,16,512]{2,1,0:T(8,128)}), f32[8,16,512]{2,1,0:T(8,128)S(1)}, u32[]{:S(2)}, u32[]{:S(2)}) %all-to-all-start.1) | async-done | bytes 262176 | tf_op jit(solution)/shard_map/all_to_all | solution.py:205
  218.8 0.6 multiply_subtract_fusion
  (46 shorter events, 2.8 us)
Async XLA Ops:
  7.2 36.7 %all-gather.5.cloned.1.call-start = ((), (), s32[]{:S(2)}) async-start(), calls=%async_computation.2 | async-start | bytes 2433024 | tf_op jit(solution)/shard_map/all_gather | solution.py:165
  10.9 33.0 %copy-start.1 = (bf16[8,512]{1,0:T(8,128)(2,1)S(1)}, bf16[8,512]{1,0:T(8,128)(2,1)}, u32[]{:S(2)}) copy-start(bf16[8,512]{1,0:T(8,128)(2,1)} %param.12) | copy-start | bytes 24580
  10.9 104.8 %all-gather.7.cloned.1.call-start = ((), (), s32[]{:S(2)}) async-start(), calls=%async_computation.3 | async-start | bytes 14598144 | tf_op jit(solution)/shard_map/all_gather | solution.py:166
  116.7 1.8 copy-start.3
  118.5 29.7 %copy-start.2 = (f32[512]{0:T(512)S(1)}, f32[512]{0:T(512)}, u32[]{:S(2)}) copy-start(f32[512]{0:T(512)} %param.10) | copy-start | bytes 6148
  149.5 23.1 %all-to-all-start = ((f32[16,33,512]{2,1,0:T(8,128)}), f32[16,33,512]{2,1,0:T(8,128)S(1)}, u32[]{:S(2)}, u32[]{:S(2)}) async-start(f32[16,33,512]{2,1,0:T(8,128)} %broadcast_in_dim.31), calls=%async_computation | async-start | bytes 2621440 | tf_op jit(solution)/shard_map/all_to_all | solution.py:188
  176.0 42.8 %copy-start = (f32[8,512]{1,0:T(8,128)S(1)}, f32[8,512]{1,0:T(8,128)}, u32[]{:S(2)}) copy-start(f32[8,512]{1,0:T(8,128)} %param.13) | copy-start | bytes 49156
  206.7 12.1 %all-to-all-start.1 = ((f32[8,16,512]{2,1,0:T(8,128)}), f32[8,16,512]{2,1,0:T(8,128)S(1)}, u32[]{:S(2)}, u32[]{:S(2)}) async-start(f32[8,16,512]{2,1,0:T(8,128)} %broadcast_in_dim.32), calls=%async_computation.1 | async-start | bytes 524288 | tf_op jit(solution)/shard_map/all_to_all | solution.py:205
Sparse Core Ops, SparseCore 0:
  11.1 32.7 all-gather.4
  45.5 70.1 all-gather.6

commit v12 on v10

--- a/solution.py
+++ b/solution.py
@@ -175,18 +175,14 @@
         row_kernel, my_ids, my_cnt, g_col, targets, x_all, rows,
         jax.ShapeDtypeStruct((blocks, 1, rows), jnp.float32), scale,
     )
-    stats = jnp.concatenate(
-        [row_top.reshape(blocks, rows), row_total.reshape(blocks, rows), log_a[None]], axis=0
-    )
-    stats_all = lax.all_to_all(
-        jnp.broadcast_to(stats[None], (blocks,) + stats.shape), "src", 0, 0, tiled=True
-    )
-    tops = stats_all[:, :blocks]
-    top = jnp.max(tops, axis=0)
-    total = jnp.sum(stats_all[:, blocks : 2 * blocks] * jnp.exp(tops - top[None]), axis=0)
-    log_a_all = stats_all[:, 2 * blocks]
-    f_all = EPSILON * log_a_all - EPSILON * (top + jnp.log(total))
-    f_new = lax.dynamic_index_in_dim(f_all, me, 0, False)
+    sent = jnp.stack([row_top.reshape(blocks, rows), row_total.reshape(blocks, rows)], axis=1)
+    got = lax.all_to_all(sent, "src", 0, 0, tiled=True)
+    top = jnp.max(got[:, 0], axis=0)
+    total = jnp.sum(got[:, 1] * jnp.exp(got[:, 0] - top[None]), axis=0)
+    f_new = EPSILON * log_a - EPSILON * (top + jnp.log(total))
+    f_all = lax.all_to_all(
+        jnp.broadcast_to(f_new[None], (blocks,) + f_new.shape), "src", 0, 0, tiled=True
+    )
 
     f_col = (f_all / EPSILON)[:, :, None]
     tile_top, tile_total = resident_call(

time: 202 us -> 191 us (0.946)
  blocking collectives: 22.6 us -> 33.2 us
  waiting for transfers between devices: 82.5 us -> 73.7 us
  starting transfers between devices: 5.75 us -> 0.04 us
  other arithmetic: 12.1 us -> 7.8 us
  local copies, waits for them, and re-layouts: 8.95 us -> 6.66 us
    all_to_all x1 -> x3, blocking collectives: 22.6 us -> 33.2 us  [the longest x1 14.5 us: local(): lax.all_to_all(jnp.broadcast_to(col[None], (loop_size,) + col.shape), 'lo...]
    all_to_all x1 -> x0, waiting for transfers between devices: 8.83 us -> none  [local(): lax.all_to_all(jnp.broadcast_to(col[None], (loop_size,) + col.shape), 'lo...]
    all_to_all x1 -> x0, starting transfers between devices: 5.71 us -> none  [local(): lax.all_to_all(jnp.broadcast_to(col[None], (loop_size,) + col.shape), 'lo...]
    div x1, other arithmetic: 4.52 us -> 0.01 us  [local(): f_col = (f_all / EPSILON)[:, :, None]]
    sub x1 -> x0, local copies, waits for them, and re-layouts: 2.65 us -> none  [local(): f_all = EPSILON * log_a_all - EPSILON * (top + jnp.log(total))]
    div x0 -> x1, local copies, waits for them, and re-layouts: none -> 2.64 us  [local(): f_col = (f_all / EPSILON)[:, :, None]]
  transfers between devices with their start and end apart: 2 -> 1, of which waited for: 2 -> 1; matrix products, arithmetic and copies ran while one was open for 2% -> 1% of each run, Pallas kernels for 0% -> 0%
where the time goes in v12:
time: 191 us; the launch traced here: 189 us
  waiting for transfers between devices  73.7 us (39%)
  Pallas kernels  53.1 us (28%)
  blocking collectives  33.2 us (17%)
  between operations  14.1 us (7%)
  other arithmetic  7.8 us (4%)
  local copies, waits for them, and re-layouts  6.66 us (3%)
    all_gather x1, waiting for transfers between devices, local(): x_all = lax.all_gather(packed, 'src')  73.7 us
    pallas_call x2, Pallas kernels, resident_call(): pl.pallas_call(kernel, out_shape=(out_shape, out_shape), in_specs=[smem,...  53.1 us
    all_to_all x1, blocking collectives, local(): lax.all_to_all(jnp.broadcast_to(col[None], (loop_size,) + col.shape), 'lo...  14.5 us
    all_to_all x1, blocking collectives, local(): got = lax.all_to_all(sent, 'src', 0, 0, tiled=True)  10 us
    all_to_all x1, blocking collectives, local(): lax.all_to_all(jnp.broadcast_to(f_new[None], (blocks,) + f_new.shape), 's...  8.66 us
  transfers between devices with their start and end apart: 1, of which 1 were waited for; matrix products, arithmetic and copies ran while one was open for 1% of the time, Pallas kernels for 0%

profile of v12, /device:TPU:0, one launch (start us, length us, event | category | flops | bytes accessed | tf_op | source)
XLA Modules:
  0.0 188.6 jit_solution(1312400368876609673)
XLA Ops:
  7.2 0.7 convert.8
  7.9 0.7 convert.9
  8.6 0.1 copy.29
  8.6 0.1 concatenate.19
  8.7 0.1 fusion.11
  8.8 2.1 %pad_maximum_fusion = bf16[528,768]{1,0:T(8,128)(2,1)} fusion(bf16[16,768]{1,0:T(8,128)(2,1)S(1)} %fusion.11, bf16[512,768]{1,0:T(8,128)(2,1)} %param.9), kind=kLoop, calls=%fused_computation | loop fusion | flops 1622016 | bytes 1622016 | tf_op jit(solution)/shard_map/concatenate | solution.py:164
  10.9 0.7 multiply_bitcast_fusion
  11.7 2.0 %copy.32.refs_3_ = f32[8,512,1]{2,1,0:T(8,128)} copy(f32[8,512,1]{1,0,2:T(8,128)S(1)} %multiply_bitcast_fusion) | data formatting | bytes 32768 | tf_op jit(solution)/shard_map/broadcast_in_dim | solution.py:173
  13.6 73.7 %all-gather.3.cloned.1.call-done = bf16[8448,768]{1,0:T(8,128)(2,1)} async-done(((bf16[528,768]{1,0:T(8,128)(2,1)}), bf16[8448,768]{1,0:T(8,128)(2,1)}) %all-gather.3.cloned.1.call-update) | async-done | bytes 12976144 | tf_op jit(solution)/shard_map/all_gather | solution.py:165
  87.3 0.8 slice_convert_fusion
  88.2 0.2 dynamic-slice_reduce_fusion.refs_1_
  88.4 0.1 copy.31
  88.5 0.6 min.14.refs_0_
  89.1 0.1 select_reduce_fusion
  89.3 1.0 sort.19
  90.3 26.2 %shard_map.86 = (f32[16,1,512]{2,1,0:T(1,128)}, f32[16,1,512]{2,1,0:T(1,128)}) custom-call(s32[32]{0:T(128)} %min.14.refs_0_, s32[16]{0:T(128)} %copy-done.3, s32[8]{0:T(128)} %get-tuple-element.19.refs_2_, f32[8,512,1]{2,1,0:T(8,128)} %copy.32.refs_3_, bf16[8,512,768]{2,1,0:T(8,128)(2,1)} %refs_4_.3, bf16[16,528,768]{2,1,0:T(8,128)(2,1)} %bitcast.33), custom_call_target="tpu_custom_call" | custom-call | flops 12884901888 | bytes 18874368 | tf_op jit(solution)/shard_map/pallas_call | solution.py:135
  116.6 0.8 pad_maximum_fusion.1
  117.4 10.0 %all_to_all.16 = f32[16,2,512]{2,1,0:T(2,128)S(1)} all-to-all(f32[16,2,512]{2,1,0:T(2,128)S(1)} %pad_maximum_fusion.1), channel_id=1, replica_groups=mesh['src'=16,'loop'=8] {'src'}, dimensions={0} | all-to-all | bytes 131072 | tf_op jit(solution)/shard_map/all_to_all | solution.py:179
  127.6 8.7 %all_to_all.17 = f32[16,1,512]{2,1,0:T(1,128)S(1)} all-to-all(f32[16,1,512]{2,1,0:T(1,128)S(1)} %broadcast_in_dim.25), channel_id=1, replica_groups=mesh['src'=16,'loop'=8] {'src'}, dimensions={0} | all-to-all | bytes 65536 | tf_op jit(solution)/shard_map/all_to_all | solution.py:183
  136.3 2.6 %copy.35.refs_3_ = f32[16,512,1]{2,1,0:T(8,128)} copy(f32[16,512,1]{1,0,2:T(8,128)S(1)} %fusion.10) | data formatting | bytes 65536 | tf_op jit(solution)/shard_map/div | solution.py:187
  138.9 26.9 %shard_map.87 = (f32[8,1,512]{2,1,0:T(1,128)}, f32[8,1,512]{2,1,0:T(1,128)}) custom-call(s32[32]{0:T(128)} %min.14.refs_0_, s32[16]{0:T(128)} %copy-done.3, s32[8]{0:T(128)} %get-tuple-element.19.refs_2_, f32[16,512,1]{2,1,0:T(8,128)} %copy.35.refs_3_, bf16[8,512,768]{2,1,0:T(8,128)(2,1)} %refs_4_.3, bf16[16,528,768]{2,1,0:T(8,128)(2,1)} %bitcast.34), custom_call_target="tpu_custom_call" | custom-call | flops 12884901888 | bytes 18874368 | tf_op jit(solution)/shard_map/pallas_call | solution.py:135
  165.8 0.7 copy_bitcast_fusion.1
  166.6 14.5 %all_to_all.18 = f32[8,16,512]{2,1,0:T(8,128)S(1)} all-to-all(f32[8,16,512]{2,1,0:T(8,128)S(1)} %broadcast_in_dim.26), channel_id=1, replica_groups=mesh['src'=16,'loop'=8] {'loop'}, dimensions={0} | all-to-all | bytes 524288 | tf_op jit(solution)/shard_map/all_to_all | solution.py:194
  181.2 0.6 multiply_subtract_fusion
  (26 shorter events, 0.5 us)
Async XLA Ops:
  7.2 80.1 %all-gather.3.cloned.1.call-start = ((), (), s32[]{:S(2)}) async-start(), calls=%async_computation.3 | async-start | bytes 13787136 | tf_op jit(solution)/shard_map/all_gather | solution.py:165
  88.4 1.9 %copy-start.3 = (s32[16]{0:T(128)}, s32[16]{0:T(128)S(1)}, u32[]{:S(2)}) copy-start(s32[16]{0:T(128)S(1)} %dynamic-slice_reduce_fusion.refs_1_) | copy-start | bytes 196
  90.3 37.2 %copy-start.2 = (f32[512]{0:T(512)S(1)}, f32[512]{0:T(512)}, u32[]{:S(2)}) copy-start(f32[512]{0:T(512)} %param.10) | copy-start | bytes 6148
  127.6 38.3 %copy-start.1 = (f32[512]{0:T(512)}, f32[512]{0:T(512)S(1)}, u32[]{:S(2)}) copy-start(f32[512]{0:T(512)S(1)} %multiply_subtract_fusion.1) | copy-start | bytes 6148
  138.9 42.3 %copy-start = (f32[8,512]{1,0:T(8,128)S(1)}, f32[8,512]{1,0:T(8,128)}, u32[]{:S(2)}) copy-start(f32[8,512]{1,0:T(8,128)} %param.13) | copy-start | bytes 49156
Sparse Core Ops, SparseCore 0:
  11.1 76.1 all-gather.2

commit v13 on v12

--- a/solution.py
+++ b/solution.py
@@ -9,6 +9,8 @@
 
 EPSILON = 0.1
 VERY_LOW = -1e30
+LOG2E = 1.0 / math.log(2.0)
+LN2 = math.log(2.0)
 NT_DIMS = (((1,), (1,)), ((), ()))
 
 
@@ -71,8 +73,8 @@
                 logits = g_ref[t] + kt * scale
                 old = top_ref[s]
                 new = jnp.maximum(old, jnp.max(logits, axis=0, keepdims=True))
-                tot_ref[s] = tot_ref[s] * jnp.exp(old - new) + jnp.sum(
-                    jnp.exp(logits - new), axis=0, keepdims=True
+                tot_ref[s] = tot_ref[s] * jnp.exp2(old - new) + jnp.sum(
+                    jnp.exp2(logits - new), axis=0, keepdims=True
                 )
                 top_ref[s] = new
 
@@ -99,8 +101,8 @@
                 logits = f_ref[s] + k * scale
                 old = top_ref[t]
                 new = jnp.maximum(old, jnp.max(logits, axis=0, keepdims=True))
-                tot_ref[t] = tot_ref[t] * jnp.exp(old - new) + jnp.sum(
-                    jnp.exp(logits - new), axis=0, keepdims=True
+                tot_ref[t] = tot_ref[t] * jnp.exp2(old - new) + jnp.sum(
+                    jnp.exp2(logits - new), axis=0, keepdims=True
                 )
                 top_ref[t] = new
 
@@ -155,7 +157,7 @@
     slots_per = tile_ids.shape[2]
     groups = tile_ids.shape[1]
     me = lax.axis_index("src")
-    scale = 1.0 / (math.sqrt(depth) * EPSILON)
+    scale = LOG2E / (math.sqrt(depth) * EPSILON)
 
     meta = jnp.concatenate([tile_ids[0].reshape(-1), live_count[0].reshape(-1)])
     meta_rows = jnp.zeros((16, depth), jnp.bfloat16).at[0, : meta.shape[0]].set(
@@ -170,7 +172,7 @@
     my_ids = jnp.clip(lax.dynamic_index_in_dim(ids_all, me, 1, False) - me * tiles_own, 0, tiles_own - 1)
     my_cnt = lax.dynamic_index_in_dim(cnt_all, me, 1, False)
 
-    g_col = (g_old.astype(jnp.float32) / EPSILON)[:, :, None]
+    g_col = (g_old.astype(jnp.float32) * (LOG2E / EPSILON))[:, :, None]
     row_top, row_total = resident_call(
         row_kernel, my_ids, my_cnt, g_col, targets, x_all, rows,
         jax.ShapeDtypeStruct((blocks, 1, rows), jnp.float32), scale,
@@ -178,13 +180,13 @@
     sent = jnp.stack([row_top.reshape(blocks, rows), row_total.reshape(blocks, rows)], axis=1)
     got = lax.all_to_all(sent, "src", 0, 0, tiled=True)
     top = jnp.max(got[:, 0], axis=0)
-    total = jnp.sum(got[:, 1] * jnp.exp(got[:, 0] - top[None]), axis=0)
-    f_new = EPSILON * log_a - EPSILON * (top + jnp.log(total))
+    total = jnp.sum(got[:, 1] * jnp.exp2(got[:, 0] - top[None]), axis=0)
+    f_new = EPSILON * log_a - EPSILON * (top * LN2 + jnp.log(total))
     f_all = lax.all_to_all(
         jnp.broadcast_to(f_new[None], (blocks,) + f_new.shape), "src", 0, 0, tiled=True
     )
 
-    f_col = (f_all / EPSILON)[:, :, None]
+    f_col = (f_all * (LOG2E / EPSILON))[:, :, None]
     tile_top, tile_total = resident_call(
         col_kernel, my_ids, my_cnt, f_col, targets, x_all, rows,
         jax.ShapeDtypeStruct((tiles_own, 1, width), jnp.float32), scale,
@@ -196,8 +198,8 @@
     )
     tops = col_all[:, :tiles_own]
     all_top = jnp.max(tops, axis=0)
-    all_total = jnp.sum(col_all[:, tiles_own:] * jnp.exp(tops - all_top[None]), axis=0)
-    g_new = EPSILON * log_b - EPSILON * (all_top + jnp.log(all_total))
+    all_total = jnp.sum(col_all[:, tiles_own:] * jnp.exp2(tops - all_top[None]), axis=0)
+    g_new = EPSILON * log_b - EPSILON * (all_top * LN2 + jnp.log(all_total))
     return (f_new, g_new)
 
 

time: 191 us -> 191 us (level)
    div x1 -> x0, local copies, waits for them, and re-layouts: 2.64 us -> none  [local(): f_col = (f_all / EPSILON)[:, :, None]]
    mul x0 -> x1, local copies, waits for them, and re-layouts: none -> 2.64 us  [local(): f_col = (f_all * (LOG2E / EPSILON))[:, :, None]]
where the time goes in v13:
time: 191 us; the launch traced here: 190 us
  waiting for transfers between devices  73.7 us (39%)
  Pallas kernels  53.8 us (28%)
  blocking collectives  33.6 us (18%)
  between operations  14.1 us (7%)
  other arithmetic  7.81 us (4%)
  local copies, waits for them, and re-layouts  6.66 us (3%)
    all_gather x1, waiting for transfers between devices, local(): x_all = lax.all_gather(packed, 'src')  73.7 us
    pallas_call x2, Pallas kernels, resident_call(): pl.pallas_call(kernel, out_shape=(out_shape, out_shape), in_specs=[smem,...  53.8 us
    all_to_all x1, blocking collectives, local(): lax.all_to_all(jnp.broadcast_to(col[None], (loop_size,) + col.shape), 'lo...  14.7 us
    all_to_all x1, blocking collectives, local(): got = lax.all_to_all(sent, 'src', 0, 0, tiled=True)  10.2 us
    all_to_all x1, blocking collectives, local(): lax.all_to_all(jnp.broadcast_to(f_new[None], (blocks,) + f_new.shape), 's...  8.66 us
  transfers between devices with their start and end apart: 1, of which 1 were waited for; matrix products, arithmetic and copies ran while one was open for 1% of the time, Pallas kernels for 0%

profile of v13, /device:TPU:0, one launch (start us, length us, event | category | flops | bytes accessed | tf_op | source)
XLA Modules:
  0.0 189.6 jit_solution(13945538780175121093)
XLA Ops:
  7.2 0.7 convert.8
  7.9 0.7 convert.9
  8.6 0.1 copy.29
  8.6 0.1 concatenate.19
  8.7 0.1 fusion.12
  8.8 2.1 %pad_maximum_fusion = bf16[528,768]{1,0:T(8,128)(2,1)} fusion(bf16[16,768]{1,0:T(8,128)(2,1)S(1)} %fusion.12, bf16[512,768]{1,0:T(8,128)(2,1)} %param.9), kind=kLoop, calls=%fused_computation | loop fusion | flops 1622016 | bytes 1622016 | tf_op jit(solution)/shard_map/concatenate | solution.py:166
  10.9 0.7 multiply_bitcast_fusion
  11.7 2.0 %copy.32.refs_3_ = f32[8,512,1]{2,1,0:T(8,128)} copy(f32[8,512,1]{1,0,2:T(8,128)S(1)} %multiply_bitcast_fusion) | data formatting | bytes 32768 | tf_op jit(solution)/shard_map/broadcast_in_dim | solution.py:175
  13.6 73.7 %all-gather.3.cloned.1.call-done = bf16[8448,768]{1,0:T(8,128)(2,1)} async-done(((bf16[528,768]{1,0:T(8,128)(2,1)}), bf16[8448,768]{1,0:T(8,128)(2,1)}) %all-gather.3.cloned.1.call-update) | async-done | bytes 12976144 | tf_op jit(solution)/shard_map/all_gather | solution.py:167
  87.3 0.8 slice_convert_fusion
  88.2 0.2 dynamic-slice_reduce_fusion.refs_1_
  88.4 0.1 copy.31
  88.5 0.6 min.14.refs_0_
  89.1 0.1 select_reduce_fusion
  89.3 1.0 sort.19
  90.3 26.6 %shard_map.86 = (f32[16,1,512]{2,1,0:T(1,128)}, f32[16,1,512]{2,1,0:T(1,128)}) custom-call(s32[32]{0:T(128)} %min.14.refs_0_, s32[16]{0:T(128)} %copy-done.3, s32[8]{0:T(128)} %get-tuple-element.19.refs_2_, f32[8,512,1]{2,1,0:T(8,128)} %copy.32.refs_3_, bf16[8,512,768]{2,1,0:T(8,128)(2,1)} %refs_4_.3, bf16[16,528,768]{2,1,0:T(8,128)(2,1)} %bitcast.35), custom_call_target="tpu_custom_call" | custom-call | flops 12884901888 | bytes 18874368 | tf_op jit(solution)/shard_map/pallas_call | solution.py:137
  116.9 0.8 pad_maximum_fusion.1
  117.7 10.2 %all_to_all.16 = f32[16,2,512]{2,1,0:T(2,128)S(1)} all-to-all(f32[16,2,512]{2,1,0:T(2,128)S(1)} %pad_maximum_fusion.1), channel_id=1, replica_groups=mesh['src'=16,'loop'=8] {'src'}, dimensions={0} | all-to-all | bytes 131072 | tf_op jit(solution)/shard_map/all_to_all | solution.py:181
  128.1 8.7 %all_to_all.17 = f32[16,1,512]{2,1,0:T(1,128)S(1)} all-to-all(f32[16,1,512]{2,1,0:T(1,128)S(1)} %broadcast_in_dim.25), channel_id=1, replica_groups=mesh['src'=16,'loop'=8] {'src'}, dimensions={0} | all-to-all | bytes 65536 | tf_op jit(solution)/shard_map/all_to_all | solution.py:185
  136.8 2.6 %copy.35.refs_3_ = f32[16,512,1]{2,1,0:T(8,128)} copy(f32[16,512,1]{1,0,2:T(8,128)S(1)} %fusion.11) | data formatting | bytes 65536 | tf_op jit(solution)/shard_map/mul | solution.py:189
  139.4 27.2 %shard_map.87 = (f32[8,1,512]{2,1,0:T(1,128)}, f32[8,1,512]{2,1,0:T(1,128)}) custom-call(s32[32]{0:T(128)} %min.14.refs_0_, s32[16]{0:T(128)} %copy-done.3, s32[8]{0:T(128)} %get-tuple-element.19.refs_2_, f32[16,512,1]{2,1,0:T(8,128)} %copy.35.refs_3_, bf16[8,512,768]{2,1,0:T(8,128)(2,1)} %refs_4_.3, bf16[16,528,768]{2,1,0:T(8,128)(2,1)} %bitcast.36), custom_call_target="tpu_custom_call" | custom-call | flops 12884901888 | bytes 18874368 | tf_op jit(solution)/shard_map/pallas_call | solution.py:137
  166.6 0.7 copy_bitcast_fusion.1
  167.4 14.7 %all_to_all.18 = f32[8,16,512]{2,1,0:T(8,128)S(1)} all-to-all(f32[8,16,512]{2,1,0:T(8,128)S(1)} %broadcast_in_dim.26), channel_id=1, replica_groups=mesh['src'=16,'loop'=8] {'loop'}, dimensions={0} | all-to-all | bytes 524288 | tf_op jit(solution)/shard_map/all_to_all | solution.py:196
  182.2 0.6 multiply_subtract_fusion
  (26 shorter events, 0.5 us)
Async XLA Ops:
  7.2 80.1 %all-gather.3.cloned.1.call-start = ((), (), s32[]{:S(2)}) async-start(), calls=%async_computation.3 | async-start | bytes 13787136 | tf_op jit(solution)/shard_map/all_gather | solution.py:167
  88.4 1.9 %copy-start.3 = (s32[16]{0:T(128)}, s32[16]{0:T(128)S(1)}, u32[]{:S(2)}) copy-start(s32[16]{0:T(128)S(1)} %dynamic-slice_reduce_fusion.refs_1_) | copy-start | bytes 196
  90.3 37.7 %copy-start.2 = (f32[512]{0:T(512)S(1)}, f32[512]{0:T(512)}, u32[]{:S(2)}) copy-start(f32[512]{0:T(512)} %param.10) | copy-start | bytes 6148
  128.1 38.6 %copy-start.1 = (f32[512]{0:T(512)}, f32[512]{0:T(512)S(1)}, u32[]{:S(2)}) copy-start(f32[512]{0:T(512)S(1)} %multiply_subtract_fusion.1) | copy-start | bytes 6148
  139.4 42.8 %copy-start = (f32[8,512]{1,0:T(8,128)S(1)}, f32[8,512]{1,0:T(8,128)}, u32[]{:S(2)}) copy-start(f32[8,512]{1,0:T(8,128)} %param.13) | copy-start | bytes 49156
Sparse Core Ops, SparseCore 0:
  11.1 76.1 all-gather.2

commit v14 on v12

--- a/solution.py
+++ b/solution.py
@@ -158,13 +158,11 @@
     scale = 1.0 / (math.sqrt(depth) * EPSILON)
 
     meta = jnp.concatenate([tile_ids[0].reshape(-1), live_count[0].reshape(-1)])
-    meta_rows = jnp.zeros((16, depth), jnp.bfloat16).at[0, : meta.shape[0]].set(
-        meta.astype(jnp.bfloat16)
-    )
-    packed = jnp.concatenate([sources, meta_rows], axis=0)
-    x_all = lax.all_gather(packed, "src")
-    meta_all = x_all[:, rows, : meta.shape[0]].astype(jnp.int32)
+    x_all = lax.all_gather(sources, "src")
     blocks = x_all.shape[0]
+    meta_all = lax.all_to_all(
+        jnp.broadcast_to(meta[None], (blocks,) + meta.shape), "src", 0, 0, tiled=True
+    )
     ids_all = meta_all[:, : groups * slots_per].reshape(blocks, groups, slots_per)
     cnt_all = meta_all[:, groups * slots_per :]
     my_ids = jnp.clip(lax.dynamic_index_in_dim(ids_all, me, 1, False) - me * tiles_own, 0, tiles_own - 1)

time: 191 us -> 185 us (0.969)
  waiting for transfers between devices: 73.7 us -> 63.4 us
  starting transfers between devices: 0.04 us -> 6.49 us
  other arithmetic: 7.8 us -> 4.21 us
    all_gather x1, waiting for transfers between devices: 73.7 us -> 59.5 us  [local(): x_all = lax.all_gather(sources, 'src')]
    all_to_all x0 -> x1, starting transfers between devices: none -> 6.46 us  [local(): lax.all_to_all(jnp.broadcast_to(meta[None], (blocks,) + meta.shape), 'src...]
    all_to_all x0 -> x1, waiting for transfers between devices: none -> 3.29 us  [local(): lax.all_to_all(jnp.broadcast_to(meta[None], (blocks,) + meta.shape), 'src...]
    concatenate x1 -> x0, other arithmetic: 2.1 us -> none  [local(): packed = jnp.concatenate([sources, meta_rows], axis=0)]
    all_to_all x1, blocking collectives: 14.5 us -> 12.4 us  [local(): lax.all_to_all(jnp.broadcast_to(col[None], (loop_size,) + col.shape), 'lo...]
  transfers between devices with their start and end apart: 1 -> 2, of which waited for: 1 -> 2; matrix products, arithmetic and copies ran while one was open for 1% -> 4% of each run, Pallas kernels for 0% -> 0%
where the time goes in v14:
time: 185 us; the launch traced here: 184 us
  waiting for transfers between devices  63.4 us (34%)
  Pallas kernels  54.7 us (30%)
  blocking collectives  32.8 us (18%)
  between operations  14.1 us (8%)
  local copies, waits for them, and re-layouts  7.76 us (4%)
  starting transfers between devices  6.49 us (4%)
  other arithmetic  4.21 us (2%)
    all_gather x1, waiting for transfers between devices, local(): x_all = lax.all_gather(sources, 'src')  59.5 us
    pallas_call x2, Pallas kernels, resident_call(): pl.pallas_call(kernel, out_shape=(out_shape, out_shape), in_specs=[smem,...  54.7 us
    all_to_all x1, blocking collectives, local(): lax.all_to_all(jnp.broadcast_to(col[None], (loop_size,) + col.shape), 'lo...  12.4 us
    all_to_all x1, blocking collectives, local(): got = lax.all_to_all(sent, 'src', 0, 0, tiled=True)  11.7 us
    all_to_all x1, blocking collectives, local(): lax.all_to_all(jnp.broadcast_to(f_new[None], (blocks,) + f_new.shape), 's...  8.66 us
    all_to_all x1, starting transfers between devices, local(): lax.all_to_all(jnp.broadcast_to(meta[None], (blocks,) + meta.shape), 'src...  6.46 us
  transfers between devices with their start and end apart: 2, of which 2 were waited for; matrix products, arithmetic and copies ran while one was open for 4% of the time, Pallas kernels for 0%

profile of v14, /device:TPU:0, one launch (start us, length us, event | category | flops | bytes accessed | tf_op | source)
XLA Modules:
  0.0 183.5 jit_solution(5807301248999301806)
XLA Ops:
  7.2 0.7 all-gather.3.cloned.1.call-update
  7.9 0.8 copy.35
  8.7 0.1 reshape_squeeze.3
  8.7 0.7 pad_add_fusion
  9.5 0.6 broadcast_in_dim.24
  10.1 6.5 %all-to-all-start = ((s32[16,1,48]{2,1,0:T(1,128)}), s32[16,1,48]{2,1,0:T(1,128)S(1)}, u32[]{:S(2)}, u32[]{:S(2)}) async-start(s32[16,1,48]{2,1,0:T(1,128)} %broadcast_in_dim.24), calls=%async_computation | async-start | bytes 16384 | tf_op jit(solution)/shard_map/all_to_all | solution.py:163
  16.5 0.7 multiply_bitcast_fusion
  17.3 2.0 %copy.38.refs_3_ = f32[8,512,1]{2,1,0:T(8,128)} copy(f32[8,512,1]{1,0,2:T(8,128)S(1)} %multiply_bitcast_fusion) | data formatting | bytes 32768 | tf_op jit(solution)/shard_map/broadcast_in_dim | solution.py:171
  19.3 3.3 %all-to-all-done = s32[16,1,48]{2,1,0:T(1,128)S(1)} async-done(((s32[16,1,48]{2,1,0:T(1,128)}), s32[16,1,48]{2,1,0:T(1,128)S(1)}, u32[]{:S(2)}, u32[]{:S(2)}) %all-to-all-start) | async-done | bytes 3104 | tf_op jit(solution)/shard_map/all_to_all | solution.py:163
  22.6 0.1 copy.36
  22.7 0.1 copy.37
  22.7 0.7 min.14.refs_0_
  23.5 0.1 select_reduce_fusion
  23.6 1.0 sort.19
  24.6 59.5 %all-gather.3.cloned.1.call-done = bf16[8192,768]{1,0:T(8,128)(2,1)} async-done(((bf16[512,768]{1,0:T(8,128)(2,1)}), bf16[8192,768]{1,0:T(8,128)(2,1)}) %all-gather.3.cloned.1.call-update) | async-done | bytes 12582928 | tf_op jit(solution)/shard_map/all_gather | solution.py:161
  84.0 27.0 %shard_map.86 = (f32[16,1,512]{2,1,0:T(1,128)}, f32[16,1,512]{2,1,0:T(1,128)}) custom-call(s32[32]{0:T(128)} %min.14.refs_0_, s32[16]{0:T(128)} %copy-done.3, s32[8]{0:T(128)} %get-tuple-element.7.refs_2_, f32[8,512,1]{2,1,0:T(8,128)} %copy.38.refs_3_, bf16[8,512,768]{2,1,0:T(8,128)(2,1)} %refs_4_.3, bf16[16,512,768]{2,1,0:T(8,128)(2,1)} %bitcast.34), custom_call_target="tpu_custom_call" | custom-call | flops 12884901888 | bytes 18874368 | tf_op jit(solution)/shard_map/pallas_call | solution.py:135
  111.1 0.8 pad_maximum_fusion
  111.9 11.7 %all_to_all.25 = f32[16,2,512]{2,1,0:T(2,128)S(1)} all-to-all(f32[16,2,512]{2,1,0:T(2,128)S(1)} %pad_maximum_fusion), channel_id=1, replica_groups=mesh['src'=16,'loop'=8] {'src'}, dimensions={0} | all-to-all | bytes 131072 | tf_op jit(solution)/shard_map/all_to_all | solution.py:177
  123.7 8.7 %all_to_all.26 = f32[16,1,512]{2,1,0:T(1,128)S(1)} all-to-all(f32[16,1,512]{2,1,0:T(1,128)S(1)} %broadcast_in_dim.28), channel_id=1, replica_groups=mesh['src'=16,'loop'=8] {'src'}, dimensions={0} | all-to-all | bytes 65536 | tf_op jit(solution)/shard_map/all_to_all | solution.py:181
  132.4 2.6 %copy.41.refs_3_ = f32[16,512,1]{2,1,0:T(8,128)} copy(f32[16,512,1]{1,0,2:T(8,128)S(1)} %fusion.5) | data formatting | bytes 65536 | tf_op jit(solution)/shard_map/div | solution.py:185
  135.0 27.7 %shard_map.87 = (f32[8,1,512]{2,1,0:T(1,128)}, f32[8,1,512]{2,1,0:T(1,128)}) custom-call(s32[32]{0:T(128)} %min.14.refs_0_, s32[16]{0:T(128)} %copy-done.3, s32[8]{0:T(128)} %get-tuple-element.7.refs_2_, f32[16,512,1]{2,1,0:T(8,128)} %copy.41.refs_3_, bf16[8,512,768]{2,1,0:T(8,128)(2,1)} %refs_4_.3, bf16[16,512,768]{2,1,0:T(8,128)(2,1)} %bitcast.35), custom_call_target="tpu_custom_call" | custom-call | flops 12884901888 | bytes 18874368 | tf_op jit(solution)/shard_map/pallas_call | solution.py:135
  162.8 0.7 copy_bitcast_fusion.1
  163.5 12.4 %all_to_all.27 = f32[8,16,512]{2,1,0:T(8,128)S(1)} all-to-all(f32[8,16,512]{2,1,0:T(8,128)S(1)} %broadcast_in_dim.29), channel_id=1, replica_groups=mesh['src'=16,'loop'=8] {'loop'}, dimensions={0} | all-to-all | bytes 524288 | tf_op jit(solution)/shard_map/all_to_all | solution.py:192
  176.0 0.6 multiply_subtract_fusion
  (26 shorter events, 0.3 us)
Async XLA Ops:
  7.2 76.9 %all-gather.3.cloned.1.call-start = ((), (), s32[]{:S(2)}) async-start(), calls=%async_computation.4 | async-start | bytes 13369344 | tf_op jit(solution)/shard_map/all_gather | solution.py:161
  10.1 12.5 %all-to-all-start = ((s32[16,1,48]{2,1,0:T(1,128)}), s32[16,1,48]{2,1,0:T(1,128)S(1)}, u32[]{:S(2)}, u32[]{:S(2)}) async-start(s32[16,1,48]{2,1,0:T(1,128)} %broadcast_in_dim.24), calls=%async_computation | async-start | bytes 16384 | tf_op jit(solution)/shard_map/all_to_all | solution.py:163
  23.4 60.6 %copy-start.3 = (s32[16]{0:T(128)}, s32[16]{0:T(128)S(1)}, u32[]{:S(2)}) copy-start(s32[16]{0:T(128)S(1)} %dynamic-slice_bitcast_fusion.refs_1_) | copy-start | bytes 196
  84.0 39.6 %copy-start.2 = (f32[512]{0:T(512)S(1)}, f32[512]{0:T(512)}, u32[]{:S(2)}) copy-start(f32[512]{0:T(512)} %param.8) | copy-start | bytes 6148
  123.7 39.1 %copy-start.1 = (f32[512]{0:T(512)}, f32[512]{0:T(512)S(1)}, u32[]{:S(2)}) copy-start(f32[512]{0:T(512)S(1)} %multiply_subtract_fusion.1) | copy-start | bytes 6148
  135.0 41.0 %copy-start = (f32[8,512]{1,0:T(8,128)S(1)}, f32[8,512]{1,0:T(8,128)}, u32[]{:S(2)}) copy-start(f32[8,512]{1,0:T(8,128)} %param.11) | copy-start | bytes 49156
Sparse Core Ops, SparseCore 0:
  9.7 74.3 all-gather.2

commit v15 on v14

--- a/solution.py
+++ b/solution.py
@@ -89,6 +89,8 @@
 
     def step(s, carry):
         arrive(s)
+        f_row = f_ref[s]
+        f_column = jnp.transpose(jnp.broadcast_to(f_row, (128, f_row.shape[1])))[:, :1]
         for c in range(slots):
 
             @pl.when(c < cnt_ref[s])
@@ -96,7 +98,7 @@
                 t = ids_ref[s * slots + c]
                 need(t)
                 k = lax.dot_general(x_vmem[s], t_vmem[t], NT_DIMS, preferred_element_type=jnp.float32)
-                logits = f_ref[s] + k * scale
+                logits = f_column + k * scale
                 old = top_ref[t]
                 new = jnp.maximum(old, jnp.max(logits, axis=0, keepdims=True))
                 tot_ref[t] = tot_ref[t] * jnp.exp(old - new) + jnp.sum(
@@ -182,7 +184,7 @@
         jnp.broadcast_to(f_new[None], (blocks,) + f_new.shape), "src", 0, 0, tiled=True
     )
 
-    f_col = (f_all / EPSILON)[:, :, None]
+    f_col = (f_all / EPSILON)[:, None, :]
     tile_top, tile_total = resident_call(
         col_kernel, my_ids, my_cnt, f_col, targets, x_all, rows,
         jax.ShapeDtypeStruct((tiles_own, 1, width), jnp.float32), scale,

time: 185 us -> 184 us (level)
  local copies, waits for them, and re-layouts: 7.76 us -> 5.11 us
    div x1 -> x0, local copies, waits for them, and re-layouts: 2.65 us -> none  [local(): f_col = (f_all / EPSILON)[:, :, None]]
    all_to_all x1, blocking collectives: 12.4 us -> 14.9 us  [local(): lax.all_to_all(jnp.broadcast_to(col[None], (loop_size,) + col.shape), 'lo...]
    all_to_all x1, blocking collectives: 11.7 us -> 9.42 us  [local(): got = lax.all_to_all(sent, 'src', 0, 0, tiled=True)]
where the time goes in v15:
time: 184 us; the launch traced here: 182 us
  waiting for transfers between devices  63.4 us (34%)
  Pallas kernels  55.2 us (30%)
  blocking collectives  33 us (18%)
  between operations  14.1 us (8%)
  starting transfers between devices  6.49 us (4%)
  local copies, waits for them, and re-layouts  5.11 us (3%)
  other arithmetic  4.88 us (3%)
    all_gather x1, waiting for transfers between devices, local(): x_all = lax.all_gather(sources, 'src')  59.4 us
    pallas_call x2, Pallas kernels, resident_call(): pl.pallas_call(kernel, out_shape=(out_shape, out_shape), in_specs=[smem,...  55.2 us
    all_to_all x1, blocking collectives, local(): lax.all_to_all(jnp.broadcast_to(col[None], (loop_size,) + col.shape), 'lo...  14.9 us
    all_to_all x1, blocking collectives, local(): got = lax.all_to_all(sent, 'src', 0, 0, tiled=True)  9.42 us
    all_to_all x1, blocking collectives, local(): lax.all_to_all(jnp.broadcast_to(f_new[None], (blocks,) + f_new.shape), 's...  8.66 us
    all_to_all x1, starting transfers between devices, local(): lax.all_to_all(jnp.broadcast_to(meta[None], (blocks,) + meta.shape), 'src...  6.46 us
  transfers between devices with their start and end apart: 2, of which 2 were waited for; matrix products, arithmetic and copies ran while one was open for 4% of the time, Pallas kernels for 0%

profile of v15, /device:TPU:0, one launch (start us, length us, event | category | flops | bytes accessed | tf_op | source)
XLA Modules:
  0.0 182.2 jit_solution(11569198243491617418)
XLA Ops:
  7.2 0.7 all-gather.3.cloned.1.call-update
  7.9 0.8 copy.30
  8.7 0.1 reshape_squeeze.3
  8.7 0.7 pad_add_fusion
  9.5 0.6 broadcast_in_dim.24
  10.1 6.5 %all-to-all-start = ((s32[16,1,48]{2,1,0:T(1,128)}), s32[16,1,48]{2,1,0:T(1,128)S(1)}, u32[]{:S(2)}, u32[]{:S(2)}) async-start(s32[16,1,48]{2,1,0:T(1,128)} %broadcast_in_dim.24), calls=%async_computation | async-start | bytes 16384 | tf_op jit(solution)/shard_map/all_to_all | solution.py:165
  16.5 0.7 multiply_bitcast_fusion
  17.3 2.0 %copy.33.refs_3_ = f32[8,512,1]{2,1,0:T(8,128)} copy(f32[8,512,1]{1,0,2:T(8,128)S(1)} %multiply_bitcast_fusion) | data formatting | bytes 32768 | tf_op jit(solution)/shard_map/broadcast_in_dim | solution.py:173
  19.3 3.3 %all-to-all-done = s32[16,1,48]{2,1,0:T(1,128)S(1)} async-done(((s32[16,1,48]{2,1,0:T(1,128)}), s32[16,1,48]{2,1,0:T(1,128)S(1)}, u32[]{:S(2)}, u32[]{:S(2)}) %all-to-all-start) | async-done | bytes 3104 | tf_op jit(solution)/shard_map/all_to_all | solution.py:165
  22.6 0.1 copy.31
  22.7 0.1 copy.32
  22.7 0.7 min.14.refs_0_
  23.5 0.1 select_reduce_fusion
  23.6 1.0 sort.19
  24.6 59.4 %all-gather.3.cloned.1.call-done = bf16[8192,768]{1,0:T(8,128)(2,1)} async-done(((bf16[512,768]{1,0:T(8,128)(2,1)}), bf16[8192,768]{1,0:T(8,128)(2,1)}) %all-gather.3.cloned.1.call-update) | async-done | bytes 12582928 | tf_op jit(solution)/shard_map/all_gather | solution.py:163
  84.0 27.0 %shard_map.86 = (f32[16,1,512]{2,1,0:T(1,128)}, f32[16,1,512]{2,1,0:T(1,128)}) custom-call(s32[32]{0:T(128)} %min.14.refs_0_, s32[16]{0:T(128)} %copy-done.3, s32[8]{0:T(128)} %get-tuple-element.7.refs_2_, f32[8,512,1]{2,1,0:T(8,128)} %copy.33.refs_3_, bf16[8,512,768]{2,1,0:T(8,128)(2,1)} %refs_4_.3, bf16[16,512,768]{2,1,0:T(8,128)(2,1)} %bitcast.32), custom_call_target="tpu_custom_call" | custom-call | flops 12884901888 | bytes 18874368 | tf_op jit(solution)/shard_map/pallas_call | solution.py:137
  111.1 0.8 pad_maximum_fusion
  111.9 9.4 %all_to_all.25 = f32[16,2,512]{2,1,0:T(2,128)S(1)} all-to-all(f32[16,2,512]{2,1,0:T(2,128)S(1)} %pad_maximum_fusion), channel_id=1, replica_groups=mesh['src'=16,'loop'=8] {'src'}, dimensions={0} | all-to-all | bytes 131072 | tf_op jit(solution)/shard_map/all_to_all | solution.py:179
  121.5 8.7 %all_to_all.26 = f32[16,1,512]{2,1,0:T(1,128)S(1)} all-to-all(f32[16,1,512]{2,1,0:T(1,128)S(1)} %broadcast_in_dim.28), channel_id=1, replica_groups=mesh['src'=16,'loop'=8] {'src'}, dimensions={0} | all-to-all | bytes 65536 | tf_op jit(solution)/shard_map/all_to_all | solution.py:183
  130.2 0.6 broadcast_multiply_fusion.refs_3_
  130.8 28.2 %shard_map.87 = (f32[8,1,512]{2,1,0:T(1,128)}, f32[8,1,512]{2,1,0:T(1,128)}) custom-call(s32[32]{0:T(128)} %min.14.refs_0_, s32[16]{0:T(128)} %copy-done.3, s32[8]{0:T(128)} %get-tuple-element.7.refs_2_, f32[16,1,512]{2,1,0:T(1,128)} %broadcast_multiply_fusion.refs_3_, bf16[8,512,768]{2,1,0:T(8,128)(2,1)} %refs_4_.3, bf16[16,512,768]{2,1,0:T(8,128)(2,1)} %bitcast.33), custom_call_target="tpu_custom_call" | custom-call | flops 12884901888 | bytes 18874368 | tf_op jit(solution)/shard_map/pallas_call | solution.py:137
  159.0 0.7 copy_bitcast_fusion.1
  159.8 14.9 %all_to_all.27 = f32[8,16,512]{2,1,0:T(8,128)S(1)} all-to-all(f32[8,16,512]{2,1,0:T(8,128)S(1)} %broadcast_in_dim.29), channel_id=1, replica_groups=mesh['src'=16,'loop'=8] {'loop'}, dimensions={0} | all-to-all | bytes 524288 | tf_op jit(solution)/shard_map/all_to_all | solution.py:194
  174.7 0.6 multiply_subtract_fusion
  (25 shorter events, 0.3 us)
Async XLA Ops:
  7.2 76.9 %all-gather.3.cloned.1.call-start = ((), (), s32[]{:S(2)}) async-start(), calls=%async_computation.4 | async-start | bytes 13369344 | tf_op jit(solution)/shard_map/all_gather | solution.py:163
  10.1 12.5 %all-to-all-start = ((s32[16,1,48]{2,1,0:T(1,128)}), s32[16,1,48]{2,1,0:T(1,128)S(1)}, u32[]{:S(2)}, u32[]{:S(2)}) async-start(s32[16,1,48]{2,1,0:T(1,128)} %broadcast_in_dim.24), calls=%async_computation | async-start | bytes 16384 | tf_op jit(solution)/shard_map/all_to_all | solution.py:165
  23.4 60.6 %copy-start.3 = (s32[16]{0:T(128)}, s32[16]{0:T(128)S(1)}, u32[]{:S(2)}) copy-start(s32[16]{0:T(128)S(1)} %dynamic-slice_bitcast_fusion.refs_1_) | copy-start | bytes 196
  84.0 37.4 %copy-start.2 = (f32[512]{0:T(512)S(1)}, f32[512]{0:T(512)}, u32[]{:S(2)}) copy-start(f32[512]{0:T(512)} %param.8) | copy-start | bytes 6148
  121.5 37.5 %copy-start.1 = (f32[512]{0:T(512)}, f32[512]{0:T(512)S(1)}, u32[]{:S(2)}) copy-start(f32[512]{0:T(512)S(1)} %multiply_subtract_fusion.1) | copy-start | bytes 6148
  130.8 43.9 %copy-start = (f32[8,512]{1,0:T(8,128)S(1)}, f32[8,512]{1,0:T(8,128)}, u32[]{:S(2)}) copy-start(f32[8,512]{1,0:T(8,128)} %param.11) | copy-start | bytes 49156
Sparse Core Ops, SparseCore 0:
  9.7 74.3 all-gather.2

commit v16 on v15

--- a/solution.py
+++ b/solution.py
@@ -25,7 +25,7 @@
     for t in range(tiles):
         flags[t] = 0
     issue = [("x", 0), ("t", 0), ("t", 1), ("x", 1), ("t", 2), ("x", 2), ("t", 3), ("x", 3)]
-    issue = [item for item in issue if item[1] < (blocks if item[0] == "x" else tiles)]
+    issue = [item for item in issue if item[1] < (min(window, blocks) if item[0] == "x" else tiles)]
     issue += [("x", s) for s in range(4, min(window, blocks))]
     issue += [("t", k) for k in range(4, tiles)]
     for kind, k in issue:
@@ -133,7 +133,7 @@
         transcendentals=blocks * slots * rows * width,
         bytes_accessed=2 * (targets.size + blocks * rows * depth),
     )
-    kernel = lambda *refs: body(*refs, scale=scale, slots=slots, window=4)
+    kernel = lambda *refs: body(*refs, scale=scale, slots=slots, window=2)
     return pl.pallas_call(
         kernel,
         out_shape=(out_shape, out_shape),

time: 184 us -> 184 us (level); the launches traced: 182 us -> 184 us
  blocking collectives: 33 us -> 38.6 us
  Pallas kernels: 55.2 us -> 51.4 us
    pallas_call x2, Pallas kernels: 55.2 us -> 51.4 us  [resident_call(): pl.pallas_call(kernel, out_shape=(out_shape, out_shape), in_specs=[smem,...]
    all_to_all x1, blocking collectives: 14.9 us -> 18.2 us  [local(): lax.all_to_all(jnp.broadcast_to(col[None], (loop_size,) + col.shape), 'lo...]
    all_to_all x1, blocking collectives: 9.42 us -> 11.8 us  [local(): got = lax.all_to_all(sent, 'src', 0, 0, tiled=True)]
where the time goes in v16:
time: 184 us
  waiting for transfers between devices  63.4 us (34%)
  Pallas kernels  51.4 us (28%)
  blocking collectives  38.6 us (21%)
  between operations  14.1 us (8%)
  starting transfers between devices  6.49 us (4%)
  local copies, waits for them, and re-layouts  5.11 us (3%)
  other arithmetic  4.88 us (3%)
    all_gather x1, waiting for transfers between devices, local(): x_all = lax.all_gather(sources, 'src')  59.4 us
    pallas_call x2, Pallas kernels, resident_call(): pl.pallas_call(kernel, out_shape=(out_shape, out_shape), in_specs=[smem,...  51.4 us
    all_to_all x1, blocking collectives, local(): lax.all_to_all(jnp.broadcast_to(col[None], (loop_size,) + col.shape), 'lo...  18.2 us
    all_to_all x1, blocking collectives, local(): got = lax.all_to_all(sent, 'src', 0, 0, tiled=True)  11.8 us
    all_to_all x1, blocking collectives, local(): lax.all_to_all(jnp.broadcast_to(f_new[None], (blocks,) + f_new.shape), 's...  8.66 us
    all_to_all x1, starting transfers between devices, local(): lax.all_to_all(jnp.broadcast_to(meta[None], (blocks,) + meta.shape), 'src...  6.46 us
  transfers between devices with their start and end apart: 2, of which 2 were waited for; matrix products, arithmetic and copies ran while one was open for 4% of the time, Pallas kernels for 0%

profile of v16, /device:TPU:0, one launch (start us, length us, event | category | flops | bytes accessed | tf_op | source)
XLA Modules:
  0.0 184.1 jit_solution(4722373971353628462)
XLA Ops:
  7.2 0.7 all-gather.3.cloned.1.call-update
  7.9 0.8 copy.30
  8.7 0.1 reshape_squeeze.3
  8.7 0.7 pad_add_fusion
  9.5 0.6 broadcast_in_dim.24
  10.1 6.5 %all-to-all-start = ((s32[16,1,48]{2,1,0:T(1,128)}), s32[16,1,48]{2,1,0:T(1,128)S(1)}, u32[]{:S(2)}, u32[]{:S(2)}) async-start(s32[16,1,48]{2,1,0:T(1,128)} %broadcast_in_dim.24), calls=%async_computation | async-start | bytes 16384 | tf_op jit(solution)/shard_map/all_to_all | solution.py:165
  16.5 0.7 multiply_bitcast_fusion
  17.3 2.0 %copy.33.refs_3_ = f32[8,512,1]{2,1,0:T(8,128)} copy(f32[8,512,1]{1,0,2:T(8,128)S(1)} %multiply_bitcast_fusion) | data formatting | bytes 32768 | tf_op jit(solution)/shard_map/broadcast_in_dim | solution.py:173
  19.3 3.3 %all-to-all-done = s32[16,1,48]{2,1,0:T(1,128)S(1)} async-done(((s32[16,1,48]{2,1,0:T(1,128)}), s32[16,1,48]{2,1,0:T(1,128)S(1)}, u32[]{:S(2)}, u32[]{:S(2)}) %all-to-all-start) | async-done | bytes 3104 | tf_op jit(solution)/shard_map/all_to_all | solution.py:165
  22.6 0.1 copy.31
  22.7 0.1 copy.32
  22.7 0.7 min.14.refs_0_
  23.5 0.1 select_reduce_fusion
  23.6 1.0 sort.19
  24.6 59.4 %all-gather.3.cloned.1.call-done = bf16[8192,768]{1,0:T(8,128)(2,1)} async-done(((bf16[512,768]{1,0:T(8,128)(2,1)}), bf16[8192,768]{1,0:T(8,128)(2,1)}) %all-gather.3.cloned.1.call-update) | async-done | bytes 12582928 | tf_op jit(solution)/shard_map/all_gather | solution.py:163
  84.0 25.1 %shard_map.86 = (f32[16,1,512]{2,1,0:T(1,128)}, f32[16,1,512]{2,1,0:T(1,128)}) custom-call(s32[32]{0:T(128)} %min.14.refs_0_, s32[16]{0:T(128)} %copy-done.3, s32[8]{0:T(128)} %get-tuple-element.7.refs_2_, f32[8,512,1]{2,1,0:T(8,128)} %copy.33.refs_3_, bf16[8,512,768]{2,1,0:T(8,128)(2,1)} %refs_4_.3, bf16[16,512,768]{2,1,0:T(8,128)(2,1)} %bitcast.32), custom_call_target="tpu_custom_call" | custom-call | flops 12884901888 | bytes 18874368 | tf_op jit(solution)/shard_map/pallas_call | solution.py:137
  109.2 0.8 pad_maximum_fusion
  110.0 11.8 %all_to_all.25 = f32[16,2,512]{2,1,0:T(2,128)S(1)} all-to-all(f32[16,2,512]{2,1,0:T(2,128)S(1)} %pad_maximum_fusion), channel_id=1, replica_groups=mesh['src'=16,'loop'=8] {'src'}, dimensions={0} | all-to-all | bytes 131072 | tf_op jit(solution)/shard_map/all_to_all | solution.py:179
  122.0 8.7 %all_to_all.26 = f32[16,1,512]{2,1,0:T(1,128)S(1)} all-to-all(f32[16,1,512]{2,1,0:T(1,128)S(1)} %broadcast_in_dim.28), channel_id=1, replica_groups=mesh['src'=16,'loop'=8] {'src'}, dimensions={0} | all-to-all | bytes 65536 | tf_op jit(solution)/shard_map/all_to_all | solution.py:183
  130.6 0.6 broadcast_multiply_fusion.refs_3_
  131.3 26.3 %shard_map.87 = (f32[8,1,512]{2,1,0:T(1,128)}, f32[8,1,512]{2,1,0:T(1,128)}) custom-call(s32[32]{0:T(128)} %min.14.refs_0_, s32[16]{0:T(128)} %copy-done.3, s32[8]{0:T(128)} %get-tuple-element.7.refs_2_, f32[16,1,512]{2,1,0:T(1,128)} %broadcast_multiply_fusion.refs_3_, bf16[8,512,768]{2,1,0:T(8,128)(2,1)} %refs_4_.3, bf16[16,512,768]{2,1,0:T(8,128)(2,1)} %bitcast.33), custom_call_target="tpu_custom_call" | custom-call | flops 12884901888 | bytes 18874368 | tf_op jit(solution)/shard_map/pallas_call | solution.py:137
  157.6 0.7 copy_bitcast_fusion.1
  158.3 18.2 %all_to_all.27 = f32[8,16,512]{2,1,0:T(8,128)S(1)} all-to-all(f32[8,16,512]{2,1,0:T(8,128)S(1)} %broadcast_in_dim.29), channel_id=1, replica_groups=mesh['src'=16,'loop'=8] {'loop'}, dimensions={0} | all-to-all | bytes 524288 | tf_op jit(solution)/shard_map/all_to_all | solution.py:194
  176.6 0.6 multiply_subtract_fusion
  (25 shorter events, 0.3 us)
Async XLA Ops:
  7.2 76.9 %all-gather.3.cloned.1.call-start = ((), (), s32[]{:S(2)}) async-start(), calls=%async_computation.4 | async-start | bytes 13369344 | tf_op jit(solution)/shard_map/all_gather | solution.py:163
  10.1 12.5 %all-to-all-start = ((s32[16,1,48]{2,1,0:T(1,128)}), s32[16,1,48]{2,1,0:T(1,128)S(1)}, u32[]{:S(2)}, u32[]{:S(2)}) async-start(s32[16,1,48]{2,1,0:T(1,128)} %broadcast_in_dim.24), calls=%async_computation | async-start | bytes 16384 | tf_op jit(solution)/shard_map/all_to_all | solution.py:165
  23.4 60.6 %copy-start.3 = (s32[16]{0:T(128)}, s32[16]{0:T(128)S(1)}, u32[]{:S(2)}) copy-start(s32[16]{0:T(128)S(1)} %dynamic-slice_bitcast_fusion.refs_1_) | copy-start | bytes 196
  84.0 37.9 %copy-start.2 = (f32[512]{0:T(512)S(1)}, f32[512]{0:T(512)}, u32[]{:S(2)}) copy-start(f32[512]{0:T(512)} %param.8) | copy-start | bytes 6148
  121.9 35.6 %copy-start.1 = (f32[512]{0:T(512)}, f32[512]{0:T(512)S(1)}, u32[]{:S(2)}) copy-start(f32[512]{0:T(512)S(1)} %multiply_subtract_fusion.1) | copy-start | bytes 6148
  131.2 45.3 %copy-start = (f32[8,512]{1,0:T(8,128)S(1)}, f32[8,512]{1,0:T(8,128)}, u32[]{:S(2)}) copy-start(f32[8,512]{1,0:T(8,128)} %param.11) | copy-start | bytes 49156
Sparse Core Ops, SparseCore 0:
  9.7 74.3 all-gather.2

commit v17 on v16

--- a/solution.py
+++ b/solution.py
@@ -133,7 +133,7 @@
         transcendentals=blocks * slots * rows * width,
         bytes_accessed=2 * (targets.size + blocks * rows * depth),
     )
-    kernel = lambda *refs: body(*refs, scale=scale, slots=slots, window=2)
+    kernel = lambda *refs: body(*refs, scale=scale, slots=slots, window=6)
     return pl.pallas_call(
         kernel,
         out_shape=(out_shape, out_shape),

time: 184 us -> 183 us (level); the launches traced: 184 us -> 181 us
  blocking collectives: 38.6 us -> 34.2 us
    all_to_all x1, blocking collectives: 18.2 us -> 15 us  [local(): lax.all_to_all(jnp.broadcast_to(col[None], (loop_size,) + col.shape), 'lo...]
where the time goes in v17:
time: 183 us; the launch traced here: 181 us
  waiting for transfers between devices  63.4 us (35%)
  Pallas kernels  52.7 us (29%)
  blocking collectives  34.2 us (19%)
  between operations  14.1 us (8%)
  starting transfers between devices  6.49 us (4%)
  local copies, waits for them, and re-layouts  5.11 us (3%)
  other arithmetic  4.88 us (3%)
    all_gather x1, waiting for transfers between devices, local(): x_all = lax.all_gather(sources, 'src')  59.4 us
    pallas_call x2, Pallas kernels, resident_call(): pl.pallas_call(kernel, out_shape=(out_shape, out_shape), in_specs=[smem,...  52.7 us
    all_to_all x1, blocking collectives, local(): lax.all_to_all(jnp.broadcast_to(col[None], (loop_size,) + col.shape), 'lo...  15 us
    all_to_all x1, blocking collectives, local(): got = lax.all_to_all(sent, 'src', 0, 0, tiled=True)  10.5 us
    all_to_all x1, blocking collectives, local(): lax.all_to_all(jnp.broadcast_to(f_new[None], (blocks,) + f_new.shape), 's...  8.66 us
    all_to_all x1, starting transfers between devices, local(): lax.all_to_all(jnp.broadcast_to(meta[None], (blocks,) + meta.shape), 'src...  6.46 us
  transfers between devices with their start and end apart: 2, of which 2 were waited for; matrix products, arithmetic and copies ran while one was open for 4% of the time, Pallas kernels for 0%

profile of v17, /device:TPU:0, one launch (start us, length us, event | category | flops | bytes accessed | tf_op | source)
XLA Modules:
  0.0 180.9 jit_solution(12546524657361573417)
XLA Ops:
  7.2 0.7 all-gather.3.cloned.1.call-update
  7.9 0.8 copy.30
  8.7 0.1 reshape_squeeze.3
  8.7 0.7 pad_add_fusion
  9.5 0.6 broadcast_in_dim.24
  10.1 6.5 %all-to-all-start = ((s32[16,1,48]{2,1,0:T(1,128)}), s32[16,1,48]{2,1,0:T(1,128)S(1)}, u32[]{:S(2)}, u32[]{:S(2)}) async-start(s32[16,1,48]{2,1,0:T(1,128)} %broadcast_in_dim.24), calls=%async_computation | async-start | bytes 16384 | tf_op jit(solution)/shard_map/all_to_all | solution.py:165
  16.5 0.7 multiply_bitcast_fusion
  17.3 2.0 %copy.33.refs_3_ = f32[8,512,1]{2,1,0:T(8,128)} copy(f32[8,512,1]{1,0,2:T(8,128)S(1)} %multiply_bitcast_fusion) | data formatting | bytes 32768 | tf_op jit(solution)/shard_map/broadcast_in_dim | solution.py:173
  19.3 3.3 %all-to-all-done = s32[16,1,48]{2,1,0:T(1,128)S(1)} async-done(((s32[16,1,48]{2,1,0:T(1,128)}), s32[16,1,48]{2,1,0:T(1,128)S(1)}, u32[]{:S(2)}, u32[]{:S(2)}) %all-to-all-start) | async-done | bytes 3104 | tf_op jit(solution)/shard_map/all_to_all | solution.py:165
  22.6 0.1 copy.31
  22.7 0.1 copy.32
  22.7 0.7 min.14.refs_0_
  23.5 0.1 select_reduce_fusion
  23.6 1.0 sort.19
  24.6 59.4 %all-gather.3.cloned.1.call-done = bf16[8192,768]{1,0:T(8,128)(2,1)} async-done(((bf16[512,768]{1,0:T(8,128)(2,1)}), bf16[8192,768]{1,0:T(8,128)(2,1)}) %all-gather.3.cloned.1.call-update) | async-done | bytes 12582928 | tf_op jit(solution)/shard_map/all_gather | solution.py:163
  84.0 25.7 %shard_map.86 = (f32[16,1,512]{2,1,0:T(1,128)}, f32[16,1,512]{2,1,0:T(1,128)}) custom-call(s32[32]{0:T(128)} %min.14.refs_0_, s32[16]{0:T(128)} %copy-done.3, s32[8]{0:T(128)} %get-tuple-element.7.refs_2_, f32[8,512,1]{2,1,0:T(8,128)} %copy.33.refs_3_, bf16[8,512,768]{2,1,0:T(8,128)(2,1)} %refs_4_.3, bf16[16,512,768]{2,1,0:T(8,128)(2,1)} %bitcast.32), custom_call_target="tpu_custom_call" | custom-call | flops 12884901888 | bytes 18874368 | tf_op jit(solution)/shard_map/pallas_call | solution.py:137
  109.8 0.8 pad_maximum_fusion
  110.6 10.5 %all_to_all.25 = f32[16,2,512]{2,1,0:T(2,128)S(1)} all-to-all(f32[16,2,512]{2,1,0:T(2,128)S(1)} %pad_maximum_fusion), channel_id=1, replica_groups=mesh['src'=16,'loop'=8] {'src'}, dimensions={0} | all-to-all | bytes 131072 | tf_op jit(solution)/shard_map/all_to_all | solution.py:179
  121.3 8.7 %all_to_all.26 = f32[16,1,512]{2,1,0:T(1,128)S(1)} all-to-all(f32[16,1,512]{2,1,0:T(1,128)S(1)} %broadcast_in_dim.28), channel_id=1, replica_groups=mesh['src'=16,'loop'=8] {'src'}, dimensions={0} | all-to-all | bytes 65536 | tf_op jit(solution)/shard_map/all_to_all | solution.py:183
  130.0 0.6 broadcast_multiply_fusion.refs_3_
  130.6 26.9 %shard_map.87 = (f32[8,1,512]{2,1,0:T(1,128)}, f32[8,1,512]{2,1,0:T(1,128)}) custom-call(s32[32]{0:T(128)} %min.14.refs_0_, s32[16]{0:T(128)} %copy-done.3, s32[8]{0:T(128)} %get-tuple-element.7.refs_2_, f32[16,1,512]{2,1,0:T(1,128)} %broadcast_multiply_fusion.refs_3_, bf16[8,512,768]{2,1,0:T(8,128)(2,1)} %refs_4_.3, bf16[16,512,768]{2,1,0:T(8,128)(2,1)} %bitcast.33), custom_call_target="tpu_custom_call" | custom-call | flops 12884901888 | bytes 18874368 | tf_op jit(solution)/shard_map/pallas_call | solution.py:137
  157.6 0.7 copy_bitcast_fusion.1
  158.3 15.0 %all_to_all.27 = f32[8,16,512]{2,1,0:T(8,128)S(1)} all-to-all(f32[8,16,512]{2,1,0:T(8,128)S(1)} %broadcast_in_dim.29), channel_id=1, replica_groups=mesh['src'=16,'loop'=8] {'loop'}, dimensions={0} | all-to-all | bytes 524288 | tf_op jit(solution)/shard_map/all_to_all | solution.py:194
  173.4 0.6 multiply_subtract_fusion
  (25 shorter events, 0.3 us)
Async XLA Ops:
  7.2 76.9 %all-gather.3.cloned.1.call-start = ((), (), s32[]{:S(2)}) async-start(), calls=%async_computation.4 | async-start | bytes 13369344 | tf_op jit(solution)/shard_map/all_gather | solution.py:163
  10.1 12.5 %all-to-all-start = ((s32[16,1,48]{2,1,0:T(1,128)}), s32[16,1,48]{2,1,0:T(1,128)S(1)}, u32[]{:S(2)}, u32[]{:S(2)}) async-start(s32[16,1,48]{2,1,0:T(1,128)} %broadcast_in_dim.24), calls=%async_computation | async-start | bytes 16384 | tf_op jit(solution)/shard_map/all_to_all | solution.py:165
  23.4 60.6 %copy-start.3 = (s32[16]{0:T(128)}, s32[16]{0:T(128)S(1)}, u32[]{:S(2)}) copy-start(s32[16]{0:T(128)S(1)} %dynamic-slice_bitcast_fusion.refs_1_) | copy-start | bytes 196
  84.0 37.2 %copy-start.2 = (f32[512]{0:T(512)S(1)}, f32[512]{0:T(512)}, u32[]{:S(2)}) copy-start(f32[512]{0:T(512)} %param.8) | copy-start | bytes 6148
  121.3 36.3 %copy-start.1 = (f32[512]{0:T(512)}, f32[512]{0:T(512)S(1)}, u32[]{:S(2)}) copy-start(f32[512]{0:T(512)S(1)} %multiply_subtract_fusion.1) | copy-start | bytes 6148
  130.6 42.8 %copy-start = (f32[8,512]{1,0:T(8,128)S(1)}, f32[8,512]{1,0:T(8,128)}, u32[]{:S(2)}) copy-start(f32[8,512]{1,0:T(8,128)} %param.11) | copy-start | bytes 49156
Sparse Core Ops, SparseCore 0:
  9.7 74.3 all-gather.2

commit v18 on v17

--- a/solution.py
+++ b/solution.py
@@ -133,7 +133,7 @@
         transcendentals=blocks * slots * rows * width,
         bytes_accessed=2 * (targets.size + blocks * rows * depth),
     )
-    kernel = lambda *refs: body(*refs, scale=scale, slots=slots, window=6)
+    kernel = lambda *refs: body(*refs, scale=scale, slots=slots, window=8)
     return pl.pallas_call(
         kernel,
         out_shape=(out_shape, out_shape),

time: 183 us -> 184 us (level)
  blocking collectives: 34.2 us -> 37.8 us
  Pallas kernels: 52.7 us -> 50.5 us
    pallas_call x2, Pallas kernels: 52.7 us -> 50.5 us  [resident_call(): pl.pallas_call(kernel, out_shape=(out_shape, out_shape), in_specs=[smem,...]
    all_to_all x1, blocking collectives: 15 us -> 17 us  [local(): lax.all_to_all(jnp.broadcast_to(col[None], (loop_size,) + col.shape), 'lo...]
where the time goes in v18:
time: 184 us; the launch traced here: 182 us
  waiting for transfers between devices  63.4 us (34%)
  Pallas kernels  50.5 us (27%)
  blocking collectives  37.8 us (21%)
  between operations  14.1 us (8%)
  starting transfers between devices  6.49 us (4%)
  local copies, waits for them, and re-layouts  5.11 us (3%)
  other arithmetic  4.88 us (3%)
    all_gather x1, waiting for transfers between devices, local(): x_all = lax.all_gather(sources, 'src')  59.4 us
    pallas_call x2, Pallas kernels, resident_call(): pl.pallas_call(kernel, out_shape=(out_shape, out_shape), in_specs=[smem,...  50.5 us
    all_to_all x1, blocking collectives, local(): lax.all_to_all(jnp.broadcast_to(col[None], (loop_size,) + col.shape), 'lo...  17 us
    all_to_all x1, blocking collectives, local(): got = lax.all_to_all(sent, 'src', 0, 0, tiled=True)  12.1 us
    all_to_all x1, blocking collectives, local(): lax.all_to_all(jnp.broadcast_to(f_new[None], (blocks,) + f_new.shape), 's...  8.66 us
    all_to_all x1, starting transfers between devices, local(): lax.all_to_all(jnp.broadcast_to(meta[None], (blocks,) + meta.shape), 'src...  6.46 us
  transfers between devices with their start and end apart: 2, of which 2 were waited for; matrix products, arithmetic and copies ran while one was open for 4% of the time, Pallas kernels for 0%

profile of v18, /device:TPU:0, one launch (start us, length us, event | category | flops | bytes accessed | tf_op | source)
XLA Modules:
  0.0 182.3 jit_solution(14952290880223406356)
XLA Ops:
  7.2 0.7 all-gather.3.cloned.1.call-update
  7.9 0.8 copy.30
  8.7 0.1 reshape_squeeze.3
  8.7 0.7 pad_add_fusion
  9.5 0.6 broadcast_in_dim.24
  10.1 6.5 %all-to-all-start = ((s32[16,1,48]{2,1,0:T(1,128)}), s32[16,1,48]{2,1,0:T(1,128)S(1)}, u32[]{:S(2)}, u32[]{:S(2)}) async-start(s32[16,1,48]{2,1,0:T(1,128)} %broadcast_in_dim.24), calls=%async_computation | async-start | bytes 16384 | tf_op jit(solution)/shard_map/all_to_all | solution.py:165
  16.5 0.7 multiply_bitcast_fusion
  17.3 2.0 %copy.33.refs_3_ = f32[8,512,1]{2,1,0:T(8,128)} copy(f32[8,512,1]{1,0,2:T(8,128)S(1)} %multiply_bitcast_fusion) | data formatting | bytes 32768 | tf_op jit(solution)/shard_map/broadcast_in_dim | solution.py:173
  19.3 3.3 %all-to-all-done = s32[16,1,48]{2,1,0:T(1,128)S(1)} async-done(((s32[16,1,48]{2,1,0:T(1,128)}), s32[16,1,48]{2,1,0:T(1,128)S(1)}, u32[]{:S(2)}, u32[]{:S(2)}) %all-to-all-start) | async-done | bytes 3104 | tf_op jit(solution)/shard_map/all_to_all | solution.py:165
  22.6 0.1 copy.31
  22.7 0.1 copy.32
  22.7 0.7 min.14.refs_0_
  23.5 0.1 select_reduce_fusion
  23.6 1.0 sort.19
  24.6 59.4 %all-gather.3.cloned.1.call-done = bf16[8192,768]{1,0:T(8,128)(2,1)} async-done(((bf16[512,768]{1,0:T(8,128)(2,1)}), bf16[8192,768]{1,0:T(8,128)(2,1)}) %all-gather.3.cloned.1.call-update) | async-done | bytes 12582928 | tf_op jit(solution)/shard_map/all_gather | solution.py:163
  84.0 24.7 %shard_map.86 = (f32[16,1,512]{2,1,0:T(1,128)}, f32[16,1,512]{2,1,0:T(1,128)}) custom-call(s32[32]{0:T(128)} %min.14.refs_0_, s32[16]{0:T(128)} %copy-done.3, s32[8]{0:T(128)} %get-tuple-element.7.refs_2_, f32[8,512,1]{2,1,0:T(8,128)} %copy.33.refs_3_, bf16[8,512,768]{2,1,0:T(8,128)(2,1)} %refs_4_.3, bf16[16,512,768]{2,1,0:T(8,128)(2,1)} %bitcast.32), custom_call_target="tpu_custom_call" | custom-call | flops 12884901888 | bytes 18874368 | tf_op jit(solution)/shard_map/pallas_call | solution.py:137
  108.8 0.8 pad_maximum_fusion
  109.6 12.1 %all_to_all.25 = f32[16,2,512]{2,1,0:T(2,128)S(1)} all-to-all(f32[16,2,512]{2,1,0:T(2,128)S(1)} %pad_maximum_fusion), channel_id=1, replica_groups=mesh['src'=16,'loop'=8] {'src'}, dimensions={0} | all-to-all | bytes 131072 | tf_op jit(solution)/shard_map/all_to_all | solution.py:179
  121.9 8.7 %all_to_all.26 = f32[16,1,512]{2,1,0:T(1,128)S(1)} all-to-all(f32[16,1,512]{2,1,0:T(1,128)S(1)} %broadcast_in_dim.28), channel_id=1, replica_groups=mesh['src'=16,'loop'=8] {'src'}, dimensions={0} | all-to-all | bytes 65536 | tf_op jit(solution)/shard_map/all_to_all | solution.py:183
  130.6 0.6 broadcast_multiply_fusion.refs_3_
  131.2 25.8 %shard_map.87 = (f32[8,1,512]{2,1,0:T(1,128)}, f32[8,1,512]{2,1,0:T(1,128)}) custom-call(s32[32]{0:T(128)} %min.14.refs_0_, s32[16]{0:T(128)} %copy-done.3, s32[8]{0:T(128)} %get-tuple-element.7.refs_2_, f32[16,1,512]{2,1,0:T(1,128)} %broadcast_multiply_fusion.refs_3_, bf16[8,512,768]{2,1,0:T(8,128)(2,1)} %refs_4_.3, bf16[16,512,768]{2,1,0:T(8,128)(2,1)} %bitcast.33), custom_call_target="tpu_custom_call" | custom-call | flops 12884901888 | bytes 18874368 | tf_op jit(solution)/shard_map/pallas_call | solution.py:137
  157.0 0.7 copy_bitcast_fusion.1
  157.8 17.0 %all_to_all.27 = f32[8,16,512]{2,1,0:T(8,128)S(1)} all-to-all(f32[8,16,512]{2,1,0:T(8,128)S(1)} %broadcast_in_dim.29), channel_id=1, replica_groups=mesh['src'=16,'loop'=8] {'loop'}, dimensions={0} | all-to-all | bytes 524288 | tf_op jit(solution)/shard_map/all_to_all | solution.py:194
  174.8 0.6 multiply_subtract_fusion
  (25 shorter events, 0.3 us)
Async XLA Ops:
  7.2 76.9 %all-gather.3.cloned.1.call-start = ((), (), s32[]{:S(2)}) async-start(), calls=%async_computation.4 | async-start | bytes 13369344 | tf_op jit(solution)/shard_map/all_gather | solution.py:163
  10.1 12.5 %all-to-all-start = ((s32[16,1,48]{2,1,0:T(1,128)}), s32[16,1,48]{2,1,0:T(1,128)S(1)}, u32[]{:S(2)}, u32[]{:S(2)}) async-start(s32[16,1,48]{2,1,0:T(1,128)} %broadcast_in_dim.24), calls=%async_computation | async-start | bytes 16384 | tf_op jit(solution)/shard_map/all_to_all | solution.py:165
  23.4 60.6 %copy-start.3 = (s32[16]{0:T(128)}, s32[16]{0:T(128)S(1)}, u32[]{:S(2)}) copy-start(s32[16]{0:T(128)S(1)} %dynamic-slice_bitcast_fusion.refs_1_) | copy-start | bytes 196
  84.0 37.8 %copy-start.2 = (f32[512]{0:T(512)S(1)}, f32[512]{0:T(512)}, u32[]{:S(2)}) copy-start(f32[512]{0:T(512)} %param.8) | copy-start | bytes 6148
  121.9 35.1 %copy-start.1 = (f32[512]{0:T(512)}, f32[512]{0:T(512)S(1)}, u32[]{:S(2)}) copy-start(f32[512]{0:T(512)S(1)} %multiply_subtract_fusion.1) | copy-start | bytes 6148
  131.2 43.6 %copy-start = (f32[8,512]{1,0:T(8,128)S(1)}, f32[8,512]{1,0:T(8,128)}, u32[]{:S(2)}) copy-start(f32[8,512]{1,0:T(8,128)} %param.11) | copy-start | bytes 49156
Sparse Core Ops, SparseCore 0:
  9.7 74.3 all-gather.2

commit v19 on v18

--- a/solution.py
+++ b/solution.py
@@ -133,7 +133,7 @@
         transcendentals=blocks * slots * rows * width,
         bytes_accessed=2 * (targets.size + blocks * rows * depth),
     )
-    kernel = lambda *refs: body(*refs, scale=scale, slots=slots, window=8)
+    kernel = lambda *refs: body(*refs, scale=scale, slots=slots, window=5)
     return pl.pallas_call(
         kernel,
         out_shape=(out_shape, out_shape),

time: 184 us -> 183 us (level)
  blocking collectives: 37.8 us -> 34.8 us
  Pallas kernels: 50.5 us -> 53.2 us
    pallas_call x2, Pallas kernels: 50.5 us -> 53.2 us  [resident_call(): pl.pallas_call(kernel, out_shape=(out_shape, out_shape), in_specs=[smem,...]
    all_to_all x1, blocking collectives: 12.1 us -> 10.2 us  [local(): got = lax.all_to_all(sent, 'src', 0, 0, tiled=True)]
where the time goes in v19:
time: 183 us; the launch traced here: 182 us
  waiting for transfers between devices  63.4 us (35%)
  Pallas kernels  53.2 us (29%)
  blocking collectives  34.8 us (19%)
  between operations  14.1 us (8%)
  starting transfers between devices  6.49 us (4%)
  local copies, waits for them, and re-layouts  5.11 us (3%)
  other arithmetic  4.88 us (3%)
    all_gather x1, waiting for transfers between devices, local(): x_all = lax.all_gather(sources, 'src')  59.4 us
    pallas_call x2, Pallas kernels, resident_call(): pl.pallas_call(kernel, out_shape=(out_shape, out_shape), in_specs=[smem,...  53.2 us
    all_to_all x1, blocking collectives, local(): lax.all_to_all(jnp.broadcast_to(col[None], (loop_size,) + col.shape), 'lo...  15.9 us
    all_to_all x1, blocking collectives, local(): got = lax.all_to_all(sent, 'src', 0, 0, tiled=True)  10.2 us
    all_to_all x1, blocking collectives, local(): lax.all_to_all(jnp.broadcast_to(f_new[None], (blocks,) + f_new.shape), 's...  8.66 us
    all_to_all x1, starting transfers between devices, local(): lax.all_to_all(jnp.broadcast_to(meta[None], (blocks,) + meta.shape), 'src...  6.46 us
  transfers between devices with their start and end apart: 2, of which 2 were waited for; matrix products, arithmetic and copies ran while one was open for 4% of the time, Pallas kernels for 0%

profile of v19, /device:TPU:0, one launch (start us, length us, event | category | flops | bytes accessed | tf_op | source)
XLA Modules:
  0.0 182.0 jit_solution(9528406292864394236)
XLA Ops:
  7.2 0.7 all-gather.3.cloned.1.call-update
  7.9 0.8 copy.30
  8.7 0.1 reshape_squeeze.3
  8.7 0.7 pad_add_fusion
  9.5 0.6 broadcast_in_dim.24
  10.1 6.5 %all-to-all-start = ((s32[16,1,48]{2,1,0:T(1,128)}), s32[16,1,48]{2,1,0:T(1,128)S(1)}, u32[]{:S(2)}, u32[]{:S(2)}) async-start(s32[16,1,48]{2,1,0:T(1,128)} %broadcast_in_dim.24), calls=%async_computation | async-start | bytes 16384 | tf_op jit(solution)/shard_map/all_to_all | solution.py:165
  16.5 0.7 multiply_bitcast_fusion
  17.3 2.0 %copy.33.refs_3_ = f32[8,512,1]{2,1,0:T(8,128)} copy(f32[8,512,1]{1,0,2:T(8,128)S(1)} %multiply_bitcast_fusion) | data formatting | bytes 32768 | tf_op jit(solution)/shard_map/broadcast_in_dim | solution.py:173
  19.3 3.3 %all-to-all-done = s32[16,1,48]{2,1,0:T(1,128)S(1)} async-done(((s32[16,1,48]{2,1,0:T(1,128)}), s32[16,1,48]{2,1,0:T(1,128)S(1)}, u32[]{:S(2)}, u32[]{:S(2)}) %all-to-all-start) | async-done | bytes 3104 | tf_op jit(solution)/shard_map/all_to_all | solution.py:165
  22.6 0.1 copy.31
  22.7 0.1 copy.32
  22.7 0.7 min.14.refs_0_
  23.5 0.1 select_reduce_fusion
  23.6 1.0 sort.19
  24.6 59.4 %all-gather.3.cloned.1.call-done = bf16[8192,768]{1,0:T(8,128)(2,1)} async-done(((bf16[512,768]{1,0:T(8,128)(2,1)}), bf16[8192,768]{1,0:T(8,128)(2,1)}) %all-gather.3.cloned.1.call-update) | async-done | bytes 12582928 | tf_op jit(solution)/shard_map/all_gather | solution.py:163
  84.0 26.0 %shard_map.86 = (f32[16,1,512]{2,1,0:T(1,128)}, f32[16,1,512]{2,1,0:T(1,128)}) custom-call(s32[32]{0:T(128)} %min.14.refs_0_, s32[16]{0:T(128)} %copy-done.3, s32[8]{0:T(128)} %get-tuple-element.7.refs_2_, f32[8,512,1]{2,1,0:T(8,128)} %copy.33.refs_3_, bf16[8,512,768]{2,1,0:T(8,128)(2,1)} %refs_4_.3, bf16[16,512,768]{2,1,0:T(8,128)(2,1)} %bitcast.32), custom_call_target="tpu_custom_call" | custom-call | flops 12884901888 | bytes 18874368 | tf_op jit(solution)/shard_map/pallas_call | solution.py:137
  110.1 0.8 pad_maximum_fusion
  110.9 10.2 %all_to_all.25 = f32[16,2,512]{2,1,0:T(2,128)S(1)} all-to-all(f32[16,2,512]{2,1,0:T(2,128)S(1)} %pad_maximum_fusion), channel_id=1, replica_groups=mesh['src'=16,'loop'=8] {'src'}, dimensions={0} | all-to-all | bytes 131072 | tf_op jit(solution)/shard_map/all_to_all | solution.py:179
  121.3 8.7 %all_to_all.26 = f32[16,1,512]{2,1,0:T(1,128)S(1)} all-to-all(f32[16,1,512]{2,1,0:T(1,128)S(1)} %broadcast_in_dim.28), channel_id=1, replica_groups=mesh['src'=16,'loop'=8] {'src'}, dimensions={0} | all-to-all | bytes 65536 | tf_op jit(solution)/shard_map/all_to_all | solution.py:183
  129.9 0.6 broadcast_multiply_fusion.refs_3_
  130.6 27.2 %shard_map.87 = (f32[8,1,512]{2,1,0:T(1,128)}, f32[8,1,512]{2,1,0:T(1,128)}) custom-call(s32[32]{0:T(128)} %min.14.refs_0_, s32[16]{0:T(128)} %copy-done.3, s32[8]{0:T(128)} %get-tuple-element.7.refs_2_, f32[16,1,512]{2,1,0:T(1,128)} %broadcast_multiply_fusion.refs_3_, bf16[8,512,768]{2,1,0:T(8,128)(2,1)} %refs_4_.3, bf16[16,512,768]{2,1,0:T(8,128)(2,1)} %bitcast.33), custom_call_target="tpu_custom_call" | custom-call | flops 12884901888 | bytes 18874368 | tf_op jit(solution)/shard_map/pallas_call | solution.py:137
  157.8 0.7 copy_bitcast_fusion.1
  158.5 15.9 %all_to_all.27 = f32[8,16,512]{2,1,0:T(8,128)S(1)} all-to-all(f32[8,16,512]{2,1,0:T(8,128)S(1)} %broadcast_in_dim.29), channel_id=1, replica_groups=mesh['src'=16,'loop'=8] {'loop'}, dimensions={0} | all-to-all | bytes 524288 | tf_op jit(solution)/shard_map/all_to_all | solution.py:194
  174.5 0.6 multiply_subtract_fusion
  (25 shorter events, 0.3 us)
Async XLA Ops:
  7.2 76.9 %all-gather.3.cloned.1.call-start = ((), (), s32[]{:S(2)}) async-start(), calls=%async_computation.4 | async-start | bytes 13369344 | tf_op jit(solution)/shard_map/all_gather | solution.py:163
  10.1 12.5 %all-to-all-start = ((s32[16,1,48]{2,1,0:T(1,128)}), s32[16,1,48]{2,1,0:T(1,128)S(1)}, u32[]{:S(2)}, u32[]{:S(2)}) async-start(s32[16,1,48]{2,1,0:T(1,128)} %broadcast_in_dim.24), calls=%async_computation | async-start | bytes 16384 | tf_op jit(solution)/shard_map/all_to_all | solution.py:165
  23.4 60.6 %copy-start.3 = (s32[16]{0:T(128)}, s32[16]{0:T(128)S(1)}, u32[]{:S(2)}) copy-start(s32[16]{0:T(128)S(1)} %dynamic-slice_bitcast_fusion.refs_1_) | copy-start | bytes 196
  84.0 37.2 %copy-start.2 = (f32[512]{0:T(512)S(1)}, f32[512]{0:T(512)}, u32[]{:S(2)}) copy-start(f32[512]{0:T(512)} %param.8) | copy-start | bytes 6148
  121.2 36.5 %copy-start.1 = (f32[512]{0:T(512)}, f32[512]{0:T(512)S(1)}, u32[]{:S(2)}) copy-start(f32[512]{0:T(512)S(1)} %multiply_subtract_fusion.1) | copy-start | bytes 6148
  130.6 43.9 %copy-start = (f32[8,512]{1,0:T(8,128)S(1)}, f32[8,512]{1,0:T(8,128)}, u32[]{:S(2)}) copy-start(f32[8,512]{1,0:T(8,128)} %param.11) | copy-start | bytes 49156
Sparse Core Ops, SparseCore 0:
  9.7 74.3 all-gather.2

commit v20 on v19

--- a/solution.py
+++ b/solution.py
@@ -133,7 +133,7 @@
         transcendentals=blocks * slots * rows * width,
         bytes_accessed=2 * (targets.size + blocks * rows * depth),
     )
-    kernel = lambda *refs: body(*refs, scale=scale, slots=slots, window=5)
+    kernel = lambda *refs: body(*refs, scale=scale, slots=slots, window=7)
     return pl.pallas_call(
         kernel,
         out_shape=(out_shape, out_shape),

time: 183 us -> 183 us (level)
    all_to_all x1, blocking collectives: 15.9 us -> 13.7 us  [local(): lax.all_to_all(jnp.broadcast_to(col[None], (loop_size,) + col.shape), 'lo...]
where the time goes in v20:
time: 183 us; the launch traced here: 181 us
  waiting for transfers between devices  63.4 us (35%)
  Pallas kernels  53.8 us (29%)
  blocking collectives  33.3 us (18%)
  between operations  14.1 us (8%)
  starting transfers between devices  6.49 us (4%)
  local copies, waits for them, and re-layouts  5.11 us (3%)
  other arithmetic  4.88 us (3%)
    all_gather x1, waiting for transfers between devices, local(): x_all = lax.all_gather(sources, 'src')  59.4 us
    pallas_call x2, Pallas kernels, resident_call(): pl.pallas_call(kernel, out_shape=(out_shape, out_shape), in_specs=[smem,...  53.8 us
    all_to_all x1, blocking collectives, local(): lax.all_to_all(jnp.broadcast_to(col[None], (loop_size,) + col.shape), 'lo...  13.7 us
    all_to_all x1, blocking collectives, local(): got = lax.all_to_all(sent, 'src', 0, 0, tiled=True)  11 us
    all_to_all x1, blocking collectives, local(): lax.all_to_all(jnp.broadcast_to(f_new[None], (blocks,) + f_new.shape), 's...  8.66 us
    all_to_all x1, starting transfers between devices, local(): lax.all_to_all(jnp.broadcast_to(meta[None], (blocks,) + meta.shape), 'src...  6.46 us
  transfers between devices with their start and end apart: 2, of which 2 were waited for; matrix products, arithmetic and copies ran while one was open for 4% of the time, Pallas kernels for 0%

profile of v20, /device:TPU:0, one launch (start us, length us, event | category | flops | bytes accessed | tf_op | source)
XLA Modules:
  0.0 181.1 jit_solution(18444673016842718195)
XLA Ops:
  7.2 0.7 all-gather.3.cloned.1.call-update
  7.9 0.8 copy.30
  8.7 0.1 reshape_squeeze.3
  8.7 0.7 pad_add_fusion
  9.5 0.6 broadcast_in_dim.24
  10.1 6.5 %all-to-all-start = ((s32[16,1,48]{2,1,0:T(1,128)}), s32[16,1,48]{2,1,0:T(1,128)S(1)}, u32[]{:S(2)}, u32[]{:S(2)}) async-start(s32[16,1,48]{2,1,0:T(1,128)} %broadcast_in_dim.24), calls=%async_computation | async-start | bytes 16384 | tf_op jit(solution)/shard_map/all_to_all | solution.py:165
  16.5 0.7 multiply_bitcast_fusion
  17.3 2.0 %copy.33.refs_3_ = f32[8,512,1]{2,1,0:T(8,128)} copy(f32[8,512,1]{1,0,2:T(8,128)S(1)} %multiply_bitcast_fusion) | data formatting | bytes 32768 | tf_op jit(solution)/shard_map/broadcast_in_dim | solution.py:173
  19.3 3.3 %all-to-all-done = s32[16,1,48]{2,1,0:T(1,128)S(1)} async-done(((s32[16,1,48]{2,1,0:T(1,128)}), s32[16,1,48]{2,1,0:T(1,128)S(1)}, u32[]{:S(2)}, u32[]{:S(2)}) %all-to-all-start) | async-done | bytes 3104 | tf_op jit(solution)/shard_map/all_to_all | solution.py:165
  22.6 0.1 copy.31
  22.7 0.1 copy.32
  22.7 0.7 min.14.refs_0_
  23.5 0.1 select_reduce_fusion
  23.6 1.0 sort.19
  24.6 59.4 %all-gather.3.cloned.1.call-done = bf16[8192,768]{1,0:T(8,128)(2,1)} async-done(((bf16[512,768]{1,0:T(8,128)(2,1)}), bf16[8192,768]{1,0:T(8,128)(2,1)}) %all-gather.3.cloned.1.call-update) | async-done | bytes 12582928 | tf_op jit(solution)/shard_map/all_gather | solution.py:163
  84.0 26.3 %shard_map.86 = (f32[16,1,512]{2,1,0:T(1,128)}, f32[16,1,512]{2,1,0:T(1,128)}) custom-call(s32[32]{0:T(128)} %min.14.refs_0_, s32[16]{0:T(128)} %copy-done.3, s32[8]{0:T(128)} %get-tuple-element.7.refs_2_, f32[8,512,1]{2,1,0:T(8,128)} %copy.33.refs_3_, bf16[8,512,768]{2,1,0:T(8,128)(2,1)} %refs_4_.3, bf16[16,512,768]{2,1,0:T(8,128)(2,1)} %bitcast.32), custom_call_target="tpu_custom_call" | custom-call | flops 12884901888 | bytes 18874368 | tf_op jit(solution)/shard_map/pallas_call | solution.py:137
  110.4 0.8 pad_maximum_fusion
  111.2 11.0 %all_to_all.25 = f32[16,2,512]{2,1,0:T(2,128)S(1)} all-to-all(f32[16,2,512]{2,1,0:T(2,128)S(1)} %pad_maximum_fusion), channel_id=1, replica_groups=mesh['src'=16,'loop'=8] {'src'}, dimensions={0} | all-to-all | bytes 131072 | tf_op jit(solution)/shard_map/all_to_all | solution.py:179
  122.4 8.7 %all_to_all.26 = f32[16,1,512]{2,1,0:T(1,128)S(1)} all-to-all(f32[16,1,512]{2,1,0:T(1,128)S(1)} %broadcast_in_dim.28), channel_id=1, replica_groups=mesh['src'=16,'loop'=8] {'src'}, dimensions={0} | all-to-all | bytes 65536 | tf_op jit(solution)/shard_map/all_to_all | solution.py:183
  131.0 0.6 broadcast_multiply_fusion.refs_3_
  131.6 27.5 %shard_map.87 = (f32[8,1,512]{2,1,0:T(1,128)}, f32[8,1,512]{2,1,0:T(1,128)}) custom-call(s32[32]{0:T(128)} %min.14.refs_0_, s32[16]{0:T(128)} %copy-done.3, s32[8]{0:T(128)} %get-tuple-element.7.refs_2_, f32[16,1,512]{2,1,0:T(1,128)} %broadcast_multiply_fusion.refs_3_, bf16[8,512,768]{2,1,0:T(8,128)(2,1)} %refs_4_.3, bf16[16,512,768]{2,1,0:T(8,128)(2,1)} %bitcast.33), custom_call_target="tpu_custom_call" | custom-call | flops 12884901888 | bytes 18874368 | tf_op jit(solution)/shard_map/pallas_call | solution.py:137
  159.1 0.7 copy_bitcast_fusion.1
  159.9 13.7 %all_to_all.27 = f32[8,16,512]{2,1,0:T(8,128)S(1)} all-to-all(f32[8,16,512]{2,1,0:T(8,128)S(1)} %broadcast_in_dim.29), channel_id=1, replica_groups=mesh['src'=16,'loop'=8] {'loop'}, dimensions={0} | all-to-all | bytes 524288 | tf_op jit(solution)/shard_map/all_to_all | solution.py:194
  173.6 0.6 multiply_subtract_fusion
  (25 shorter events, 0.3 us)
Async XLA Ops:
  7.2 76.9 %all-gather.3.cloned.1.call-start = ((), (), s32[]{:S(2)}) async-start(), calls=%async_computation.4 | async-start | bytes 13369344 | tf_op jit(solution)/shard_map/all_gather | solution.py:163
  10.1 12.5 %all-to-all-start = ((s32[16,1,48]{2,1,0:T(1,128)}), s32[16,1,48]{2,1,0:T(1,128)S(1)}, u32[]{:S(2)}, u32[]{:S(2)}) async-start(s32[16,1,48]{2,1,0:T(1,128)} %broadcast_in_dim.24), calls=%async_computation | async-start | bytes 16384 | tf_op jit(solution)/shard_map/all_to_all | solution.py:165
  23.4 60.6 %copy-start.3 = (s32[16]{0:T(128)}, s32[16]{0:T(128)S(1)}, u32[]{:S(2)}) copy-start(s32[16]{0:T(128)S(1)} %dynamic-slice_bitcast_fusion.refs_1_) | copy-start | bytes 196
  84.0 38.2 %copy-start.2 = (f32[512]{0:T(512)S(1)}, f32[512]{0:T(512)}, u32[]{:S(2)}) copy-start(f32[512]{0:T(512)} %param.8) | copy-start | bytes 6148
  122.3 36.8 %copy-start.1 = (f32[512]{0:T(512)}, f32[512]{0:T(512)S(1)}, u32[]{:S(2)}) copy-start(f32[512]{0:T(512)S(1)} %multiply_subtract_fusion.1) | copy-start | bytes 6148
  131.6 42.0 %copy-start = (f32[8,512]{1,0:T(8,128)S(1)}, f32[8,512]{1,0:T(8,128)}, u32[]{:S(2)}) copy-start(f32[8,512]{1,0:T(8,128)} %param.11) | copy-start | bytes 49156
Sparse Core Ops, SparseCore 0:
  9.7 74.3 all-gather.2
